TPU v7x, 768 devices: a whole 4x8x12 slice. The times are simulated.
768 devices in a mesh: span: 32 (over x, y), freq: 24 (over z, core).
Axes of the slice: x: 4, y: 8, z: 12, core: 2. Of those that a mesh axis runs over, the one named last changes fastest.
Arguments:
- visibilities: bfloat16 [24, 1024, 2, 512], P('freq', 'span'), may hold values from -6 to 6
- coords: float32 [24, 1024, 2, 512], P('freq', 'span'), may hold values from -12 to 12
- vis_counts: int32 [24, 1024], P('freq', 'span'), may hold values from 128 to 512
- cover_tile: int32 [24, 1024, 1], P('freq', 'span'), may hold values from 0 to 31; in each aligned block of 32 rows (0 to 31, 32 to 63, ..., all dimensions but the last counted through in order) at most 2 rows name the same one
- offsets: int32 [24, 1024, 2], P('freq', 'span'), may hold values from 0 to 96
- channel: int32 [24, 1024], P('freq', 'span'), may hold values from 0 to 15
- taper: float32 [32, 32], replicated, may hold values from 0.2 to 1
Outputs:
- uv_terms: float32 [2, 32, 2, 128, 128], P(None, 'span')
Inputs may be any that keep to these rules, and one draw needn't show every extreme that they name: `cover_tile`: the subgrids of one device name each tile at most 2 times, a bound that some block reaches.
All inputs are finite; a program needn't handle non-finite values.
Results may differ from a plain program's by a relative error of at most 0.005.
Values may be sent and summed in bfloat16 or wider, within the bound.
No kernel may reach another device: no remote copies, remote signals or barrier semaphores. Data moves between devices by JAX's collectives and lax.ppermute only.
A program may use at most 64 MiB of HBM per device.

v0:
```python
import math

import jax
import jax.numpy as jnp
from jax import lax
from jax.sharding import PartitionSpec as P

TILE = 128
NT = 2
CH_DEV = 16


def sent_together(arrays, axis, split_dim, concat_dim, along):
    widths = [a.shape[along] for a in arrays]
    both = jnp.concatenate(arrays, axis=along)
    whole = lax.all_to_all(both, axis, split_axis=split_dim, concat_axis=concat_dim, tiled=True)
    return tuple(jnp.split(whole, [sum(widths[:k]) for k in range(1, len(widths))], axis=along))


def gathered_total(shard, axis):
    n = lax.axis_size(axis)
    flat = shard.reshape(-1)
    size = flat.shape[0]
    per = -(-size // (n * 128)) * 128
    flat = jnp.pad(flat, (0, per * n - size))
    got = lax.all_to_all(flat.reshape(n, per), axis, 0, 0, tiled=True)
    part = got.sum(axis=0)
    spread = jnp.broadcast_to(part[None], (n, per))
    whole = lax.all_to_all(spread, axis, 0, 0, tiled=True)
    return whole.reshape(-1)[:size].reshape(shard.shape)


def cmul(ar, ai, br, bi):
    return ar * br - ai * bi, ar * bi + ai * br


def phase_rows(angle):
    c, s = lax.optimization_barrier((jnp.cos(angle), jnp.sin(angle)))
    pw = [(jnp.ones_like(c), jnp.zeros_like(c)), (c, s)]
    for m in range(2, 17):
        if m % 2 == 0:
            pw.append(cmul(*pw[m // 2], *pw[m // 2]))
        else:
            pw.append(cmul(*pw[m - 1], c, s))
    rows = []
    for p in range(32):
        m = p - 16
        if m >= 0:
            rows.append(pw[m])
        else:
            rows.append((pw[-m][0], -pw[-m][1]))
    return rows


def make_subgrids(vis_b, coord_b, count_b, taper):
    kk = vis_b.shape[-1]
    live = (jnp.arange(kk, dtype=jnp.int32)[None, :] < count_b[:, None]).astype(jnp.float32)
    scale_k = 1.0 / math.sqrt(kk)
    vis_re = vis_b[:, 0, :].astype(jnp.float32) * live * scale_k
    vis_im = vis_b[:, 1, :].astype(jnp.float32) * live * scale_k
    step = -2.0 * math.pi / 32.0
    rows_u = phase_rows(step * coord_b[:, 0, :])
    rows_v = phase_rows(step * coord_b[:, 1, :])
    bf = jnp.bfloat16
    a_t = jnp.stack([r for r, _ in rows_u] + [i for _, i in rows_u], axis=1).astype(bf)
    b_rows = [cmul(vis_re, vis_im, r, i) for r, i in rows_v]
    b_t = jnp.stack([r for r, _ in b_rows] + [i for _, i in b_rows], axis=1).astype(bf)
    a_t, b_t = lax.optimization_barrier((a_t, b_t))
    f32 = jnp.float32
    s_all = jnp.einsum("bik,bjk->bij", a_t, b_t, preferred_element_type=f32)
    s_re = s_all[:, :32, :32] - s_all[:, 32:, 32:]
    s_im = s_all[:, :32, 32:] + s_all[:, 32:, :32]
    x2 = jnp.concatenate([taper * s_re, taper * s_im], axis=1)
    centred = jnp.arange(32, dtype=jnp.float32) - 16.0
    angle = -2.0 * math.pi * centred[:, None] * centred[None, :] / 32.0
    f_re, f_im = (jnp.cos(angle), jnp.sin(angle))
    hp = lax.Precision.HIGHEST
    left = jnp.concatenate(
        [jnp.concatenate([f_re, -f_im], 1), jnp.concatenate([f_im, f_re], 1)], 0
    )
    y2 = jnp.einsum("ij,bjq->biq", left, x2, precision=hp)
    ycat = jnp.concatenate([y2[:, :32], y2[:, 32:]], axis=2)
    right = jnp.concatenate(
        [jnp.concatenate([f_re, f_im], 1), jnp.concatenate([-f_im, f_re], 1)], 0
    )
    z2 = jnp.einsum("baj,jk->bak", ycat, right, precision=hp)
    z = z2.reshape(z2.shape[0], 32, 2, 32).transpose(0, 2, 1, 3)
    return (z / 32.0).astype(jnp.bfloat16)


def taylor_weights(chan_local, freq_pos, channels):
    global_chan = (freq_pos * CH_DEV + chan_local).astype(jnp.float32)
    xval = (2.0 * global_chan + 1.0 - channels) / channels
    powers = jnp.arange(NT, dtype=jnp.float32)
    return jnp.where(powers[None, :] == 0.0, 1.0, xval[:, None] ** powers[None, :])


def place_block(tile_acc, inputs):
    patch_b, weight_b, rows_b, cols_b = inputs
    hp = lax.Precision.HIGHEST
    cells = jnp.arange(TILE, dtype=jnp.int32)
    small = jnp.arange(32, dtype=jnp.int32)
    row_hot = (cells[None, :, None] == rows_b[:, None, None] + small[None, None, :]).astype(
        jnp.float32
    )
    col_hot = (cells[None, :, None] == cols_b[:, None, None] + small[None, None, :]).astype(
        jnp.float32
    )
    spread = jnp.einsum("scab,sQb->scaQ", patch_b.astype(jnp.float32), col_hot, precision=hp)
    terms = []
    for term in range(NT):
        weighted = spread * weight_b[:, term][:, None, None, None]
        terms.append(jnp.einsum("sRa,scaQ->cRQ", row_hot, weighted, precision=hp))
    return (tile_acc + jnp.stack(terms, 0), None)


def body(visibilities, coords, vis_counts, cover_tile, offsets, channel, taper):
    n_span = lax.axis_size("span")
    n_freq = lax.axis_size("freq")
    channels = CH_DEV * n_freq
    freq_pos = lax.axis_index("freq")
    sub_count = visibilities.shape[1]
    groups = sub_count // 32
    vis_loc = visibilities[0].reshape(groups, 32, 2, -1)
    coord_loc = coords[0].reshape(groups, 32, 2, -1)
    count_loc = vis_counts[0].reshape(groups, 32)

    def block_work(inputs):
        return make_subgrids(inputs[0], inputs[1], inputs[2], taper)

    patches = lax.map(block_work, (vis_loc, coord_loc, count_loc)).reshape(sub_count, 2, 32, 32)
    dest = cover_tile[0, :, 0]
    row_off = offsets[0, :, 0]
    col_off = offsets[0, :, 1]
    chan_loc = channel[0]
    cap = 2 * sub_count // n_span
    onehot = (dest[:, None] == jnp.arange(n_span, dtype=jnp.int32)[None, :]).astype(jnp.float32)
    order = jnp.arange(sub_count, dtype=jnp.int32)
    lower = (order[:, None] > order[None, :]).astype(jnp.float32)
    earlier = jnp.dot(lower, onehot, preferred_element_type=jnp.float32)
    rank = jnp.sum(earlier * onehot, axis=1).astype(jnp.int32)
    slot = dest * cap + rank
    payload = (
        jnp.zeros((n_span * cap, 2048), jnp.bfloat16).at[slot].set(patches.reshape(sub_count, 2048))
    )
    info = jnp.stack([jnp.ones_like(dest), row_off, col_off, chan_loc], 1).astype(jnp.bfloat16)
    meta = jnp.zeros((n_span * cap, 4), jnp.bfloat16).at[slot].set(info)
    got_payload, got_meta = sent_together(
        (payload.reshape(n_span, cap, 2048), meta.reshape(n_span, cap, 4)), "span", 0, 0, 2
    )
    slots = n_span * cap
    got_meta = got_meta.reshape(slots, 4).astype(jnp.int32)
    valid = got_meta[:, 0].astype(jnp.float32)
    weight = taylor_weights(got_meta[:, 3], freq_pos, channels) * valid[:, None]
    blocks = slots // 32
    inputs = (
        got_payload.reshape(blocks, 32, 2, 32, 32),
        weight.reshape(blocks, 32, NT),
        got_meta[:, 1].reshape(blocks, 32),
        got_meta[:, 2].reshape(blocks, 32),
    )
    start_tile = jnp.zeros((NT, 2, TILE, TILE), jnp.float32)
    local, _ = lax.scan(place_block, start_tile, inputs)
    local = local.reshape(NT, 1, 2, TILE, TILE)
    total = gathered_total(local, "freq")
    scale = TILE / (32.0 * math.sqrt(n_freq * sub_count))
    return total * scale


def solution(mesh):
    return jax.shard_map(
        body,
        mesh=mesh,
        in_specs=(
            P("freq", "span", None, None),
            P("freq", "span", None, None),
            P("freq", "span"),
            P("freq", "span", None),
            P("freq", "span", None),
            P("freq", "span"),
            P(),
        ),
        out_specs=P(None, "span", None, None, None),
        check_vma=False,
    )
```

profile of v0, /device:TPU:1, one launch (start us, length us, event | category | flops | bytes accessed | tf_op | source)
XLA Modules:
  0.0 147.5 jit_solution(3320045486258018474)
XLA Ops:
  0.0 0.9 copy.95
  0.9 4.3 %fusion.320 = (f32[32,1,512]{2,1,0:T(1,128)S(1)}, f32[32,1,512]{2,1,0:T(1,128)S(1)}, f32[32,1,512]{2,1,0:T(1,128)S(1)}, f32[32,1,512]{2,1,0:T(1,128)S(1)}) fusion(f32[32,2,512]{2,1,0:T(2,128)} %bitcast.1342), kind=kLoop, calls=%fused_computation.574 | loop fusion | flops 32768 | bytes 393216 | tf_op jit(solution)/shard_map/while/body/eval_jaxpr/sin | solution.py:38
  5.7 0.8 constant_dynamic-update-slice_fusion.127
  6.4 0.8 constant_dynamic-update-slice_fusion.126
  13.2 0.7 constant_dynamic-update-slice_fusion.63
  13.8 0.7 constant_dynamic-update-slice_fusion.62
  14.5 0.6 constant_dynamic-update-slice_fusion.61
  15.1 0.6 constant_dynamic-update-slice_fusion.60
  16.4 0.7 constant_dynamic-update-slice_fusion.58
  17.0 0.6 constant_dynamic-update-slice_fusion.57
  17.7 0.6 constant_dynamic-update-slice_fusion.56
  18.9 0.6 constant_dynamic-update-slice_fusion.54
  19.5 0.6 constant_dynamic-update-slice_fusion.53
  20.1 0.6 constant_dynamic-update-slice_fusion.52
  20.8 0.6 constant_dynamic-update-slice_fusion.51
  22.0 0.6 constant_dynamic-update-slice_fusion.49
  22.6 0.6 constant_dynamic-update-slice_fusion.48
  23.8 0.6 constant_dynamic-update-slice_fusion.46
  25.7 0.6 constant_dynamic-update-slice_fusion.43
  26.3 0.6 constant_dynamic-update-slice_fusion.42
  27.5 0.6 constant_dynamic-update-slice_fusion.40
  28.7 0.6 constant_dynamic-update-slice_fusion.38
  29.4 0.6 constant_dynamic-update-slice_fusion.37
  30.6 0.6 constant_dynamic-update-slice_fusion.35
  31.8 0.6 constant_dynamic-update-slice_fusion.33
  32.5 0.6 constant_dynamic-update-slice_fusion.32
  33.7 0.6 constant_dynamic-update-slice_fusion.30
  34.3 0.6 constant_dynamic-update-slice_fusion.29
  34.9 0.6 constant_dynamic-update-slice_fusion.28
  36.2 0.6 constant_dynamic-update-slice_fusion.26
  36.8 0.6 constant_dynamic-update-slice_fusion.25
  37.4 0.6 constant_dynamic-update-slice_fusion.24
  39.9 0.6 constant_dynamic-update-slice_fusion.20
  40.5 0.6 constant_dynamic-update-slice_fusion.19
  41.1 0.6 constant_dynamic-update-slice_fusion.18
  41.8 0.6 constant_dynamic-update-slice_fusion.17
  42.4 0.6 constant_dynamic-update-slice_fusion.16
  43.6 0.6 constant_dynamic-update-slice_fusion.14
  44.9 0.6 constant_dynamic-update-slice_fusion.12
  45.5 0.6 constant_dynamic-update-slice_fusion.11
  46.1 0.6 constant_dynamic-update-slice_fusion.10
  46.7 0.6 constant_dynamic-update-slice_fusion.9
  47.3 0.6 constant_dynamic-update-slice_fusion.8
  48.6 0.6 constant_dynamic-update-slice_fusion.6
  49.2 0.6 constant_dynamic-update-slice_fusion.5
  50.4 0.6 constant_dynamic-update-slice_fusion.3
  51.0 0.6 constant_dynamic-update-slice_fusion.2
  51.7 0.6 constant_dynamic-update-slice_fusion.1
  53.0 3.9 %fusion.18 = f32[32,64,64]{1,2,0:T(8,128)S(1)} fusion(bf16[32,64,512]{2,0,1:T(8,128)(2,1)S(1)} %constant_dynamic-update-slice_fusion.64, bf16[32,64,512]{2,0,1:T(8,128)(2,1)} %constant_dynamic-update-slice_fusion), kind=kOutput, calls=%fused_computation.29 | convolution fusion | flops 134217728 | bytes 4718592 | tf_op jit(solution)/shard_map/while/body/eval_jaxpr/bik,bjk->bij/dot_general | solution.py:70
  57.4 0.6 convolution_bitcast_fusion.2
  58.3 1.8 %fusion.21 = bf16[32,32,64]{2,1,0:T(8,128)(2,1)S(1)} fusion(f32[32,32,32]{1,2,0:T(8,128)S(1)} %get-tuple-element.179, f32[32,32,32]{1,2,0:T(8,128)S(1)} %get-tuple-element.178, f32[32,32]{1,0:T(8,128)S(1)} %get-tuple-element.187, f32[32,32]{1,0:T(8,128)S(1)} %get-tuple-element.185, f32[32,32]{1,0:T(8,128)S(1)} %get-tuple-element.186), kind=kOutput, calls=%fused_computation.34 | convolution fusion | flops 50540544 | bytes 405504 | tf_op jit(solution)/shard_map/while/body/eval_jaxpr/baj,jk->bak/dot_general | solution.py:86
  61.2 0.9 scatter_custom_fusion
  62.5 0.8 scatter_custom_fusion.1
  63.4 1.0 pad_maximum_fusion
  64.3 10.5 %all-to-all-start = ((bf16[32,2,2052]{2,1,0:T(2,128)(2,1)}), bf16[32,2,2052]{2,1,0:T(2,128)(2,1)S(1)}, u32[]{:S(2)}, u32[]{:S(2)}) async-start(bf16[32,2,2052]{2,1,0:T(2,128)(2,1)} %pad_maximum_fusion), calls=%async_computation | async-start | bytes 557056 | tf_op jit(solution)/shard_map/all_to_all | solution.py:16
  74.9 9.7 %all-to-all-done = bf16[32,2,2052]{2,1,0:T(2,128)(2,1)S(1)} async-done(((bf16[32,2,2052]{2,1,0:T(2,128)(2,1)}), bf16[32,2,2052]{2,1,0:T(2,128)(2,1)S(1)}, u32[]{:S(2)}, u32[]{:S(2)}) %all-to-all-start) | async-done | bytes 262688 | tf_op jit(solution)/shard_map/all_to_all | solution.py:16
  86.2 6.0 %while.3 = (s32[]{:T(128)}, f32[2,2,128,128]{2,3,1,0:T(8,128)S(1)}, bf16[2,32,2,32,32]{4,3,2,1,0:T(8,128)(2,1)S(1)}, s32[2,32]{1,0:T(2,128)S(1)}, f32[2,32,2]{1,...) while((s32[]{:T(128)}, f32[2,2,128,128]{2,3,1,0:T(8,128)S(1)}, ...), condition=%wide.region_4.5_spmd.clone, body=%wide.region_3.4_spmd.clone.sunk | while | flops 823199744 | bytes 4753515 | solution.py:163
  86.7 1.2 convolution_bitcast_fusion.6
  87.9 1.2 convolution_bitcast_fusion.5
  89.7 1.2 convolution_bitcast_fusion.6
  90.9 1.2 convolution_bitcast_fusion.5
  92.4 34.1 %all_to_all.20 = f32[24,1,2816]{2,1,0:T(1,128)S(1)} all-to-all(f32[24,1,2816]{2,1,0:T(1,128)S(1)} %bitcast.1339), channel_id=1, replica_groups=mesh['span'=32,'freq'=24] {'freq'}, dimensions={0} | all-to-all | bytes 540672 | tf_op jit(solution)/shard_map/all_to_all | solution.py:26
  126.8 19.9 %all_to_all.21 = f32[24,1,2816]{2,1,0:T(1,128)S(1)} all-to-all(f32[24,1,2816]{2,1,0:T(1,128)S(1)} %broadcast_in_dim.39), channel_id=1, replica_groups=mesh['span'=32,'freq'=24] {'freq'}, dimensions={0} | all-to-all | bytes 540672 | tf_op jit(solution)/shard_map/all_to_all | solution.py:29
  146.7 0.7 slice_multiply_fusion
  (144 shorter events, 23.9 us)
Async XLA Ops:
  0.0 7.2 %copy-start = (s32[1,32]{1,0:T(1,128)S(1)}, s32[1,32]{1,0:T(1,128)}, u32[]{:S(2)}) copy-start(s32[1,32]{1,0:T(1,128)} %param.11) | copy-start | bytes 388
  31.8 21.1 %copy-start.1 = (f32[32,32]{1,0:T(8,128)S(1)}, f32[32,32]{1,0:T(8,128)}, u32[]{:S(2)}) copy-start(f32[32,32]{1,0:T(8,128)} %param.15) | copy-start | bytes 12292
  58.2 2.8 %copy-start.3 = (s32[1,32,1]{1,2,0:T(1,128)S(1)}, s32[1,32,1]{1,2,0:T(1,128)}, u32[]{:S(2)}) copy-start(s32[1,32,1]{1,2,0:T(1,128)} %param.12) | copy-start | bytes 388
  58.3 4.0 %copy-start.2 = (s32[1,32,2]{1,2,0:T(2,128)S(1)}, s32[1,32,2]{1,2,0:T(2,128)}, u32[]{:S(2)}) copy-start(s32[1,32,2]{1,2,0:T(2,128)} %param.13) | copy-start | bytes 772
  58.3 4.0 %copy-start.4 = (s32[1,32]{1,0:T(1,128)S(1)}, s32[1,32]{1,0:T(1,128)}, u32[]{:S(2)}) copy-start(s32[1,32]{1,0:T(1,128)} %param.14) | copy-start | bytes 388
  64.3 20.3 %all-to-all-start = ((bf16[32,2,2052]{2,1,0:T(2,128)(2,1)}), bf16[32,2,2052]{2,1,0:T(2,128)(2,1)S(1)}, u32[]{:S(2)}, u32[]{:S(2)}) async-start(bf16[32,2,2052]{2,1,0:T(2,128)(2,1)} %pad_maximum_fusion), calls=%async_computation | async-start | bytes 557056 | tf_op jit(solution)/shard_map/all_to_all | solution.py:16
where the time goes:
time: 148 us; the launch traced here: 147 us
  blocking collectives  54.1 us (37%)
  other arithmetic  45.3 us (31%)
  local copies, waits for them, and re-layouts  15.3 us (10%)
  matrix products  12 us (8%)
  starting transfers between devices  10.5 us (7%)
  waiting for transfers between devices  9.73 us (7%)
    unnamed x113, other arithmetic  37.8 us
    all_to_all x1, blocking collectives, gathered_total(): got = lax.all_to_all(flat.reshape(n, per), axis, 0, 0, tiled=True)  34.1 us
    all_to_all x1, blocking collectives, gathered_total(): whole = lax.all_to_all(spread, axis, 0, 0, tiled=True)  19.9 us
    all_to_all x1, starting transfers between devices, sent_together(): lax.all_to_all(both, axis, split_axis=split_dim, concat_axis=concat_dim,...  10.5 us
    all_to_all x1, waiting for transfers between devices, sent_together(): lax.all_to_all(both, axis, split_axis=split_dim, concat_axis=concat_dim,...  9.73 us
    unnamed x28, local copies, waits for them, and re-layouts  9.62 us
    dot_general x4, matrix products, place_block(): terms.append(jnp.einsum('sRa,scaQ->cRQ', row_hot, weighted, precision=hp))  4.73 us
    sin x1, other arithmetic, phase_rows(): c, s = lax.optimization_barrier((jnp.cos(angle), jnp.sin(angle)))  4.34 us
  transfers between devices with their start and end apart: 1, of which 1 were waited for; matrix products, arithmetic and copies ran while one was open for 0% of the time, Pallas kernels for 0%

commit v1 on v0

--- a/solution.py
+++ b/solution.py
@@ -34,22 +34,33 @@
     return ar * br - ai * bi, ar * bi + ai * br
 
 
-def phase_rows(angle):
-    c, s = lax.optimization_barrier((jnp.cos(angle), jnp.sin(angle)))
-    pw = [(jnp.ones_like(c), jnp.zeros_like(c)), (c, s)]
-    for m in range(2, 17):
-        if m % 2 == 0:
-            pw.append(cmul(*pw[m // 2], *pw[m // 2]))
-        else:
-            pw.append(cmul(*pw[m - 1], c, s))
-    rows = []
-    for p in range(32):
-        m = p - 16
-        if m >= 0:
-            rows.append(pw[m])
-        else:
-            rows.append((pw[-m][0], -pw[-m][1]))
-    return rows
+def bit_powers(c, s, bits, first, count):
+    j = jnp.arange(count, dtype=jnp.int32)[None, :, None]
+    re = jnp.broadcast_to(first[0][:, None, :], (c.shape[0], count, c.shape[1]))
+    im = jnp.broadcast_to(first[1][:, None, :], (c.shape[0], count, c.shape[1]))
+    for i, (br, bi) in enumerate(bits):
+        on = ((j >> i) & 1) == 1
+        mr, mi = cmul(re, im, br[:, None, :], bi[:, None, :])
+        re, im = jnp.where(on, mr, re), jnp.where(on, mi, im)
+    return re, im
+
+
+def phase_table(angle, vis=None):
+    c, s = jnp.cos(angle), jnp.sin(angle)
+    w2 = cmul(c, s, c, s)
+    w4 = cmul(*w2, *w2)
+    w8 = cmul(*w4, *w4)
+    w16 = cmul(*w8, *w8)
+    lo = (w16[0], -w16[1])
+    if vis is not None:
+        lo = cmul(vis[0], vis[1], *lo)
+    one = (jnp.ones_like(c), jnp.zeros_like(c))
+    small = bit_powers(c, s, [(c, s), w2], one, 4)
+    big = bit_powers(c, s, [w4, w8, w16], lo, 8)
+    small, big = lax.optimization_barrier((small, big))
+    re, im = cmul(big[0][:, :, None, :], big[1][:, :, None, :], small[0][:, None], small[1][:, None])
+    n = c.shape[0]
+    return re.reshape(n, 32, -1), im.reshape(n, 32, -1)
 
 
 def make_subgrids(vis_b, coord_b, count_b, taper):
@@ -59,12 +70,11 @@
     vis_re = vis_b[:, 0, :].astype(jnp.float32) * live * scale_k
     vis_im = vis_b[:, 1, :].astype(jnp.float32) * live * scale_k
     step = -2.0 * math.pi / 32.0
-    rows_u = phase_rows(step * coord_b[:, 0, :])
-    rows_v = phase_rows(step * coord_b[:, 1, :])
     bf = jnp.bfloat16
-    a_t = jnp.stack([r for r, _ in rows_u] + [i for _, i in rows_u], axis=1).astype(bf)
-    b_rows = [cmul(vis_re, vis_im, r, i) for r, i in rows_v]
-    b_t = jnp.stack([r for r, _ in b_rows] + [i for _, i in b_rows], axis=1).astype(bf)
+    a_re, a_im = phase_table(step * coord_b[:, 0, :])
+    b_re, b_im = phase_table(step * coord_b[:, 1, :], (vis_re, vis_im))
+    a_t = jnp.concatenate([a_re, a_im], axis=1).astype(bf)
+    b_t = jnp.concatenate([b_re, b_im], axis=1).astype(bf)
     a_t, b_t = lax.optimization_barrier((a_t, b_t))
     f32 = jnp.float32
     s_all = jnp.einsum("bik,bjk->bij", a_t, b_t, preferred_element_type=f32)

time: 148 us -> 111 us (0.75)
  other arithmetic: 45.3 us -> 14.5 us
  local copies, waits for them, and re-layouts: 15.3 us -> 10.4 us
  matrix products: 12 us -> 10.4 us
    unnamed x113 -> x1, other arithmetic: 37.8 us -> 0.01 us
    unnamed x28 -> x16, local copies, waits for them, and re-layouts: 9.62 us -> 2.24 us
    sin x1 -> x0, other arithmetic: 4.34 us -> none  [phase_rows(): c, s = lax.optimization_barrier((jnp.cos(angle), jnp.sin(angle)))]
    another operation x2 -> x3, other arithmetic: 0.1 us -> 3.41 us  [the longest x1 0.09 us: make_subgrids(): jnp.stack([r for r, _ in b_rows] + [i for _, i in b_rows], axis=1)]
    concatenate x0 -> x2, other arithmetic: none -> 3.01 us  [the longest x1 1.55 us: make_subgrids(): b_t = jnp.concatenate([b_re, b_im], axis=1).astype(bf)]
    select_n x0 -> x2, other arithmetic: none -> 2.82 us  [bit_powers(): re, im = (jnp.where(on, mr, re), jnp.where(on, mi, im))]
    sub x0 -> x2, local copies, waits for them, and re-layouts: none -> 2.23 us  [cmul(): return (ar * br - ai * bi, ar * bi + ai * br)]
    dot_general x1, matrix products: 3.92 us -> 2.28 us  [make_subgrids(): s_all = jnp.einsum('bik,bjk->bij', a_t, b_t, preferred_element_type=f32)]
where the time goes in v1:
time: 111 us; the launch traced here: 110 us
  blocking collectives  54.1 us (49%)
  other arithmetic  14.5 us (13%)
  starting transfers between devices  10.7 us (10%)
  local copies, waits for them, and re-layouts  10.4 us (9%)
  matrix products  10.4 us (9%)
  waiting for transfers between devices  9.55 us (9%)
    all_to_all x1, blocking collectives, gathered_total(): got = lax.all_to_all(flat.reshape(n, per), axis, 0, 0, tiled=True)  34.1 us
    all_to_all x1, blocking collectives, gathered_total(): whole = lax.all_to_all(spread, axis, 0, 0, tiled=True)  19.9 us
    all_to_all x1, starting transfers between devices, sent_together(): lax.all_to_all(both, axis, split_axis=split_dim, concat_axis=concat_dim,...  10.7 us
    all_to_all x1, waiting for transfers between devices, sent_together(): lax.all_to_all(both, axis, split_axis=split_dim, concat_axis=concat_dim,...  9.55 us
    dot_general x4, matrix products, place_block(): terms.append(jnp.einsum('sRa,scaQ->cRQ', row_hot, weighted, precision=hp))  4.72 us
    another operation x3, other arithmetic  3.41 us
    select_n x2, other arithmetic, bit_powers(): re, im = (jnp.where(on, mr, re), jnp.where(on, mi, im))  2.82 us
    dot_general x1, matrix products, make_subgrids(): s_all = jnp.einsum('bik,bjk->bij', a_t, b_t, preferred_element_type=f32)  2.28 us
  transfers between devices with their start and end apart: 1, of which 1 were waited for; matrix products, arithmetic and copies ran while one was open for 0% of the time, Pallas kernels for 0%

profile of v1, /device:TPU:1, one launch (start us, length us, event | category | flops | bytes accessed | tf_op | source)
XLA Modules:
  0.0 110.0 jit_solution(1349824669039513673)
XLA Ops:
  0.0 0.9 copy.119
  1.0 0.9 copy.120
  1.8 0.6 fusion.92
  2.4 1.0 fusion.54
  3.4 0.6 fusion.55
  4.0 1.1 %select_select_fusion.4 = (f32[32,4,512]{2,1,0:T(4,128)S(1)}, f32[32,4,512]{2,1,0:T(4,128)S(1)}, f32[32,4,512]{2,1,0:T(4,128)S(1)}, f32[32,4,512]{2,1,0:T(4,128)}) fusion(f32[32,512]{1,0:T(8,128)S(1)} %get-tuple-element.144, f32[32,512]{1,0:T(8,128)S(1)} %get-tuple-element.151, f32[32,512]{1,0:T(8,128)S(1)} %get-tuple-element.145, ...), kind=kLoop, calls=%fused_computation.83 | loop fusion | flops 1310720 | bytes 1572872 | tf_op jit(solution)/shard_map/while/body/eval_jaxpr/jit(_where)/select_n | solution.py:44
  5.1 1.7 %fusion.40 = (f32[32,8,512]{2,1,0:T(8,128)S(1)}, f32[32,8,512]{2,1,0:T(8,128)S(1)}, f32[32,8,512]{2,1,0:T(8,128)}, f32[32,8,512]{2,1,0:T(8,128)}) fusion(f32[32,512]{1,0:T(8,128)S(1)} %get-tuple-element.136, f32[32,512]{1,0:T(8,128)S(1)} %get-tuple-element.140, f32[32,512]{1,0:T(8,128)S(1)} %get-tuple-element.135, f32[32,512]{1,0:T(8,128)S(1)} %get-tuple-element.113, ...), kind=kLoop, calls=%fused_computation.72 | loop fusion | flops 4718592 | bytes 3080216 | tf_op jit(solution)/shard_map/while/body/eval_jaxpr/jit(_where)/select_n | solution.py:44
  6.8 1.1 %subtract_convert_fusion = (bf16[32,8,4,512]{3,2,1,0:T(4,128)(2,1)S(1)}, bf16[32,8,4,512]{3,2,1,0:T(4,128)(2,1)S(1)}) fusion(f32[32,4,512]{2,1,0:T(4,128)S(1)} %get-tuple-element.72, f32[32,8,512]{2,1,0:T(8,128)S(1)} %get-tuple-element.71, f32[32,4,512]{2,1,0:T(4,128)S(1)} %get-tuple-element.70, f32[32,8,512]{2,1,0:T(8,128)S(1)} %get-tuple-element.69), kind=kLoop, calls=%fused_computation.32 | loop fusion | flops 4194304 | bytes 3670016 | tf_op jit(solution)/shard_map/convert.13
  8.0 0.3 add.263
  8.2 1.1 %sub.189 = bf16[32,32,512]{2,1,0:T(8,128)(2,1)} reshape(bf16[32,8,4,512]{3,2,1,0:T(4,128)(2,1)S(1)} %get-tuple-element.118) | data formatting | bytes 2097152 | tf_op jit(solution)/shard_map/while/body/eval_jaxpr/sub | solution.py:34
  9.4 2.3 %subtract_convert_fusion.1 = (bf16[32,8,4,512]{3,2,1,0:T(4,128)(2,1)S(1)}, bf16[32,8,4,512]{3,2,1,0:T(4,128)(2,1)S(1)}) fusion(f32[32,4,512]{2,1,0:T(4,128)} %get-tuple-element.68, f32[32,8,512]{2,1,0:T(8,128)} %get-tuple-element.67, f32[32,4,512]{2,1,0:T(4,128)S(1)} %get-tuple-element.66, f32[32,8,512]{2,1,0:T(8,128)} %get-tuple-element.65), kind=kLoop, calls=%fused_computation.34 | loop fusion | flops 4194304 | bytes 3670016 | tf_op jit(solution)/shard_map/convert.17
  11.6 1.2 %add.251 = bf16[32,32,512]{2,1,0:T(8,128)(2,1)} reshape(bf16[32,8,4,512]{3,2,1,0:T(4,128)(2,1)S(1)} %get-tuple-element.121) | data formatting | bytes 2097152 | tf_op jit(solution)/shard_map/while/body/eval_jaxpr/add | solution.py:34
  12.8 1.1 %sub.177 = bf16[32,32,512]{2,1,0:T(8,128)(2,1)} reshape(bf16[32,8,4,512]{3,2,1,0:T(4,128)(2,1)S(1)} %get-tuple-element.120) | data formatting | bytes 2097152 | tf_op jit(solution)/shard_map/while/body/eval_jaxpr/sub | solution.py:34
  13.9 1.5 %pad_maximum_fusion.1 = bf16[32,64,512]{2,1,0:T(8,128)(2,1)S(1)} fusion(bf16[32,32,512]{2,1,0:T(8,128)(2,1)S(1)} %add.263, bf16[32,32,512]{2,1,0:T(8,128)(2,1)} %sub.189), kind=kLoop, calls=%fused_computation.30 | loop fusion | flops 4194304 | bytes 4194304 | tf_op jit(solution)/shard_map/while/body/eval_jaxpr/concatenate | solution.py:77
  15.5 0.3 copy-done.1
  15.8 1.5 %pad_maximum_fusion = bf16[32,64,512]{2,1,0:T(8,128)(2,1)} fusion(bf16[32,32,512]{2,1,0:T(8,128)(2,1)S(1)} %copy-done, bf16[32,32,512]{2,1,0:T(8,128)(2,1)S(1)} %copy-done.1), kind=kLoop, calls=%fused_computation.29 | loop fusion | flops 4194304 | bytes 4194304 | tf_op jit(solution)/shard_map/while/body/eval_jaxpr/concatenate | solution.py:76
  17.2 0.1 copy.101
  17.3 2.3 %fusion.96 = f32[32,64,64]{1,2,0:T(8,128)S(1)} fusion(bf16[32,64,512]{2,1,0:T(8,128)(2,1)} %pad_maximum_fusion, bf16[32,64,512]{2,1,0:T(8,128)(2,1)S(1)} %pad_maximum_fusion.1), kind=kOutput, calls=%fused_computation.209 | convolution fusion | flops 134217728 | bytes 4718592 | tf_op jit(solution)/shard_map/while/body/eval_jaxpr/bik,bjk->bij/dot_general | solution.py:80
  19.6 0.3 fusion.44
  19.9 0.1 fusion.83
  20.1 0.6 convolution_bitcast_fusion.2
  20.7 0.2 fusion.95
  21.0 1.8 %fusion.18 = bf16[32,32,64]{2,1,0:T(8,128)(2,1)S(1)} fusion(f32[32,32,32]{1,2,0:T(8,128)S(1)} %get-tuple-element.127, f32[32,32,32]{1,2,0:T(8,128)S(1)} %get-tuple-element.126, f32[32,32]{1,0:T(8,128)S(1)} %get-tuple-element.159, f32[32,32]{1,0:T(8,128)S(1)} %get-tuple-element.157, f32[32,32]{1,0:T(8,128)S(1)} %get-tuple-element.158), kind=kOutput, calls=%fused_computation.37 | convolution fusion | flops 50540544 | bytes 405504 | tf_op jit(solution)/shard_map/while/body/eval_jaxpr/baj,jk->bak/dot_general | solution.py:96
  22.8 0.2 convert_element_type.68
  23.1 0.1 copy.118
  23.2 0.5 reshape.318
  23.7 0.1 fusion.19
  23.9 0.9 scatter_custom_fusion
  24.8 0.2 reshape.309
  25.0 0.1 pad_maximum_fusion.9
  25.1 0.1 copy.106
  25.2 0.7 scatter_custom_fusion.1
  25.9 1.0 pad_maximum_fusion.2
  26.9 10.7 %all-to-all-start = ((bf16[32,2,2052]{2,1,0:T(2,128)(2,1)}), bf16[32,2,2052]{2,1,0:T(2,128)(2,1)S(1)}, u32[]{:S(2)}, u32[]{:S(2)}) async-start(bf16[32,2,2052]{2,1,0:T(2,128)(2,1)} %pad_maximum_fusion.2), calls=%async_computation | async-start | bytes 557056 | tf_op jit(solution)/shard_map/all_to_all | solution.py:16
  37.6 9.6 %all-to-all-done = bf16[32,2,2052]{2,1,0:T(2,128)(2,1)S(1)} async-done(((bf16[32,2,2052]{2,1,0:T(2,128)(2,1)}), bf16[32,2,2052]{2,1,0:T(2,128)(2,1)S(1)}, u32[]{:S(2)}, u32[]{:S(2)}) %all-to-all-start) | async-done | bytes 262688 | tf_op jit(solution)/shard_map/all_to_all | solution.py:16
  47.2 0.2 slice_reduce_fusion
  47.4 0.1 fusion.70
  47.5 0.1 copy.114
  47.6 0.1 pow.16
  47.7 0.1 mul.1133
  47.7 0.2 split.8
  47.9 0.5 reshape.311
  48.5 0.1 reshape_squeeze.6
  48.5 0.1 reshape_squeeze.7
  48.6 0.1 select_multiply_fusion.18
  48.7 6.0 %while.3 = (s32[]{:T(128)}, f32[2,2,128,128]{2,3,1,0:T(8,128)S(1)}, bf16[2,32,2,32,32]{4,3,2,1,0:T(8,128)(2,1)S(1)}, s32[2,32]{1,0:T(2,128)S(1)}, f32[2,32,2]{1,...) while((s32[]{:T(128)}, f32[2,2,128,128]{2,3,1,0:T(8,128)S(1)}, ...), condition=%wide.region_4.5_spmd.clone, body=%wide.region_3.4_spmd.clone.sunk | while | flops 823199744 | bytes 4753515 | solution.py:173
  48.7 0.1 iota_add_fusion.5
  48.8 0.4 fusion.114
  49.1 0.1 iota_add_fusion.6
  49.2 1.2 %convolution_bitcast_fusion.6 = f32[1,2,128,128]{2,3,1,0:T(8,128)S(1)} fusion(f32[32,2,32,128]{3,2,1,0:T(8,128)S(1)} %fusion.114, f32[32]{0:T(128)S(1)} %get-tuple-element.214, s32[32,32]{1,0:T(8,128)S(1)} %iota_add_fusion.6), kind=kOutput, calls=%fused_computation.3.clone.1 | convolution fusion | flops 403046400 | bytes 1183872 | tf_op jit(solution)/shard_map/while/body/eval_jaxpr/sRa,scaQ->cRQ/dot_general | solution.py:123
  50.4 1.2 %convolution_bitcast_fusion.5 = f32[1,2,128,128]{2,3,1,0:T(8,128)S(1)} fusion(f32[32,2,32,128]{3,2,1,0:T(8,128)S(1)} %fusion.114, f32[32]{0:T(128)S(1)} %get-tuple-element.212, s32[32,32]{1,0:T(8,128)S(1)} %iota_add_fusion.6), kind=kOutput, calls=%fused_computation.2.clone.1 | convolution fusion | flops 403046400 | bytes 1183872 | tf_op jit(solution)/shard_map/while/body/eval_jaxpr/sRa,scaQ->cRQ/dot_general | solution.py:123
  51.6 0.1 maximum_add_fusion.2
  51.7 0.1 iota_add_fusion.5
  51.8 0.4 fusion.114
  52.2 0.1 iota_add_fusion.6
  52.2 1.2 %convolution_bitcast_fusion.6 = f32[1,2,128,128]{2,3,1,0:T(8,128)S(1)} fusion(f32[32,2,32,128]{3,2,1,0:T(8,128)S(1)} %fusion.114, f32[32]{0:T(128)S(1)} %get-tuple-element.214, s32[32,32]{1,0:T(8,128)S(1)} %iota_add_fusion.6), kind=kOutput, calls=%fused_computation.3.clone.1 | convolution fusion | flops 403046400 | bytes 1183872 | tf_op jit(solution)/shard_map/while/body/eval_jaxpr/sRa,scaQ->cRQ/dot_general | solution.py:123
  53.4 1.2 %convolution_bitcast_fusion.5 = f32[1,2,128,128]{2,3,1,0:T(8,128)S(1)} fusion(f32[32,2,32,128]{3,2,1,0:T(8,128)S(1)} %fusion.114, f32[32]{0:T(128)S(1)} %get-tuple-element.212, s32[32,32]{1,0:T(8,128)S(1)} %iota_add_fusion.6), kind=kOutput, calls=%fused_computation.2.clone.1 | convolution fusion | flops 403046400 | bytes 1183872 | tf_op jit(solution)/shard_map/while/body/eval_jaxpr/sRa,scaQ->cRQ/dot_general | solution.py:123
  54.6 0.1 maximum_add_fusion.2
  54.7 0.1 copy.108
  54.9 34.1 %all_to_all.20 = f32[24,1,2816]{2,1,0:T(1,128)S(1)} all-to-all(f32[24,1,2816]{2,1,0:T(1,128)S(1)} %bitcast.191), channel_id=1, replica_groups=mesh['span'=32,'freq'=24] {'freq'}, dimensions={0} | all-to-all | bytes 540672 | tf_op jit(solution)/shard_map/all_to_all | solution.py:26
  89.0 0.2 reduce_sum.19
  89.2 0.1 broadcast_in_dim.341
  89.3 19.9 %all_to_all.21 = f32[24,1,2816]{2,1,0:T(1,128)S(1)} all-to-all(f32[24,1,2816]{2,1,0:T(1,128)S(1)} %broadcast_in_dim.341), channel_id=1, replica_groups=mesh['span'=32,'freq'=24] {'freq'}, dimensions={0} | all-to-all | bytes 540672 | tf_op jit(solution)/shard_map/all_to_all | solution.py:29
  109.3 0.7 slice_multiply_fusion
  (32 shorter events, 0.2 us)
Async XLA Ops:
  13.9 1.6 %copy-start = (bf16[32,32,512]{2,1,0:T(8,128)(2,1)S(1)}, bf16[32,32,512]{2,1,0:T(8,128)(2,1)}, u32[]{:S(2)}) copy-start(bf16[32,32,512]{2,1,0:T(8,128)(2,1)} %add.251) | copy-start | bytes 3145732
  13.9 1.9 %copy-start.1 = (bf16[32,32,512]{2,1,0:T(8,128)(2,1)S(1)}, bf16[32,32,512]{2,1,0:T(8,128)(2,1)}, u32[]{:S(2)}) copy-start(bf16[32,32,512]{2,1,0:T(8,128)(2,1)} %sub.177) | copy-start | bytes 3145732
  15.8 1.5 %copy-start.2 = (f32[32,32]{1,0:T(8,128)S(1)}, f32[32,32]{1,0:T(8,128)}, u32[]{:S(2)}) copy-start(f32[32,32]{1,0:T(8,128)} %param.15) | copy-start | bytes 12292
  20.9 2.8 %copy-start.4 = (s32[1,32,1]{1,2,0:T(1,128)S(1)}, s32[1,32,1]{1,2,0:T(1,128)}, u32[]{:S(2)}) copy-start(s32[1,32,1]{1,2,0:T(1,128)} %param.12) | copy-start | bytes 388
  21.0 4.0 %copy-start.3 = (s32[1,32,2]{1,2,0:T(2,128)S(1)}, s32[1,32,2]{1,2,0:T(2,128)}, u32[]{:S(2)}) copy-start(s32[1,32,2]{1,2,0:T(2,128)} %param.13) | copy-start | bytes 772
  21.0 4.0 %copy-start.5 = (s32[1,32]{1,0:T(1,128)S(1)}, s32[1,32]{1,0:T(1,128)}, u32[]{:S(2)}) copy-start(s32[1,32]{1,0:T(1,128)} %param.14) | copy-start | bytes 388
  26.9 20.3 %all-to-all-start = ((bf16[32,2,2052]{2,1,0:T(2,128)(2,1)}), bf16[32,2,2052]{2,1,0:T(2,128)(2,1)S(1)}, u32[]{:S(2)}, u32[]{:S(2)}) async-start(bf16[32,2,2052]{2,1,0:T(2,128)(2,1)} %pad_maximum_fusion.2), calls=%async_computation | async-start | bytes 557056 | tf_op jit(solution)/shard_map/all_to_all | solution.py:16

commit v2 on v1

--- a/solution.py
+++ b/solution.py
@@ -23,9 +23,9 @@
     size = flat.shape[0]
     per = -(-size // (n * 128)) * 128
     flat = jnp.pad(flat, (0, per * n - size))
-    got = lax.all_to_all(flat.reshape(n, per), axis, 0, 0, tiled=True)
+    got = lax.all_to_all(flat.reshape(n, per // 128, 128), axis, 0, 0, tiled=True)
     part = got.sum(axis=0)
-    spread = jnp.broadcast_to(part[None], (n, per))
+    spread = jnp.broadcast_to(part[None], (n, per // 128, 128))
     whole = lax.all_to_all(spread, axis, 0, 0, tiled=True)
     return whole.reshape(-1)[:size].reshape(shard.shape)
 

time: 111 us -> 112 us (level)
  blocking collectives: 54.1 us -> 55.5 us
where the time goes in v2:
time: 112 us; the launch traced here: 111 us
  blocking collectives  55.5 us (50%)
  other arithmetic  14.4 us (13%)
  starting transfers between devices  10.7 us (10%)
  matrix products  10.4 us (9%)
  local copies, waits for them, and re-layouts  10.3 us (9%)
  waiting for transfers between devices  9.55 us (9%)
    all_to_all x1, blocking collectives, gathered_total(): lax.all_to_all(flat.reshape(n, per // 128, 128), axis, 0, 0, tiled=True)  34.7 us
    all_to_all x1, blocking collectives, gathered_total(): whole = lax.all_to_all(spread, axis, 0, 0, tiled=True)  20.8 us
    all_to_all x1, starting transfers between devices, sent_together(): lax.all_to_all(both, axis, split_axis=split_dim, concat_axis=concat_dim,...  10.7 us
    all_to_all x1, waiting for transfers between devices, sent_together(): lax.all_to_all(both, axis, split_axis=split_dim, concat_axis=concat_dim,...  9.55 us
    dot_general x4, matrix products, place_block(): terms.append(jnp.einsum('sRa,scaQ->cRQ', row_hot, weighted, precision=hp))  4.72 us
    another operation x3, other arithmetic  3.41 us
    select_n x2, other arithmetic, bit_powers(): re, im = (jnp.where(on, mr, re), jnp.where(on, mi, im))  2.82 us
    dot_general x1, matrix products, make_subgrids(): s_all = jnp.einsum('bik,bjk->bij', a_t, b_t, preferred_element_type=f32)  2.28 us
  transfers between devices with their start and end apart: 1, of which 1 were waited for; matrix products, arithmetic and copies ran while one was open for 0% of the time, Pallas kernels for 0%

profile of v2, /device:TPU:1, one launch (start us, length us, event | category | flops | bytes accessed | tf_op | source)
XLA Modules:
  0.0 111.2 jit_solution(11829290864186094437)
XLA Ops:
  0.0 0.9 copy.80
  1.0 0.9 copy.81
  1.8 0.6 fusion.92
  2.4 1.0 fusion.54
  3.4 0.6 fusion.55
  4.0 1.1 %select_select_fusion.4 = (f32[32,4,512]{2,1,0:T(4,128)S(1)}, f32[32,4,512]{2,1,0:T(4,128)S(1)}, f32[32,4,512]{2,1,0:T(4,128)S(1)}, f32[32,4,512]{2,1,0:T(4,128)}) fusion(f32[32,512]{1,0:T(8,128)S(1)} %get-tuple-element.144, f32[32,512]{1,0:T(8,128)S(1)} %get-tuple-element.151, f32[32,512]{1,0:T(8,128)S(1)} %get-tuple-element.145, ...), kind=kLoop, calls=%fused_computation.83 | loop fusion | flops 1310720 | bytes 1572872 | tf_op jit(solution)/shard_map/while/body/eval_jaxpr/jit(_where)/select_n | solution.py:44
  5.1 1.7 %fusion.40 = (f32[32,8,512]{2,1,0:T(8,128)S(1)}, f32[32,8,512]{2,1,0:T(8,128)S(1)}, f32[32,8,512]{2,1,0:T(8,128)}, f32[32,8,512]{2,1,0:T(8,128)}) fusion(f32[32,512]{1,0:T(8,128)S(1)} %get-tuple-element.136, f32[32,512]{1,0:T(8,128)S(1)} %get-tuple-element.140, f32[32,512]{1,0:T(8,128)S(1)} %get-tuple-element.135, f32[32,512]{1,0:T(8,128)S(1)} %get-tuple-element.113, ...), kind=kLoop, calls=%fused_computation.72 | loop fusion | flops 4718592 | bytes 3080216 | tf_op jit(solution)/shard_map/while/body/eval_jaxpr/jit(_where)/select_n | solution.py:44
  6.8 1.1 %subtract_convert_fusion = (bf16[32,8,4,512]{3,2,1,0:T(4,128)(2,1)S(1)}, bf16[32,8,4,512]{3,2,1,0:T(4,128)(2,1)S(1)}) fusion(f32[32,4,512]{2,1,0:T(4,128)S(1)} %get-tuple-element.72, f32[32,8,512]{2,1,0:T(8,128)S(1)} %get-tuple-element.71, f32[32,4,512]{2,1,0:T(4,128)S(1)} %get-tuple-element.70, f32[32,8,512]{2,1,0:T(8,128)S(1)} %get-tuple-element.69), kind=kLoop, calls=%fused_computation.32 | loop fusion | flops 4194304 | bytes 3670016 | tf_op jit(solution)/shard_map/convert.13
  8.0 0.3 add.263
  8.2 1.1 sub.189
  9.4 2.3 %subtract_convert_fusion.1 = (bf16[32,8,4,512]{3,2,1,0:T(4,128)(2,1)S(1)}, bf16[32,8,4,512]{3,2,1,0:T(4,128)(2,1)S(1)}) fusion(f32[32,4,512]{2,1,0:T(4,128)} %get-tuple-element.68, f32[32,8,512]{2,1,0:T(8,128)} %get-tuple-element.67, f32[32,4,512]{2,1,0:T(4,128)S(1)} %get-tuple-element.66, f32[32,8,512]{2,1,0:T(8,128)} %get-tuple-element.65), kind=kLoop, calls=%fused_computation.34 | loop fusion | flops 4194304 | bytes 3670016 | tf_op jit(solution)/shard_map/convert.17
  11.6 1.2 %add.251 = bf16[32,32,512]{2,1,0:T(8,128)(2,1)} reshape(bf16[32,8,4,512]{3,2,1,0:T(4,128)(2,1)S(1)} %get-tuple-element.121) | data formatting | bytes 2097152 | tf_op jit(solution)/shard_map/while/body/eval_jaxpr/add | solution.py:34
  12.8 1.1 %sub.177 = bf16[32,32,512]{2,1,0:T(8,128)(2,1)} reshape(bf16[32,8,4,512]{3,2,1,0:T(4,128)(2,1)S(1)} %get-tuple-element.120) | data formatting | bytes 2097152 | tf_op jit(solution)/shard_map/while/body/eval_jaxpr/sub | solution.py:34
  13.9 1.5 %pad_maximum_fusion.1 = bf16[32,64,512]{2,1,0:T(8,128)(2,1)S(1)} fusion(bf16[32,32,512]{2,1,0:T(8,128)(2,1)S(1)} %add.263, bf16[32,32,512]{2,1,0:T(8,128)(2,1)} %sub.189), kind=kLoop, calls=%fused_computation.30 | loop fusion | flops 4194304 | bytes 4194304 | tf_op jit(solution)/shard_map/while/body/eval_jaxpr/concatenate | solution.py:77
  15.5 0.3 copy-done.1
  15.8 1.5 %pad_maximum_fusion = bf16[32,64,512]{2,1,0:T(8,128)(2,1)} fusion(bf16[32,32,512]{2,1,0:T(8,128)(2,1)S(1)} %copy-done, bf16[32,32,512]{2,1,0:T(8,128)(2,1)S(1)} %copy-done.1), kind=kLoop, calls=%fused_computation.29 | loop fusion | flops 4194304 | bytes 4194304 | tf_op jit(solution)/shard_map/while/body/eval_jaxpr/concatenate | solution.py:76
  17.2 0.1 copy.64
  17.3 2.3 %fusion.96 = f32[32,64,64]{1,2,0:T(8,128)S(1)} fusion(bf16[32,64,512]{2,1,0:T(8,128)(2,1)} %pad_maximum_fusion, bf16[32,64,512]{2,1,0:T(8,128)(2,1)S(1)} %pad_maximum_fusion.1), kind=kOutput, calls=%fused_computation.209 | convolution fusion | flops 134217728 | bytes 4718592 | tf_op jit(solution)/shard_map/while/body/eval_jaxpr/bik,bjk->bij/dot_general | solution.py:80
  19.6 0.3 fusion.44
  19.9 0.1 fusion.83
  20.1 0.6 convolution_bitcast_fusion.2
  20.7 0.2 fusion.95
  20.9 0.0 copy-start.4
  21.0 0.0 copy-start.3
  21.0 1.8 %fusion.18 = bf16[32,32,64]{2,1,0:T(8,128)(2,1)S(1)} fusion(f32[32,32,32]{1,2,0:T(8,128)S(1)} %get-tuple-element.127, f32[32,32,32]{1,2,0:T(8,128)S(1)} %get-tuple-element.126, f32[32,32]{1,0:T(8,128)S(1)} %get-tuple-element.159, f32[32,32]{1,0:T(8,128)S(1)} %get-tuple-element.157, f32[32,32]{1,0:T(8,128)S(1)} %get-tuple-element.158), kind=kOutput, calls=%fused_computation.37 | convolution fusion | flops 50540544 | bytes 405504 | tf_op jit(solution)/shard_map/while/body/eval_jaxpr/baj,jk->bak/dot_general | solution.py:96
  22.8 0.2 convert_element_type.68
  23.1 0.1 copy.79
  23.2 0.5 reshape.312
  23.7 0.1 fusion.19
  23.9 0.9 scatter_custom_fusion
  24.8 0.2 reshape.302
  25.0 0.1 pad_maximum_fusion.9
  25.1 0.1 copy.69
  25.2 0.7 scatter_custom_fusion.1
  25.9 1.0 pad_maximum_fusion.2
  26.9 10.7 %all-to-all-start = ((bf16[32,2,2052]{2,1,0:T(2,128)(2,1)}), bf16[32,2,2052]{2,1,0:T(2,128)(2,1)S(1)}, u32[]{:S(2)}, u32[]{:S(2)}) async-start(bf16[32,2,2052]{2,1,0:T(2,128)(2,1)} %pad_maximum_fusion.2), calls=%async_computation | async-start | bytes 557056 | tf_op jit(solution)/shard_map/all_to_all | solution.py:16
  37.6 9.6 %all-to-all-done = bf16[32,2,2052]{2,1,0:T(2,128)(2,1)S(1)} async-done(((bf16[32,2,2052]{2,1,0:T(2,128)(2,1)}), bf16[32,2,2052]{2,1,0:T(2,128)(2,1)S(1)}, u32[]{:S(2)}, u32[]{:S(2)}) %all-to-all-start) | async-done | bytes 262688 | tf_op jit(solution)/shard_map/all_to_all | solution.py:16
  47.2 0.2 slice_reduce_fusion
  47.4 0.1 fusion.70
  47.5 0.1 copy.75
  47.6 0.1 pow.16
  47.7 0.1 mul.1133
  47.7 0.2 split.8
  47.9 0.5 reshape.304
  48.5 0.1 reshape_squeeze.6
  48.5 0.1 reshape_squeeze.7
  48.6 0.1 select_multiply_fusion.18
  48.7 6.0 %while.3 = (s32[]{:T(128)}, f32[2,2,128,128]{2,3,1,0:T(8,128)S(1)}, bf16[2,32,2,32,32]{4,3,2,1,0:T(8,128)(2,1)S(1)}, s32[2,32]{1,0:T(2,128)S(1)}, f32[2,32,2]{1,...) while((s32[]{:T(128)}, f32[2,2,128,128]{2,3,1,0:T(8,128)S(1)}, ...), condition=%wide.region_4.5_spmd.clone, body=%wide.region_3.4_spmd.clone.sunk | while | flops 823199744 | bytes 4753515 | solution.py:173
  48.7 0.1 iota_add_fusion.5
  48.8 0.4 fusion.114
  49.1 0.1 iota_add_fusion.6
  49.2 1.2 %convolution_bitcast_fusion.6 = f32[1,2,128,128]{2,3,1,0:T(8,128)S(1)} fusion(f32[32,2,32,128]{3,2,1,0:T(8,128)S(1)} %fusion.114, f32[32]{0:T(128)S(1)} %get-tuple-element.214, s32[32,32]{1,0:T(8,128)S(1)} %iota_add_fusion.6), kind=kOutput, calls=%fused_computation.3.clone.1 | convolution fusion | flops 403046400 | bytes 1183872 | tf_op jit(solution)/shard_map/while/body/eval_jaxpr/sRa,scaQ->cRQ/dot_general | solution.py:123
  50.4 1.2 %convolution_bitcast_fusion.5 = f32[1,2,128,128]{2,3,1,0:T(8,128)S(1)} fusion(f32[32,2,32,128]{3,2,1,0:T(8,128)S(1)} %fusion.114, f32[32]{0:T(128)S(1)} %get-tuple-element.212, s32[32,32]{1,0:T(8,128)S(1)} %iota_add_fusion.6), kind=kOutput, calls=%fused_computation.2.clone.1 | convolution fusion | flops 403046400 | bytes 1183872 | tf_op jit(solution)/shard_map/while/body/eval_jaxpr/sRa,scaQ->cRQ/dot_general | solution.py:123
  51.6 0.1 maximum_add_fusion.2
  51.7 0.1 iota_add_fusion.5
  51.8 0.4 fusion.114
  52.2 0.1 iota_add_fusion.6
  52.2 1.2 %convolution_bitcast_fusion.6 = f32[1,2,128,128]{2,3,1,0:T(8,128)S(1)} fusion(f32[32,2,32,128]{3,2,1,0:T(8,128)S(1)} %fusion.114, f32[32]{0:T(128)S(1)} %get-tuple-element.214, s32[32,32]{1,0:T(8,128)S(1)} %iota_add_fusion.6), kind=kOutput, calls=%fused_computation.3.clone.1 | convolution fusion | flops 403046400 | bytes 1183872 | tf_op jit(solution)/shard_map/while/body/eval_jaxpr/sRa,scaQ->cRQ/dot_general | solution.py:123
  53.4 1.2 %convolution_bitcast_fusion.5 = f32[1,2,128,128]{2,3,1,0:T(8,128)S(1)} fusion(f32[32,2,32,128]{3,2,1,0:T(8,128)S(1)} %fusion.114, f32[32]{0:T(128)S(1)} %get-tuple-element.212, s32[32,32]{1,0:T(8,128)S(1)} %iota_add_fusion.6), kind=kOutput, calls=%fused_computation.2.clone.1 | convolution fusion | flops 403046400 | bytes 1183872 | tf_op jit(solution)/shard_map/while/body/eval_jaxpr/sRa,scaQ->cRQ/dot_general | solution.py:123
  54.6 0.1 maximum_add_fusion.2
  54.7 0.1 copy.71
  54.9 34.7 %all_to_all.15 = f32[24,22,128]{2,1,0:T(8,128)S(1)} all-to-all(f32[24,22,128]{2,1,0:T(8,128)S(1)} %reshape.305), channel_id=1, replica_groups=mesh['span'=32,'freq'=24] {'freq'}, dimensions={0} | all-to-all | bytes 540672 | tf_op jit(solution)/shard_map/all_to_all | solution.py:26
  89.7 20.8 %all_to_all.16 = f32[24,22,128]{2,1,0:T(8,128)S(1)} all-to-all(f32[24,22,128]{2,1,0:T(8,128)S(1)} %broadcast_in_dim.341), channel_id=1, replica_groups=mesh['span'=32,'freq'=24] {'freq'}, dimensions={0} | all-to-all | bytes 540672 | tf_op jit(solution)/shard_map/all_to_all | solution.py:29
  110.5 0.7 slice_multiply_fusion
  (34 shorter events, 0.3 us)
Async XLA Ops:
  13.9 1.6 %copy-start = (bf16[32,32,512]{2,1,0:T(8,128)(2,1)S(1)}, bf16[32,32,512]{2,1,0:T(8,128)(2,1)}, u32[]{:S(2)}) copy-start(bf16[32,32,512]{2,1,0:T(8,128)(2,1)} %add.251) | copy-start | bytes 3145732
  13.9 1.9 %copy-start.1 = (bf16[32,32,512]{2,1,0:T(8,128)(2,1)S(1)}, bf16[32,32,512]{2,1,0:T(8,128)(2,1)}, u32[]{:S(2)}) copy-start(bf16[32,32,512]{2,1,0:T(8,128)(2,1)} %sub.177) | copy-start | bytes 3145732
  15.8 1.5 %copy-start.2 = (f32[32,32]{1,0:T(8,128)S(1)}, f32[32,32]{1,0:T(8,128)}, u32[]{:S(2)}) copy-start(f32[32,32]{1,0:T(8,128)} %param.15) | copy-start | bytes 12292
  20.9 2.8 %copy-start.4 = (s32[1,32,1]{1,2,0:T(1,128)S(1)}, s32[1,32,1]{1,2,0:T(1,128)}, u32[]{:S(2)}) copy-start(s32[1,32,1]{1,2,0:T(1,128)} %param.12) | copy-start | bytes 388
  21.0 4.0 %copy-start.3 = (s32[1,32,2]{1,2,0:T(2,128)S(1)}, s32[1,32,2]{1,2,0:T(2,128)}, u32[]{:S(2)}) copy-start(s32[1,32,2]{1,2,0:T(2,128)} %param.13) | copy-start | bytes 772
  21.0 4.0 %copy-start.5 = (s32[1,32]{1,0:T(1,128)S(1)}, s32[1,32]{1,0:T(1,128)}, u32[]{:S(2)}) copy-start(s32[1,32]{1,0:T(1,128)} %param.14) | copy-start | bytes 388
  26.9 20.3 %all-to-all-start = ((bf16[32,2,2052]{2,1,0:T(2,128)(2,1)}), bf16[32,2,2052]{2,1,0:T(2,128)(2,1)S(1)}, u32[]{:S(2)}, u32[]{:S(2)}) async-start(bf16[32,2,2052]{2,1,0:T(2,128)(2,1)} %pad_maximum_fusion.2), calls=%async_computation | async-start | bytes 557056 | tf_op jit(solution)/shard_map/all_to_all | solution.py:16

commit v3 on v2

--- a/solution.py
+++ b/solution.py
@@ -75,7 +75,6 @@
     b_re, b_im = phase_table(step * coord_b[:, 1, :], (vis_re, vis_im))
     a_t = jnp.concatenate([a_re, a_im], axis=1).astype(bf)
     b_t = jnp.concatenate([b_re, b_im], axis=1).astype(bf)
-    a_t, b_t = lax.optimization_barrier((a_t, b_t))
     f32 = jnp.float32
     s_all = jnp.einsum("bik,bjk->bij", a_t, b_t, preferred_element_type=f32)
     s_re = s_all[:, :32, :32] - s_all[:, 32:, 32:]
@@ -105,23 +104,19 @@
     return jnp.where(powers[None, :] == 0.0, 1.0, xval[:, None] ** powers[None, :])
 
 
-def place_block(tile_acc, inputs):
-    patch_b, weight_b, rows_b, cols_b = inputs
-    hp = lax.Precision.HIGHEST
+def place_all(patch, weight, rows, cols):
+    bf, f32 = jnp.bfloat16, jnp.float32
     cells = jnp.arange(TILE, dtype=jnp.int32)
     small = jnp.arange(32, dtype=jnp.int32)
-    row_hot = (cells[None, :, None] == rows_b[:, None, None] + small[None, None, :]).astype(
-        jnp.float32
-    )
-    col_hot = (cells[None, :, None] == cols_b[:, None, None] + small[None, None, :]).astype(
-        jnp.float32
-    )
-    spread = jnp.einsum("scab,sQb->scaQ", patch_b.astype(jnp.float32), col_hot, precision=hp)
-    terms = []
-    for term in range(NT):
-        weighted = spread * weight_b[:, term][:, None, None, None]
-        terms.append(jnp.einsum("sRa,scaQ->cRQ", row_hot, weighted, precision=hp))
-    return (tile_acc + jnp.stack(terms, 0), None)
+    col_hot = (small[None, :, None] + cols[:, None, None] == cells[None, None, :]).astype(bf)
+    spread = jnp.einsum("scab,sbq->scaq", patch, col_hot, preferred_element_type=f32).astype(bf)
+    row_hot = (cells[None, :, None] == rows[:, None, None] + small[None, None, :]).astype(f32)
+    w_hi = weight.astype(bf)
+    w_lo = (weight - w_hi.astype(f32)).astype(bf)
+    w_both = jnp.stack([w_hi, w_lo], 0).astype(f32)
+    lhs = (w_both.transpose(0, 2, 1)[:, :, None, :, None] * row_hot.transpose(1, 0, 2)[None, None]).astype(bf)
+    out = jnp.einsum("htrsa,scaq->htcrq", lhs, spread, preferred_element_type=f32)
+    return out[0] + out[1]
 
 
 def body(visibilities, coords, vis_counts, cover_tile, offsets, channel, taper):
@@ -162,15 +157,9 @@
     got_meta = got_meta.reshape(slots, 4).astype(jnp.int32)
     valid = got_meta[:, 0].astype(jnp.float32)
     weight = taylor_weights(got_meta[:, 3], freq_pos, channels) * valid[:, None]
-    blocks = slots // 32
-    inputs = (
-        got_payload.reshape(blocks, 32, 2, 32, 32),
-        weight.reshape(blocks, 32, NT),
-        got_meta[:, 1].reshape(blocks, 32),
-        got_meta[:, 2].reshape(blocks, 32),
+    local = place_all(
+        got_payload.reshape(slots, 2, 32, 32), weight, got_meta[:, 1], got_meta[:, 2]
     )
-    start_tile = jnp.zeros((NT, 2, TILE, TILE), jnp.float32)
-    local, _ = lax.scan(place_block, start_tile, inputs)
     local = local.reshape(NT, 1, 2, TILE, TILE)
     total = gathered_total(local, "freq")
     scale = TILE / (32.0 * math.sqrt(n_freq * sub_count))

time: 112 us -> 104 us (0.929)
  other arithmetic: 14.4 us -> 9.6 us
  matrix products: 10.4 us -> 6.22 us
    dot_general x6 -> x2, matrix products: 5.45 us -> 1.37 us  [the longest x1 0.87 us: place_all(): jnp.einsum('htrsa,scaq->htcrq', lhs, spread, preferred_element_type=f32)]
    concatenate x2 -> x0, other arithmetic: 3.01 us -> none  [the longest x1 1.55 us: make_subgrids(): b_t = jnp.concatenate([b_re, b_im], axis=1).astype(bf)]
    unnamed x16 -> x18, local copies, waits for them, and re-layouts: 2.24 us -> 2.64 us
where the time goes in v3:
time: 104 us; the launch traced here: 103 us
  blocking collectives  55.5 us (53%)
  local copies, waits for them, and re-layouts  11.2 us (11%)
  starting transfers between devices  10.7 us (10%)
  other arithmetic  9.6 us (9%)
  waiting for transfers between devices  9.57 us (9%)
  matrix products  6.22 us (6%)
    all_to_all x1, blocking collectives, gathered_total(): lax.all_to_all(flat.reshape(n, per // 128, 128), axis, 0, 0, tiled=True)  34.7 us
    all_to_all x1, blocking collectives, gathered_total(): whole = lax.all_to_all(spread, axis, 0, 0, tiled=True)  20.8 us
    all_to_all x1, starting transfers between devices, sent_together(): lax.all_to_all(both, axis, split_axis=split_dim, concat_axis=concat_dim,...  10.7 us
    all_to_all x1, waiting for transfers between devices, sent_together(): lax.all_to_all(both, axis, split_axis=split_dim, concat_axis=concat_dim,...  9.57 us
    another operation x3, other arithmetic  3.24 us
    unnamed x18, local copies, waits for them, and re-layouts  2.64 us
    sub x2, local copies, waits for them, and re-layouts, cmul(): return (ar * br - ai * bi, ar * bi + ai * br)  2.27 us
    add x2, local copies, waits for them, and re-layouts, cmul(): return (ar * br - ai * bi, ar * bi + ai * br)  2.24 us
  transfers between devices with their start and end apart: 1, of which 1 were waited for; matrix products, arithmetic and copies ran while one was open for 0% of the time, Pallas kernels for 0%

profile of v3, /device:TPU:1, one launch (start us, length us, event | category | flops | bytes accessed | tf_op | source)
XLA Modules:
  0.0 103.1 jit_solution(14189574409942570978)
XLA Ops:
  0.0 0.0 copy-start.3
  0.1 0.9 copy.83
  1.0 0.9 copy.84
  1.8 0.6 fusion.97
  2.4 0.0 copy-done.3
  2.4 0.3 fusion.57
  2.8 0.6 fusion.58
  3.3 1.1 %select_select_fusion.4 = (f32[32,4,512]{2,1,0:T(4,128)S(1)}, f32[32,4,512]{2,1,0:T(4,128)S(1)}, f32[32,4,512]{2,1,0:T(4,128)S(1)}, f32[32,4,512]{2,1,0:T(4,128)}) fusion(f32[32,512]{1,0:T(8,128)S(1)} %get-tuple-element.70, f32[32,512]{1,0:T(8,128)S(1)} %get-tuple-element.77, f32[32,512]{1,0:T(8,128)S(1)} %get-tuple-element.71, ...), kind=kLoop, calls=%fused_computation.75 | loop fusion | flops 1310720 | bytes 1572872 | tf_op jit(solution)/shard_map/while/body/eval_jaxpr/jit(_where)/select_n | solution.py:44
  4.4 0.7 fusion.42
  5.1 1.2 %subtract_convert_fusion = (bf16[32,8,4,512]{3,2,1,0:T(4,128)(2,1)S(1)}, bf16[32,8,4,512]{3,2,1,0:T(4,128)(2,1)S(1)}) fusion(f32[32,4,512]{2,1,0:T(4,128)S(1)} %get-tuple-element.38, f32[32,8,512]{2,1,0:T(8,128)S(1)} %get-tuple-element.37, f32[32,4,512]{2,1,0:T(4,128)S(1)} %get-tuple-element.36, f32[32,8,512]{2,1,0:T(8,128)S(1)} %get-tuple-element.35), kind=kLoop, calls=%fused_computation.15 | loop fusion | flops 4194304 | bytes 3670016 | tf_op jit(solution)/shard_map/convert.14
  6.3 1.1 %add.262 = bf16[32,32,512]{2,1,0:T(8,128)(2,1)} reshape(bf16[32,8,4,512]{3,2,1,0:T(4,128)(2,1)S(1)} %get-tuple-element.45) | data formatting | bytes 2097152 | tf_op jit(solution)/shard_map/while/body/eval_jaxpr/add | solution.py:34
  7.5 1.1 %sub.199 = bf16[32,32,512]{2,1,0:T(8,128)(2,1)} reshape(bf16[32,8,4,512]{3,2,1,0:T(4,128)(2,1)S(1)} %get-tuple-element.44) | data formatting | bytes 2097152 | tf_op jit(solution)/shard_map/while/body/eval_jaxpr/sub | solution.py:34
  8.6 2.1 %subtract_convert_fusion.1 = (bf16[32,8,4,512]{3,2,1,0:T(4,128)(2,1)S(1)}, bf16[32,8,4,512]{3,2,1,0:T(4,128)(2,1)S(1)}) fusion(f32[32,4,512]{2,1,0:T(4,128)} %get-tuple-element.34, f32[32,8,512]{2,1,0:T(8,128)S(1)} %get-tuple-element.33, f32[32,4,512]{2,1,0:T(4,128)S(1)} %get-tuple-element.32, f32[32,8,512]{2,1,0:T(8,128)S(1)} %get-tuple-element.31), kind=kLoop, calls=%fused_computation.17 | loop fusion | flops 4194304 | bytes 3670016 | tf_op jit(solution)/shard_map/convert.18
  10.6 0.0 copy-start.2
  10.6 1.1 %add.250 = bf16[32,32,512]{2,1,0:T(8,128)(2,1)} reshape(bf16[32,8,4,512]{3,2,1,0:T(4,128)(2,1)S(1)} %get-tuple-element.47) | data formatting | bytes 2097152 | tf_op jit(solution)/shard_map/while/body/eval_jaxpr/add | solution.py:34
  11.8 0.0 copy-start
  11.8 0.0 copy-start.1
  11.8 1.2 %sub.187 = bf16[32,32,512]{2,1,0:T(8,128)(2,1)} reshape(bf16[32,8,4,512]{3,2,1,0:T(4,128)(2,1)S(1)} %get-tuple-element.46) | data formatting | bytes 2097152 | tf_op jit(solution)/shard_map/while/body/eval_jaxpr/sub | solution.py:34
  12.9 0.0 copy-done.2
  12.9 0.1 copy.60
  13.0 0.4 copy-done
  13.4 0.3 copy-done.1
  13.7 2.2 %fusion.3 = f32[32,64,64]{1,2,0:T(8,128)S(1)} fusion(bf16[32,32,512]{2,1,0:T(8,128)(2,1)} %add.250, bf16[32,32,512]{2,1,0:T(8,128)(2,1)} %sub.187, bf16[32,32,512]{2,1,0:T(8,128)(2,1)S(1)} %copy-done, bf16[32,32,512]{2,1,0:T(8,128)(2,1)S(1)} %copy-done.1), kind=kOutput, calls=%fused_computation.5 | convolution fusion | flops 142606336 | bytes 4718592 | tf_op jit(solution)/shard_map/while/body/eval_jaxpr/bik,bjk->bij/dot_general | solution.py:79
  15.9 0.3 fusion.46
  16.3 0.1 fusion.86
  16.4 0.6 convolution_bitcast_fusion
  17.1 0.2 fusion.100
  17.3 1.8 %fusion.16 = bf16[32,32,64]{2,1,0:T(8,128)(2,1)S(1)} fusion(f32[32,32,32]{1,2,0:T(8,128)S(1)} %get-tuple-element.53, f32[32,32,32]{1,2,0:T(8,128)S(1)} %get-tuple-element.52, f32[32,32]{1,0:T(8,128)S(1)} %get-tuple-element.88, f32[32,32]{1,0:T(8,128)S(1)} %get-tuple-element.86, f32[32,32]{1,0:T(8,128)S(1)} %get-tuple-element.87), kind=kOutput, calls=%fused_computation.23 | convolution fusion | flops 50540544 | bytes 405504 | tf_op jit(solution)/shard_map/while/body/eval_jaxpr/baj,jk->bak/dot_general | solution.py:95
  19.1 0.2 convert_element_type.115
  19.4 0.0 copy-start.5
  19.4 0.0 copy-start.4
  19.4 0.0 copy-start.6
  19.4 0.1 copy.82
  19.5 0.5 reshape.485
  20.1 0.0 copy-done.5
  20.1 0.1 fusion.17
  20.2 0.9 scatter_custom_fusion
  21.1 0.2 reshape.475
  21.3 0.0 copy-done.4
  21.3 0.0 copy-done.6
  21.4 0.1 pad_maximum_fusion.7
  21.5 0.1 copy.65
  21.6 0.7 scatter_custom_fusion.1
  22.2 1.0 pad_maximum_fusion
  23.2 10.7 %all-to-all-start = ((bf16[32,2,2052]{2,1,0:T(2,128)(2,1)}), bf16[32,2,2052]{2,1,0:T(2,128)(2,1)S(1)}, u32[]{:S(2)}, u32[]{:S(2)}) async-start(bf16[32,2,2052]{2,1,0:T(2,128)(2,1)} %pad_maximum_fusion), calls=%async_computation | async-start | bytes 557056 | tf_op jit(solution)/shard_map/all_to_all | solution.py:16
  33.9 9.6 %all-to-all-done = bf16[32,2,2052]{2,1,0:T(2,128)(2,1)S(1)} async-done(((bf16[32,2,2052]{2,1,0:T(2,128)(2,1)}), bf16[32,2,2052]{2,1,0:T(2,128)(2,1)S(1)}, u32[]{:S(2)}, u32[]{:S(2)}) %all-to-all-start) | async-done | bytes 262688 | tf_op jit(solution)/shard_map/all_to_all | solution.py:16
  43.5 0.2 split.8
  43.6 0.5 reshape.477
  44.2 0.2 slice_reduce_fusion.1
  44.4 0.1 iota_add_fusion.1
  44.4 0.1 add_multiply_fusion.8
  44.6 0.1 copy.76
  44.6 0.1 iota_add_fusion
  44.7 0.4 fusion.24
  45.1 0.5 fusion.12
  45.6 0.1 fusion.93
  45.7 0.9 fusion.13
  46.6 0.1 copy.68
  46.8 34.7 %all_to_all.15 = f32[24,22,128]{2,1,0:T(8,128)S(1)} all-to-all(f32[24,22,128]{2,1,0:T(8,128)S(1)} %reshape.478), channel_id=1, replica_groups=mesh['span'=32,'freq'=24] {'freq'}, dimensions={0} | all-to-all | bytes 540672 | tf_op jit(solution)/shard_map/all_to_all | solution.py:26
  81.6 20.8 %all_to_all.16 = f32[24,22,128]{2,1,0:T(8,128)S(1)} all-to-all(f32[24,22,128]{2,1,0:T(8,128)S(1)} %broadcast_in_dim.337), channel_id=1, replica_groups=mesh['span'=32,'freq'=24] {'freq'}, dimensions={0} | all-to-all | bytes 540672 | tf_op jit(solution)/shard_map/all_to_all | solution.py:29
  102.3 0.7 slice_multiply_fusion
  (19 shorter events, 0.3 us)
Async XLA Ops:
  0.0 2.4 %copy-start.3 = (s32[1,32]{1,0:T(1,128)S(1)}, s32[1,32]{1,0:T(1,128)}, u32[]{:S(2)}) copy-start(s32[1,32]{1,0:T(1,128)} %param.9) | copy-start | bytes 388
  10.6 2.3 %copy-start.2 = (f32[32,32]{1,0:T(8,128)S(1)}, f32[32,32]{1,0:T(8,128)}, u32[]{:S(2)}) copy-start(f32[32,32]{1,0:T(8,128)} %param.13) | copy-start | bytes 12292
  11.8 1.6 %copy-start = (bf16[32,32,512]{2,1,0:T(8,128)(2,1)S(1)}, bf16[32,32,512]{2,1,0:T(8,128)(2,1)}, u32[]{:S(2)}) copy-start(bf16[32,32,512]{2,1,0:T(8,128)(2,1)} %add.262) | copy-start | bytes 3145732
  11.8 1.9 %copy-start.1 = (bf16[32,32,512]{2,1,0:T(8,128)(2,1)S(1)}, bf16[32,32,512]{2,1,0:T(8,128)(2,1)}, u32[]{:S(2)}) copy-start(bf16[32,32,512]{2,1,0:T(8,128)(2,1)} %sub.199) | copy-start | bytes 3145732
  19.4 0.7 copy-start.5
  19.4 1.9 %copy-start.4 = (s32[1,32,2]{1,2,0:T(2,128)S(1)}, s32[1,32,2]{1,2,0:T(2,128)}, u32[]{:S(2)}) copy-start(s32[1,32,2]{1,2,0:T(2,128)} %param.11) | copy-start | bytes 772
  19.4 2.0 %copy-start.6 = (s32[1,32]{1,0:T(1,128)S(1)}, s32[1,32]{1,0:T(1,128)}, u32[]{:S(2)}) copy-start(s32[1,32]{1,0:T(1,128)} %param.12) | copy-start | bytes 388
  23.2 20.3 %all-to-all-start = ((bf16[32,2,2052]{2,1,0:T(2,128)(2,1)}), bf16[32,2,2052]{2,1,0:T(2,128)(2,1)S(1)}, u32[]{:S(2)}, u32[]{:S(2)}) async-start(bf16[32,2,2052]{2,1,0:T(2,128)(2,1)} %pad_maximum_fusion), calls=%async_computation | async-start | bytes 557056 | tf_op jit(solution)/shard_map/all_to_all | solution.py:16

commit v4 on v3

--- a/solution.py
+++ b/solution.py
@@ -58,9 +58,12 @@
     small = bit_powers(c, s, [(c, s), w2], one, 4)
     big = bit_powers(c, s, [w4, w8, w16], lo, 8)
     small, big = lax.optimization_barrier((small, big))
-    re, im = cmul(big[0][:, :, None, :], big[1][:, :, None, :], small[0][:, None], small[1][:, None])
+    qr, qi = big[0][:, None, :, None, :], big[1][:, None, :, None, :]
+    pr, pi = small[0][:, None, None], small[1][:, None, None]
+    part = lax.broadcasted_iota(jnp.int32, (1, 2, 1, 1, 1), 1)
+    table = jnp.where(part == 0, qr * pr - qi * pi, qr * pi + qi * pr)
     n = c.shape[0]
-    return re.reshape(n, 32, -1), im.reshape(n, 32, -1)
+    return table.reshape(n, 64, -1)
 
 
 def make_subgrids(vis_b, coord_b, count_b, taper):
@@ -71,10 +74,8 @@
     vis_im = vis_b[:, 1, :].astype(jnp.float32) * live * scale_k
     step = -2.0 * math.pi / 32.0
     bf = jnp.bfloat16
-    a_re, a_im = phase_table(step * coord_b[:, 0, :])
-    b_re, b_im = phase_table(step * coord_b[:, 1, :], (vis_re, vis_im))
-    a_t = jnp.concatenate([a_re, a_im], axis=1).astype(bf)
-    b_t = jnp.concatenate([b_re, b_im], axis=1).astype(bf)
+    a_t = phase_table(step * coord_b[:, 0, :]).astype(bf)
+    b_t = phase_table(step * coord_b[:, 1, :], (vis_re, vis_im)).astype(bf)
     f32 = jnp.float32
     s_all = jnp.einsum("bik,bjk->bij", a_t, b_t, preferred_element_type=f32)
     s_re = s_all[:, :32, :32] - s_all[:, 32:, 32:]

time: 104 us -> 116 us (1.12)
  local copies, waits for them, and re-layouts: 11.2 us -> 19.2 us
  matrix products: 6.22 us -> 8.41 us
  other arithmetic: 9.6 us -> 11.5 us
    broadcast_in_dim x0 -> x10, local copies, waits for them, and re-layouts: none -> 13 us  [phase_table(): table = jnp.where(part == 0, qr * pr - qi * pi, qr * pi + qi * pr)]
    add x0 -> x2, other arithmetic: none -> 3.44 us  [phase_table(): table = jnp.where(part == 0, qr * pr - qi * pi, qr * pi + qi * pr)]
    another operation x3 -> x1, other arithmetic: 3.24 us -> 0.01 us
    sub x2 -> x0, local copies, waits for them, and re-layouts: 2.27 us -> none  [cmul(): return (ar * br - ai * bi, ar * bi + ai * br)]
    add x2 -> x0, local copies, waits for them, and re-layouts: 2.24 us -> none  [cmul(): return (ar * br - ai * bi, ar * bi + ai * br)]
    dot_general x1, matrix products: 2.23 us -> 4.42 us  [make_subgrids(): s_all = jnp.einsum('bik,bjk->bij', a_t, b_t, preferred_element_type=f32)]
    unnamed x18 -> x12, local copies, waits for them, and re-layouts: 2.64 us -> 1.95 us
where the time goes in v4:
time: 116 us; the launch traced here: 115 us
  blocking collectives  55.5 us (48%)
  local copies, waits for them, and re-layouts  19.2 us (17%)
  other arithmetic  11.5 us (10%)
  starting transfers between devices  10.5 us (9%)
  waiting for transfers between devices  9.74 us (8%)
  matrix products  8.41 us (7%)
    all_to_all x1, blocking collectives, gathered_total(): lax.all_to_all(flat.reshape(n, per // 128, 128), axis, 0, 0, tiled=True)  34.7 us
    all_to_all x1, blocking collectives, gathered_total(): whole = lax.all_to_all(spread, axis, 0, 0, tiled=True)  20.8 us
    broadcast_in_dim x10, local copies, waits for them, and re-layouts, phase_table(): table = jnp.where(part == 0, qr * pr - qi * pi, qr * pi + qi * pr)  13 us
    all_to_all x1, starting transfers between devices, sent_together(): lax.all_to_all(both, axis, split_axis=split_dim, concat_axis=concat_dim,...  10.5 us
    all_to_all x1, waiting for transfers between devices, sent_together(): lax.all_to_all(both, axis, split_axis=split_dim, concat_axis=concat_dim,...  9.74 us
    dot_general x1, matrix products, make_subgrids(): s_all = jnp.einsum('bik,bjk->bij', a_t, b_t, preferred_element_type=f32)  4.42 us
    add x2, other arithmetic, phase_table(): table = jnp.where(part == 0, qr * pr - qi * pi, qr * pi + qi * pr)  3.44 us
    select_n x2, other arithmetic, bit_powers(): re, im = (jnp.where(on, mr, re), jnp.where(on, mi, im))  2.79 us
  transfers between devices with their start and end apart: 1, of which 1 were waited for; matrix products, arithmetic and copies ran while one was open for 0% of the time, Pallas kernels for 0%

profile of v4, /device:TPU:1, one launch (start us, length us, event | category | flops | bytes accessed | tf_op | source)
XLA Modules:
  0.0 115.2 jit_solution(17744131859344087954)
XLA Ops:
  0.1 0.9 copy.83
  1.0 0.9 copy.84
  1.9 0.6 fusion.91
  2.4 1.0 fusion.52
  3.4 0.6 fusion.53
  4.0 1.1 select_select_fusion.4
  5.1 1.7 %fusion.37 = (f32[32,8,512]{2,1,0:T(8,128)S(1)}, f32[32,8,512]{2,1,0:T(8,128)S(1)}, f32[32,8,512]{2,1,0:T(8,128)}, f32[32,8,512]{2,1,0:T(8,128)}) fusion(f32[32,512]{1,0:T(8,128)S(1)} %get-tuple-element.62, f32[32,512]{1,0:T(8,128)S(1)} %get-tuple-element.66, f32[32,512]{1,0:T(8,128)S(1)} %get-tuple-element.61, f32[32,512]{1,0:T(8,128)S(1)} %get-tuple-element.43, ...), kind=kLoop, calls=%fused_computation.60 | loop fusion | flops 4718592 | bytes 3080216 | tf_op jit(solution)/shard_map/while/body/eval_jaxpr/jit(_where)/select_n | solution.py:44
  6.8 1.2 %multiply_add_fusion = (bf16[32,8,4,512]{3,2,1,0:T(4,128)(2,1)S(1)}, bf16[32,8,4,512]{3,2,1,0:T(4,128)(2,1)S(1)}) fusion(f32[32,4,512]{2,1,0:T(4,128)S(1)} %get-tuple-element.38, f32[32,8,512]{2,1,0:T(8,128)S(1)} %get-tuple-element.37, f32[32,4,512]{2,1,0:T(4,128)S(1)} %get-tuple-element.36, f32[32,8,512]{2,1,0:T(8,128)S(1)} %get-tuple-element.35), kind=kLoop, calls=%fused_computation.10 | loop fusion | flops 4194304 | bytes 3670016 | tf_op jit(solution)/shard_map/while/body/eval_jaxpr/add | solution.py:64
  8.0 1.0 broadcast_in_dim.411
  9.0 2.1 %broadcast_in_dim.412 = bf16[32,64,512]{2,1,0:T(8,128)(2,1)} reshape(bf16[32,2,8,4,512]{4,3,2,1,0:T(4,128)(2,1)S(1)} %broadcast_in_dim.411) | data formatting | bytes 4194304 | tf_op jit(solution)/shard_map/while/body/eval_jaxpr/jit(_where)/broadcast_in_dim | solution.py:64
  11.1 1.3 %broadcast_in_dim.413 = bf16[32,2,8,4,512]{4,3,2,1,0:T(4,128)(2,1)S(1)} broadcast(bf16[32,8,4,512]{3,2,1,0:T(4,128)(2,1)S(1)} %get-tuple-element.44), dimensions={0,2,3,4} | broadcast | bytes 3145728 | tf_op jit(solution)/shard_map/while/body/eval_jaxpr/jit(_where)/broadcast_in_dim | solution.py:64
  12.3 2.1 %broadcast_in_dim.414 = bf16[32,64,512]{2,1,0:T(8,128)(2,1)} reshape(bf16[32,2,8,4,512]{4,3,2,1,0:T(4,128)(2,1)S(1)} %broadcast_in_dim.413) | data formatting | bytes 4194304 | tf_op jit(solution)/shard_map/while/body/eval_jaxpr/jit(_where)/broadcast_in_dim | solution.py:64
  14.4 2.3 %multiply_add_fusion.1 = (bf16[32,8,4,512]{3,2,1,0:T(4,128)(2,1)S(1)}, bf16[32,8,4,512]{3,2,1,0:T(4,128)(2,1)S(1)}) fusion(f32[32,4,512]{2,1,0:T(4,128)} %get-tuple-element.34, f32[32,8,512]{2,1,0:T(8,128)} %get-tuple-element.33, f32[32,4,512]{2,1,0:T(4,128)S(1)} %get-tuple-element.32, f32[32,8,512]{2,1,0:T(8,128)} %get-tuple-element.31), kind=kLoop, calls=%fused_computation.12 | loop fusion | flops 4194304 | bytes 3670016 | tf_op jit(solution)/shard_map/while/body/eval_jaxpr/add | solution.py:64
  16.7 1.0 broadcast_in_dim.399
  17.7 2.1 %broadcast_in_dim.400 = bf16[32,64,512]{2,1,0:T(8,128)(2,1)} reshape(bf16[32,2,8,4,512]{4,3,2,1,0:T(4,128)(2,1)S(1)} %broadcast_in_dim.399) | data formatting | bytes 4194304 | tf_op jit(solution)/shard_map/while/body/eval_jaxpr/jit(_where)/broadcast_in_dim | solution.py:64
  19.8 1.3 %broadcast_in_dim.401 = bf16[32,2,8,4,512]{4,3,2,1,0:T(4,128)(2,1)S(1)} broadcast(bf16[32,8,4,512]{3,2,1,0:T(4,128)(2,1)S(1)} %get-tuple-element.46), dimensions={0,2,3,4} | broadcast | bytes 3145728 | tf_op jit(solution)/shard_map/while/body/eval_jaxpr/jit(_where)/broadcast_in_dim | solution.py:64
  21.0 0.0 copy-start
  21.1 2.1 %broadcast_in_dim.402 = bf16[32,64,512]{2,1,0:T(8,128)(2,1)} reshape(bf16[32,2,8,4,512]{4,3,2,1,0:T(4,128)(2,1)S(1)} %broadcast_in_dim.401) | data formatting | bytes 4194304 | tf_op jit(solution)/shard_map/while/body/eval_jaxpr/jit(_where)/broadcast_in_dim | solution.py:64
  23.1 0.1 broadcast_in_dim.383
  23.2 0.1 broadcast_in_dim.384
  23.3 0.0 copy-done
  23.3 0.1 copy.60
  23.4 4.4 %fusion = f32[32,64,64]{1,2,0:T(8,128)S(1)} fusion(bf16[32,64,512]{2,1,0:T(8,128)(2,1)} %broadcast_in_dim.400, bf16[32,64,512]{2,1,0:T(8,128)(2,1)} %broadcast_in_dim.402, bf16[32,64,512]{2,1,0:T(8,128)(2,1)} %broadcast_in_dim.412, bf16[32,64,512]{2,1,0:T(8,128)(2,1)} %broadcast_in_dim.414, pred[64]{0:T(512)(128)(4,1)S(1)} %broadcast_in_dim.384), kind=kOutput, calls=%fused_computation.5 | convolution fusion | flops 136314880 | bytes 8912960 | tf_op jit(solution)/shard_map/while/body/eval_jaxpr/bik,bjk->bij/dot_general | solution.py:80
  27.8 0.3 fusion.41
  28.2 0.1 fusion.81
  28.3 0.6 convolution_bitcast_fusion
  29.0 0.2 fusion.94
  29.2 0.0 copy-start.2
  29.2 0.0 copy-start.1
  29.2 0.0 copy-start.3
  29.2 1.8 %fusion.11 = bf16[32,32,64]{2,1,0:T(8,128)(2,1)S(1)} fusion(f32[32,32,32]{1,2,0:T(8,128)S(1)} %get-tuple-element.53, f32[32,32,32]{1,2,0:T(8,128)S(1)} %get-tuple-element.52, f32[32,32]{1,0:T(8,128)S(1)} %get-tuple-element.88, f32[32,32]{1,0:T(8,128)S(1)} %get-tuple-element.86, f32[32,32]{1,0:T(8,128)S(1)} %get-tuple-element.87), kind=kOutput, calls=%fused_computation.20 | convolution fusion | flops 50540544 | bytes 405504 | tf_op jit(solution)/shard_map/while/body/eval_jaxpr/baj,jk->bak/dot_general | solution.py:96
  31.1 0.2 convert_element_type.121
  31.3 0.1 copy.82
  31.4 0.5 reshape.500
  32.0 0.0 copy-done.2
  32.0 0.1 fusion.12
  32.1 1.1 scatter_custom_fusion
  33.2 0.2 reshape.490
  33.4 0.0 copy-done.1
  33.4 0.0 copy-done.3
  33.5 0.1 pad_maximum_fusion.7
  33.5 0.1 copy.65
  33.6 0.7 scatter_custom_fusion.1
  34.3 1.0 pad_maximum_fusion
  35.3 10.5 %all-to-all-start = ((bf16[32,2,2052]{2,1,0:T(2,128)(2,1)}), bf16[32,2,2052]{2,1,0:T(2,128)(2,1)S(1)}, u32[]{:S(2)}, u32[]{:S(2)}) async-start(bf16[32,2,2052]{2,1,0:T(2,128)(2,1)} %pad_maximum_fusion), calls=%async_computation | async-start | bytes 557056 | tf_op jit(solution)/shard_map/all_to_all | solution.py:16
  45.8 9.7 %all-to-all-done = bf16[32,2,2052]{2,1,0:T(2,128)(2,1)S(1)} async-done(((bf16[32,2,2052]{2,1,0:T(2,128)(2,1)}), bf16[32,2,2052]{2,1,0:T(2,128)(2,1)S(1)}, u32[]{:S(2)}, u32[]{:S(2)}) %all-to-all-start) | async-done | bytes 262688 | tf_op jit(solution)/shard_map/all_to_all | solution.py:16
  55.6 0.2 split.8
  55.7 0.5 reshape.492
  56.3 0.2 slice_reduce_fusion.1
  56.5 0.1 iota_add_fusion.1
  56.5 0.1 add_multiply_fusion.8
  56.7 0.1 copy.76
  56.7 0.1 iota_add_fusion
  56.8 0.4 fusion.19
  57.2 0.5 fusion.7
  57.7 0.1 fusion.87
  57.8 0.9 fusion.8
  58.7 0.1 copy.68
  58.9 34.7 %all_to_all.15 = f32[24,22,128]{2,1,0:T(8,128)S(1)} all-to-all(f32[24,22,128]{2,1,0:T(8,128)S(1)} %reshape.493), channel_id=1, replica_groups=mesh['span'=32,'freq'=24] {'freq'}, dimensions={0} | all-to-all | bytes 540672 | tf_op jit(solution)/shard_map/all_to_all | solution.py:26
  93.7 20.8 %all_to_all.16 = f32[24,22,128]{2,1,0:T(8,128)S(1)} all-to-all(f32[24,22,128]{2,1,0:T(8,128)S(1)} %broadcast_in_dim.418), channel_id=1, replica_groups=mesh['span'=32,'freq'=24] {'freq'}, dimensions={0} | all-to-all | bytes 540672 | tf_op jit(solution)/shard_map/all_to_all | solution.py:29
  114.4 0.7 slice_multiply_fusion
  (20 shorter events, 0.3 us)
Async XLA Ops:
  21.0 2.3 %copy-start = (f32[32,32]{1,0:T(8,128)S(1)}, f32[32,32]{1,0:T(8,128)}, u32[]{:S(2)}) copy-start(f32[32,32]{1,0:T(8,128)} %param.13) | copy-start | bytes 12292
  29.2 2.8 %copy-start.2 = (s32[1,32,1]{1,2,0:T(1,128)S(1)}, s32[1,32,1]{1,2,0:T(1,128)}, u32[]{:S(2)}) copy-start(s32[1,32,1]{1,2,0:T(1,128)} %param.10) | copy-start | bytes 388
  29.2 4.2 %copy-start.1 = (s32[1,32,2]{1,2,0:T(2,128)S(1)}, s32[1,32,2]{1,2,0:T(2,128)}, u32[]{:S(2)}) copy-start(s32[1,32,2]{1,2,0:T(2,128)} %param.11) | copy-start | bytes 772
  29.2 4.2 %copy-start.3 = (s32[1,32]{1,0:T(1,128)S(1)}, s32[1,32]{1,0:T(1,128)}, u32[]{:S(2)}) copy-start(s32[1,32]{1,0:T(1,128)} %param.12) | copy-start | bytes 388
  35.3 20.3 %all-to-all-start = ((bf16[32,2,2052]{2,1,0:T(2,128)(2,1)}), bf16[32,2,2052]{2,1,0:T(2,128)(2,1)S(1)}, u32[]{:S(2)}, u32[]{:S(2)}) async-start(bf16[32,2,2052]{2,1,0:T(2,128)(2,1)} %pad_maximum_fusion), calls=%async_computation | async-start | bytes 557056 | tf_op jit(solution)/shard_map/all_to_all | solution.py:16

commit v5 on v3

--- a/solution.py
+++ b/solution.py
@@ -3,6 +3,7 @@
 import jax
 import jax.numpy as jnp
 from jax import lax
+from jax.experimental import pallas as pl
 from jax.sharding import PartitionSpec as P
 
 TILE = 128
@@ -57,10 +58,49 @@
     one = (jnp.ones_like(c), jnp.zeros_like(c))
     small = bit_powers(c, s, [(c, s), w2], one, 4)
     big = bit_powers(c, s, [w4, w8, w16], lo, 8)
-    small, big = lax.optimization_barrier((small, big))
-    re, im = cmul(big[0][:, :, None, :], big[1][:, :, None, :], small[0][:, None], small[1][:, None])
-    n = c.shape[0]
-    return re.reshape(n, 32, -1), im.reshape(n, 32, -1)
+    return small, big
+
+
+def phase_rows(pr, pi, qr, qi, b):
+    p_r = jnp.concatenate([pr[b], pr[b]], axis=0)
+    p_i = jnp.concatenate([pi[b], pi[b]], axis=0)
+    first = lax.broadcasted_iota(jnp.int32, p_r.shape, 0) < 4
+    res, ims = [], []
+    for m in range(4):
+        q_r = jnp.where(first, qr[b, 2 * m : 2 * m + 1, :], qr[b, 2 * m + 1 : 2 * m + 2, :])
+        q_i = jnp.where(first, qi[b, 2 * m : 2 * m + 1, :], qi[b, 2 * m + 1 : 2 * m + 2, :])
+        r, i = cmul(q_r, q_i, p_r, p_i)
+        res.append(r)
+        ims.append(i)
+    return jnp.concatenate(res + ims, axis=0).astype(jnp.bfloat16)
+
+
+def s_kernel(upr, upi, uqr, uqi, vpr, vpi, vqr, vqi, out):
+    for b in range(out.shape[0]):
+        a = phase_rows(upr, upi, uqr, uqi, b)
+        bb = phase_rows(vpr, vpi, vqr, vqi, b)
+        out[b] = lax.dot_general(
+            a, bb, (((1,), (1,)), ((), ())), preferred_element_type=jnp.float32
+        )
+
+
+def s_matrices(small_u, big_u, small_v, big_v):
+    n, _, kk = small_u[0].shape
+    per = 8
+    spec_p = pl.BlockSpec((per, 4, kk), lambda g: (g, 0, 0))
+    spec_q = pl.BlockSpec((per, 8, kk), lambda g: (g, 0, 0))
+    return pl.pallas_call(
+        s_kernel,
+        grid=(n // per,),
+        in_specs=[spec_p, spec_p, spec_q, spec_q] * 2,
+        out_specs=pl.BlockSpec((per, 64, 64), lambda g: (g, 0, 0)),
+        out_shape=jax.ShapeDtypeStruct((n, 64, 64), jnp.float32),
+        cost_estimate=pl.CostEstimate(
+            flops=2 * n * 64 * 64 * kk + 24 * n * 64 * kk,
+            transcendentals=0,
+            bytes_accessed=4 * n * 24 * kk * 2 + 4 * n * 64 * 64,
+        ),
+    )(*small_u, *big_u, *small_v, *big_v)
 
 
 def make_subgrids(vis_b, coord_b, count_b, taper):
@@ -71,12 +111,9 @@
     vis_im = vis_b[:, 1, :].astype(jnp.float32) * live * scale_k
     step = -2.0 * math.pi / 32.0
     bf = jnp.bfloat16
-    a_re, a_im = phase_table(step * coord_b[:, 0, :])
-    b_re, b_im = phase_table(step * coord_b[:, 1, :], (vis_re, vis_im))
-    a_t = jnp.concatenate([a_re, a_im], axis=1).astype(bf)
-    b_t = jnp.concatenate([b_re, b_im], axis=1).astype(bf)
-    f32 = jnp.float32
-    s_all = jnp.einsum("bik,bjk->bij", a_t, b_t, preferred_element_type=f32)
+    small_u, big_u = phase_table(step * coord_b[:, 0, :])
+    small_v, big_v = phase_table(step * coord_b[:, 1, :], (vis_re, vis_im))
+    s_all = s_matrices(small_u, big_u, small_v, big_v)
     s_re = s_all[:, :32, :32] - s_all[:, 32:, 32:]
     s_im = s_all[:, :32, 32:] + s_all[:, 32:, :32]
     x2 = jnp.concatenate([taper * s_re, taper * s_im], axis=1)

time: 104 us -> 102 us (0.981)
  local copies, waits for them, and re-layouts: 11.2 us -> 5.92 us
  Pallas kernels: 0 us -> 4.73 us
  matrix products: 6.22 us -> 5.17 us
    pallas_call x0 -> x1, Pallas kernels: none -> 4.73 us  [s_matrices(): pl.pallas_call(s_kernel, grid=(n // per,), in_specs=[spec_p, spec_p, spec...]
    another operation x3 -> x1, other arithmetic: 3.24 us -> 0.01 us
    sub x2 -> x0, local copies, waits for them, and re-layouts: 2.27 us -> none  [cmul(): return (ar * br - ai * bi, ar * bi + ai * br)]
    add x2 -> x0, local copies, waits for them, and re-layouts: 2.24 us -> none  [cmul(): return (ar * br - ai * bi, ar * bi + ai * br)]
    dot_general x1 -> x0, matrix products: 2.23 us -> none  [make_subgrids(): s_all = jnp.einsum('bik,bjk->bij', a_t, b_t, preferred_element_type=f32)]
    mul x1, other arithmetic: 0.34 us -> 1.91 us  [make_subgrids(): x2 = jnp.concatenate([taper * s_re, taper * s_im], axis=1)]
    select_n x2, other arithmetic: 1.81 us -> 3.26 us  [bit_powers(): re, im = (jnp.where(on, mr, re), jnp.where(on, mi, im))]
    dot_general x1, matrix products: 0.65 us -> 1.83 us  [make_subgrids(): y2 = jnp.einsum('ij,bjq->biq', left, x2, precision=hp)]
where the time goes in v5:
time: 102 us; the launch traced here: 101 us
  blocking collectives  55.5 us (54%)
  starting transfers between devices  10.7 us (10%)
  waiting for transfers between devices  9.56 us (9%)
  other arithmetic  9.38 us (9%)
  local copies, waits for them, and re-layouts  5.92 us (6%)
  matrix products  5.17 us (5%)
  Pallas kernels  4.73 us (5%)
    all_to_all x1, blocking collectives, gathered_total(): lax.all_to_all(flat.reshape(n, per // 128, 128), axis, 0, 0, tiled=True)  34.7 us
    all_to_all x1, blocking collectives, gathered_total(): whole = lax.all_to_all(spread, axis, 0, 0, tiled=True)  20.8 us
    all_to_all x1, starting transfers between devices, sent_together(): lax.all_to_all(both, axis, split_axis=split_dim, concat_axis=concat_dim,...  10.7 us
    all_to_all x1, waiting for transfers between devices, sent_together(): lax.all_to_all(both, axis, split_axis=split_dim, concat_axis=concat_dim,...  9.56 us
    pallas_call x1, Pallas kernels, s_matrices(): pl.pallas_call(s_kernel, grid=(n // per,), in_specs=[spec_p, spec_p, spec...  4.73 us
    select_n x2, other arithmetic, bit_powers(): re, im = (jnp.where(on, mr, re), jnp.where(on, mi, im))  3.26 us
  transfers between devices with their start and end apart: 1, of which 1 were waited for; matrix products, arithmetic and copies ran while one was open for 0% of the time, Pallas kernels for 0%

profile of v5, /device:TPU:1, one launch (start us, length us, event | category | flops | bytes accessed | tf_op | source)
XLA Modules:
  0.0 101.2 jit_solution(6361617573868886869)
XLA Ops:
  0.0 0.0 copy-start.1
  0.1 0.9 copy.84
  1.0 0.9 copy.85
  1.8 0.6 fusion.89
  2.4 0.0 copy-done.1
  2.4 0.3 fusion.50
  2.8 0.6 fusion.51
  3.3 1.4 %select_select_fusion.4 = (f32[32,4,512]{2,1,0:T(4,128)}, f32[32,4,512]{2,1,0:T(4,128)}, f32[32,4,512]{2,1,0:T(4,128)}, f32[32,4,512]{2,1,0:T(4,128)}) fusion(f32[32,512]{1,0:T(8,128)S(1)} %get-tuple-element.50, f32[32,512]{1,0:T(8,128)S(1)} %get-tuple-element.57, f32[32,512]{1,0:T(8,128)S(1)} %get-tuple-element.51, f32[32,512]{1,0:T(8,128)S(1)} %get-tuple-element.58, ...), kind=kLoop, calls=%fused_computation.64 | loop fusion | flops 1310720 | bytes 1572872 | tf_op jit(solution)/shard_map/while/body/eval_jaxpr/jit(_where)/select_n | solution.py:45
  4.7 1.9 %fusion.38 = (f32[32,8,512]{2,1,0:T(8,128)}, f32[32,8,512]{2,1,0:T(8,128)}, f32[32,8,512]{2,1,0:T(8,128)}, f32[32,8,512]{2,1,0:T(8,128)}) fusion(f32[32,512]{1,0:T(8,128)S(1)} %get-tuple-element.42, f32[32,512]{1,0:T(8,128)S(1)} %get-tuple-element.46, f32[32,512]{1,0:T(8,128)S(1)} %get-tuple-element.41, f32[32,512]{1,0:T(8,128)S(1)} %get-tuple-element.26, ...), kind=kLoop, calls=%fused_computation.55 | loop fusion | flops 4718592 | bytes 3080216 | tf_op jit(solution)/shard_map/while/body/eval_jaxpr/jit(_where)/select_n | solution.py:45
  6.6 0.0 copy-start
  6.6 4.7 %eval_jaxpr.2 = f32[32,64,64]{2,1,0:T(8,128)} custom-call(f32[32,4,512]{2,1,0:T(4,128)} %get-tuple-element.69.upr, f32[32,4,512]{2,1,0:T(4,128)} %get-tuple-element.70.upi, f32[32,8,512]{2,1,0:T(8,128)} %get-tuple-element.64.uqr, f32[32,8,512]{2,1,0:T(8,128)} %get-tuple-element.65.uqi, f32[32,4,512]{2,1,0:T(4,128)} %get-tuple-element.37.vpr, ...), custom_call_target="tpu_custom_call" | custom-call | flops 159383552 | bytes 3670016 | tf_op jit(solution)/shard_map/while/body/eval_jaxpr/pallas_call | solution.py:92
  11.3 0.0 copy-done
  11.3 1.9 %fusion.42 = (f32[32,32,32]{2,1,0:T(8,128)S(1)}, f32[32,32,32]{2,1,0:T(8,128)S(1)}) fusion(f32[32,64,64]{2,1,0:T(8,128)} %eval_jaxpr.2, f32[32,32]{1,0:T(8,128)S(1)} %copy-done), kind=kLoop, calls=%fused_computation.61 | loop fusion | flops 131072 | bytes 790528 | tf_op jit(solution)/shard_map/while/body/eval_jaxpr/mul | solution.py:119
  13.2 0.1 fusion.79
  13.4 1.8 %convolution_bitcast_fusion = f32[32,64,32]{1,2,0:T(8,128)S(1)} fusion(f32[32,32,32]{2,1,0:T(8,128)S(1)} %get-tuple-element.29, f32[32,32,32]{2,1,0:T(8,128)S(1)} %get-tuple-element.28, f32[32,32]{1,0:T(8,128)S(1)} %get-tuple-element.68, f32[32,32]{1,0:T(8,128)S(1)} %get-tuple-element.67, f32[32,32]{1,0:T(8,128)S(1)} %get-tuple-element.66), kind=kOutput, calls=%fused_computation.11 | convolution fusion | flops 50409472 | bytes 536576 | tf_op jit(solution)/shard_map/while/body/eval_jaxpr/ij,bjq->biq/dot_general | solution.py:127
  15.2 0.2 fusion.92
  15.4 1.8 %fusion.9 = bf16[32,32,64]{2,1,0:T(8,128)(2,1)S(1)} fusion(f32[32,32,32]{1,2,0:T(8,128)S(1)} %get-tuple-element.33, f32[32,32,32]{1,2,0:T(8,128)S(1)} %get-tuple-element.32, f32[32,32]{1,0:T(8,128)S(1)} %get-tuple-element.68, f32[32,32]{1,0:T(8,128)S(1)} %get-tuple-element.66, f32[32,32]{1,0:T(8,128)S(1)} %get-tuple-element.67), kind=kOutput, calls=%fused_computation.12 | convolution fusion | flops 50540544 | bytes 405504 | tf_op jit(solution)/shard_map/while/body/eval_jaxpr/baj,jk->bak/dot_general | solution.py:132
  17.3 0.2 convert_element_type.111
  17.5 0.0 copy-start.3
  17.5 0.0 copy-start.2
  17.5 0.0 copy-start.4
  17.6 0.1 copy.83
  17.7 0.5 reshape.437
  18.2 0.0 copy-done.3
  18.2 0.1 fusion.10
  18.4 0.9 scatter_custom_fusion
  19.3 0.2 reshape.427
  19.5 0.0 copy-done.2
  19.5 0.0 copy-done.4
  19.5 0.1 pad_maximum_fusion.7
  19.6 0.1 copy.65
  19.7 0.7 scatter_custom_fusion.1
  20.4 1.0 pad_maximum_fusion
  21.3 10.7 %all-to-all-start = ((bf16[32,2,2052]{2,1,0:T(2,128)(2,1)}), bf16[32,2,2052]{2,1,0:T(2,128)(2,1)S(1)}, u32[]{:S(2)}, u32[]{:S(2)}) async-start(bf16[32,2,2052]{2,1,0:T(2,128)(2,1)} %pad_maximum_fusion), calls=%async_computation | async-start | bytes 557056 | tf_op jit(solution)/shard_map/all_to_all | solution.py:17
  32.0 9.6 %all-to-all-done = bf16[32,2,2052]{2,1,0:T(2,128)(2,1)S(1)} async-done(((bf16[32,2,2052]{2,1,0:T(2,128)(2,1)}), bf16[32,2,2052]{2,1,0:T(2,128)(2,1)S(1)}, u32[]{:S(2)}, u32[]{:S(2)}) %all-to-all-start) | async-done | bytes 262688 | tf_op jit(solution)/shard_map/all_to_all | solution.py:17
  41.6 0.2 split.8
  41.8 0.5 reshape.429
  42.3 0.2 slice_reduce_fusion.1
  42.5 0.1 iota_add_fusion.1
  42.6 0.1 add_multiply_fusion.8
  42.7 0.1 copy.77
  42.8 0.1 iota_add_fusion
  42.9 0.4 fusion.20
  43.2 0.5 fusion.5
  43.7 0.1 fusion.85
  43.8 0.9 fusion.6
  44.7 0.1 copy.68
  44.9 34.7 %all_to_all.15 = f32[24,22,128]{2,1,0:T(8,128)S(1)} all-to-all(f32[24,22,128]{2,1,0:T(8,128)S(1)} %reshape.430), channel_id=1, replica_groups=mesh['span'=32,'freq'=24] {'freq'}, dimensions={0} | all-to-all | bytes 540672 | tf_op jit(solution)/shard_map/all_to_all | solution.py:27
  79.7 20.8 %all_to_all.16 = f32[24,22,128]{2,1,0:T(8,128)S(1)} all-to-all(f32[24,22,128]{2,1,0:T(8,128)S(1)} %broadcast_in_dim.321), channel_id=1, replica_groups=mesh['span'=32,'freq'=24] {'freq'}, dimensions={0} | all-to-all | bytes 540672 | tf_op jit(solution)/shard_map/all_to_all | solution.py:30
  100.5 0.7 slice_multiply_fusion
  (19 shorter events, 0.3 us)
Async XLA Ops:
  0.0 2.4 %copy-start.1 = (s32[1,32]{1,0:T(1,128)S(1)}, s32[1,32]{1,0:T(1,128)}, u32[]{:S(2)}) copy-start(s32[1,32]{1,0:T(1,128)} %param.9) | copy-start | bytes 388
  6.6 4.7 %copy-start = (f32[32,32]{1,0:T(8,128)S(1)}, f32[32,32]{1,0:T(8,128)}, u32[]{:S(2)}) copy-start(f32[32,32]{1,0:T(8,128)} %param.13) | copy-start | bytes 12292
  17.5 0.7 copy-start.3
  17.5 1.9 %copy-start.2 = (s32[1,32,2]{1,2,0:T(2,128)S(1)}, s32[1,32,2]{1,2,0:T(2,128)}, u32[]{:S(2)}) copy-start(s32[1,32,2]{1,2,0:T(2,128)} %param.11) | copy-start | bytes 772
  17.5 2.0 %copy-start.4 = (s32[1,32]{1,0:T(1,128)S(1)}, s32[1,32]{1,0:T(1,128)}, u32[]{:S(2)}) copy-start(s32[1,32]{1,0:T(1,128)} %param.12) | copy-start | bytes 388
  21.3 20.3 %all-to-all-start = ((bf16[32,2,2052]{2,1,0:T(2,128)(2,1)}), bf16[32,2,2052]{2,1,0:T(2,128)(2,1)S(1)}, u32[]{:S(2)}, u32[]{:S(2)}) async-start(bf16[32,2,2052]{2,1,0:T(2,128)(2,1)} %pad_maximum_fusion), calls=%async_computation | async-start | bytes 557056 | tf_op jit(solution)/shard_map/all_to_all | solution.py:17

commit v6 on v5

--- a/solution.py
+++ b/solution.py
@@ -35,72 +35,70 @@
     return ar * br - ai * bi, ar * bi + ai * br
 
 
-def bit_powers(c, s, bits, first, count):
-    j = jnp.arange(count, dtype=jnp.int32)[None, :, None]
-    re = jnp.broadcast_to(first[0][:, None, :], (c.shape[0], count, c.shape[1]))
-    im = jnp.broadcast_to(first[1][:, None, :], (c.shape[0], count, c.shape[1]))
-    for i, (br, bi) in enumerate(bits):
-        on = ((j >> i) & 1) == 1
-        mr, mi = cmul(re, im, br[:, None, :], bi[:, None, :])
-        re, im = jnp.where(on, mr, re), jnp.where(on, mi, im)
-    return re, im
-
-
-def phase_table(angle, vis=None):
+def kernel_tables(angle, vis=None):
     c, s = jnp.cos(angle), jnp.sin(angle)
-    w2 = cmul(c, s, c, s)
+    w1 = (c, s)
+    w2 = cmul(*w1, *w1)
     w4 = cmul(*w2, *w2)
     w8 = cmul(*w4, *w4)
     w16 = cmul(*w8, *w8)
     lo = (w16[0], -w16[1])
     if vis is not None:
-        lo = cmul(vis[0], vis[1], *lo)
+        lo = cmul(*vis, *lo)
     one = (jnp.ones_like(c), jnp.zeros_like(c))
-    small = bit_powers(c, s, [(c, s), w2], one, 4)
-    big = bit_powers(c, s, [w4, w8, w16], lo, 8)
+    small = [one, w1, w2, cmul(*w2, *w1)]
+    big = []
+    for j in range(8):
+        q = lo
+        for bit, wp in enumerate((w4, w8, w16)):
+            if (j >> bit) & 1:
+                q = cmul(*q, *wp)
+        big.append(q)
     return small, big
 
 
-def phase_rows(pr, pi, qr, qi, b):
-    p_r = jnp.concatenate([pr[b], pr[b]], axis=0)
-    p_i = jnp.concatenate([pi[b], pi[b]], axis=0)
+def kernel_rows(small, big, b):
+    p_r = jnp.concatenate([small[i % 4][0][b : b + 1] for i in range(8)], axis=0)
+    p_i = jnp.concatenate([small[i % 4][1][b : b + 1] for i in range(8)], axis=0)
     first = lax.broadcasted_iota(jnp.int32, p_r.shape, 0) < 4
     res, ims = [], []
     for m in range(4):
-        q_r = jnp.where(first, qr[b, 2 * m : 2 * m + 1, :], qr[b, 2 * m + 1 : 2 * m + 2, :])
-        q_i = jnp.where(first, qi[b, 2 * m : 2 * m + 1, :], qi[b, 2 * m + 1 : 2 * m + 2, :])
+        qa, qb = big[2 * m], big[2 * m + 1]
+        q_r = jnp.where(first, qa[0][b : b + 1], qb[0][b : b + 1])
+        q_i = jnp.where(first, qa[1][b : b + 1], qb[1][b : b + 1])
         r, i = cmul(q_r, q_i, p_r, p_i)
         res.append(r)
         ims.append(i)
     return jnp.concatenate(res + ims, axis=0).astype(jnp.bfloat16)
 
 
-def s_kernel(upr, upi, uqr, uqi, vpr, vpi, vqr, vqi, out):
+def s_kernel(u_ref, v_ref, vr_ref, vi_ref, out):
+    small_u, big_u = kernel_tables(u_ref[...])
+    small_v, big_v = kernel_tables(v_ref[...], (vr_ref[...], vi_ref[...]))
     for b in range(out.shape[0]):
-        a = phase_rows(upr, upi, uqr, uqi, b)
-        bb = phase_rows(vpr, vpi, vqr, vqi, b)
+        a = kernel_rows(small_u, big_u, b)
+        bb = kernel_rows(small_v, big_v, b)
         out[b] = lax.dot_general(
             a, bb, (((1,), (1,)), ((), ())), preferred_element_type=jnp.float32
         )
 
 
-def s_matrices(small_u, big_u, small_v, big_v):
-    n, _, kk = small_u[0].shape
+def s_matrices(u_ang, v_ang, vis_re, vis_im):
+    n, kk = u_ang.shape
     per = 8
-    spec_p = pl.BlockSpec((per, 4, kk), lambda g: (g, 0, 0))
-    spec_q = pl.BlockSpec((per, 8, kk), lambda g: (g, 0, 0))
+    spec = pl.BlockSpec((per, kk), lambda g: (g, 0))
     return pl.pallas_call(
         s_kernel,
         grid=(n // per,),
-        in_specs=[spec_p, spec_p, spec_q, spec_q] * 2,
+        in_specs=[spec] * 4,
         out_specs=pl.BlockSpec((per, 64, 64), lambda g: (g, 0, 0)),
         out_shape=jax.ShapeDtypeStruct((n, 64, 64), jnp.float32),
         cost_estimate=pl.CostEstimate(
             flops=2 * n * 64 * 64 * kk + 24 * n * 64 * kk,
-            transcendentals=0,
-            bytes_accessed=4 * n * 24 * kk * 2 + 4 * n * 64 * 64,
+            transcendentals=4 * n * kk,
+            bytes_accessed=4 * n * 4 * kk + 4 * n * 64 * 64,
         ),
-    )(*small_u, *big_u, *small_v, *big_v)
+    )(u_ang, v_ang, vis_re, vis_im)
 
 
 def make_subgrids(vis_b, coord_b, count_b, taper):
@@ -111,9 +109,7 @@
     vis_im = vis_b[:, 1, :].astype(jnp.float32) * live * scale_k
     step = -2.0 * math.pi / 32.0
     bf = jnp.bfloat16
-    small_u, big_u = phase_table(step * coord_b[:, 0, :])
-    small_v, big_v = phase_table(step * coord_b[:, 1, :], (vis_re, vis_im))
-    s_all = s_matrices(small_u, big_u, small_v, big_v)
+    s_all = s_matrices(step * coord_b[:, 0, :], step * coord_b[:, 1, :], vis_re, vis_im)
     s_re = s_all[:, :32, :32] - s_all[:, 32:, 32:]
     s_im = s_all[:, :32, 32:] + s_all[:, 32:, :32]
     x2 = jnp.concatenate([taper * s_re, taper * s_im], axis=1)

time: 102 us -> 103 us (level)
    select_n x2 -> x0, other arithmetic: 3.26 us -> none  [bit_powers(): re, im = (jnp.where(on, mr, re), jnp.where(on, mi, im))]
    mul x1 -> x2, other arithmetic: 0.57 us -> 2.03 us  [the longest x1 1.39 us: make_subgrids(): vis_im = vis_b[:, 1, :].astype(jnp.float32) * live * scale_k]
where the time goes in v6:
time: 103 us; the launch traced here: 102 us
  blocking collectives  55.5 us (54%)
  starting transfers between devices  10.5 us (10%)
  waiting for transfers between devices  9.74 us (9%)
  other arithmetic  8.61 us (8%)
  local copies, waits for them, and re-layouts  5.9 us (6%)
  matrix products  5.89 us (6%)
  Pallas kernels  5.44 us (5%)
    all_to_all x1, blocking collectives, gathered_total(): lax.all_to_all(flat.reshape(n, per // 128, 128), axis, 0, 0, tiled=True)  34.7 us
    all_to_all x1, blocking collectives, gathered_total(): whole = lax.all_to_all(spread, axis, 0, 0, tiled=True)  20.8 us
    all_to_all x1, starting transfers between devices, sent_together(): lax.all_to_all(both, axis, split_axis=split_dim, concat_axis=concat_dim,...  10.5 us
    all_to_all x1, waiting for transfers between devices, sent_together(): lax.all_to_all(both, axis, split_axis=split_dim, concat_axis=concat_dim,...  9.74 us
    pallas_call x1, Pallas kernels, s_matrices(): pl.pallas_call(s_kernel, grid=(n // per,), in_specs=[spec] * 4, out_specs...  5.44 us
  transfers between devices with their start and end apart: 1, of which 1 were waited for; matrix products, arithmetic and copies ran while one was open for 0% of the time, Pallas kernels for 0%

profile of v6, /device:TPU:1, one launch (start us, length us, event | category | flops | bytes accessed | tf_op | source)
XLA Modules:
  0.0 101.8 jit_solution(6931336296918665633)
XLA Ops:
  0.0 0.7 convert.18
  0.7 0.7 convert_bitcast_fusion.1
  1.4 0.9 fusion.10
  2.2 0.7 fusion.47
  2.9 0.1 pad_maximum_fusion.7
  3.0 0.1 copy.32
  3.1 0.9 copy.52
  3.9 0.0 copy-start
  4.0 0.9 copy.51
  4.9 0.6 fusion.26
  5.5 0.1 fusion.46
  5.7 1.4 %fusion.28 = (f32[32,512]{1,0:T(8,128)}, f32[32,512]{1,0:T(8,128)}) fusion(bf16[32,2,512]{2,0,1:T(8,128)(2,1)S(1)} %bitcast.81, s32[32]{0:T(128)} %bitcast.85), kind=kLoop, calls=%fused_computation.43 | loop fusion | flops 114688 | bytes 196736 | tf_op jit(solution)/shard_map/while/body/eval_jaxpr/mul | solution.py:109
  7.1 5.4 %eval_jaxpr.2 = f32[32,64,64]{2,1,0:T(8,128)} custom-call(f32[32,512]{1,0:T(8,128)} %get-tuple-element.30.u_ref, f32[32,512]{1,0:T(8,128)} %get-tuple-element.29.v_ref, f32[32,512]{1,0:T(8,128)} %get-tuple-element.32.vr_ref, f32[32,512]{1,0:T(8,128)} %get-tuple-element.31.vi_ref), custom_call_target="tpu_custom_call" | custom-call | flops 159383552 | bytes 786432 | tf_op jit(solution)/shard_map/while/body/eval_jaxpr/pallas_call | solution.py:90
  12.5 0.0 copy-done
  12.5 1.9 %fusion.22 = (f32[32,32,32]{2,1,0:T(8,128)S(1)}, f32[32,32,32]{2,1,0:T(8,128)S(1)}) fusion(f32[32,64,64]{2,1,0:T(8,128)} %eval_jaxpr.2, f32[32,32]{1,0:T(8,128)S(1)} %copy-done), kind=kLoop, calls=%fused_computation.29 | loop fusion | flops 131072 | bytes 790528 | tf_op jit(solution)/shard_map/while/body/eval_jaxpr/mul | solution.py:115
  14.4 1.8 %convolution_bitcast_fusion = f32[32,64,32]{1,2,0:T(8,128)S(1)} fusion(f32[32,32,32]{2,1,0:T(8,128)S(1)} %get-tuple-element.24, f32[32,32,32]{2,1,0:T(8,128)S(1)} %get-tuple-element.17, f32[32,32]{1,0:T(8,128)S(1)} %get-tuple-element.39, f32[32,32]{1,0:T(8,128)S(1)} %get-tuple-element.38, f32[32,32]{1,0:T(8,128)S(1)} %get-tuple-element.37), kind=kOutput, calls=%fused_computation.11 | convolution fusion | flops 50409472 | bytes 536576 | tf_op jit(solution)/shard_map/while/body/eval_jaxpr/ij,bjq->biq/dot_general | solution.py:123
  16.2 0.2 fusion.51
  16.4 1.8 %fusion.9 = bf16[32,32,64]{2,1,0:T(8,128)(2,1)S(1)} fusion(f32[32,32,32]{1,2,0:T(8,128)S(1)} %get-tuple-element.28, f32[32,32,32]{1,2,0:T(8,128)S(1)} %get-tuple-element.26, f32[32,32]{1,0:T(8,128)S(1)} %get-tuple-element.39, f32[32,32]{1,0:T(8,128)S(1)} %get-tuple-element.37, f32[32,32]{1,0:T(8,128)S(1)} %get-tuple-element.38), kind=kOutput, calls=%fused_computation.12 | convolution fusion | flops 50540544 | bytes 405504 | tf_op jit(solution)/shard_map/while/body/eval_jaxpr/baj,jk->bak/dot_general | solution.py:128
  18.3 0.2 convert_element_type.115
  18.5 0.1 copy.50
  18.6 0.5 reshape.355
  19.2 0.7 scatter_custom_fusion.1
  19.9 0.9 scatter_custom_fusion
  20.7 0.2 reshape.343
  20.9 1.0 pad_maximum_fusion
  21.9 10.5 %all-to-all-start = ((bf16[32,2,2052]{2,1,0:T(2,128)(2,1)}), bf16[32,2,2052]{2,1,0:T(2,128)(2,1)S(1)}, u32[]{:S(2)}, u32[]{:S(2)}) async-start(bf16[32,2,2052]{2,1,0:T(2,128)(2,1)} %pad_maximum_fusion), calls=%async_computation | async-start | bytes 557056 | tf_op jit(solution)/shard_map/all_to_all | solution.py:17
  32.4 9.7 %all-to-all-done = bf16[32,2,2052]{2,1,0:T(2,128)(2,1)S(1)} async-done(((bf16[32,2,2052]{2,1,0:T(2,128)(2,1)}), bf16[32,2,2052]{2,1,0:T(2,128)(2,1)S(1)}, u32[]{:S(2)}, u32[]{:S(2)}) %all-to-all-start) | async-done | bytes 262688 | tf_op jit(solution)/shard_map/all_to_all | solution.py:17
  42.2 0.2 slice_reduce_fusion.1
  42.4 0.1 add_multiply_fusion
  42.5 0.1 copy.44
  42.6 0.1 iota_add_fusion.1
  42.6 0.1 iota_add_fusion
  42.7 0.2 split.8
  42.9 0.5 reshape.345
  43.4 0.3 fusion.20
  43.8 0.1 fusion.50
  43.9 0.5 fusion.5
  44.4 0.9 fusion.6
  45.3 0.1 copy.35
  45.5 34.7 %all_to_all.15 = f32[24,22,128]{2,1,0:T(8,128)S(1)} all-to-all(f32[24,22,128]{2,1,0:T(8,128)S(1)} %reshape.346), channel_id=1, replica_groups=mesh['span'=32,'freq'=24] {'freq'}, dimensions={0} | all-to-all | bytes 540672 | tf_op jit(solution)/shard_map/all_to_all | solution.py:27
  80.3 20.8 %all_to_all.16 = f32[24,22,128]{2,1,0:T(8,128)S(1)} all-to-all(f32[24,22,128]{2,1,0:T(8,128)S(1)} %broadcast_in_dim.36), channel_id=1, replica_groups=mesh['span'=32,'freq'=24] {'freq'}, dimensions={0} | all-to-all | bytes 540672 | tf_op jit(solution)/shard_map/all_to_all | solution.py:30
  101.0 0.7 slice_multiply_fusion
  (13 shorter events, 0.2 us)
Async XLA Ops:
  3.9 8.6 %copy-start = (f32[32,32]{1,0:T(8,128)S(1)}, f32[32,32]{1,0:T(8,128)}, u32[]{:S(2)}) copy-start(f32[32,32]{1,0:T(8,128)} %param.13) | copy-start | bytes 12292
  21.9 20.3 %all-to-all-start = ((bf16[32,2,2052]{2,1,0:T(2,128)(2,1)}), bf16[32,2,2052]{2,1,0:T(2,128)(2,1)S(1)}, u32[]{:S(2)}, u32[]{:S(2)}) async-start(bf16[32,2,2052]{2,1,0:T(2,128)(2,1)} %pad_maximum_fusion), calls=%async_computation | async-start | bytes 557056 | tf_op jit(solution)/shard_map/all_to_all | solution.py:17

commit v7 on v6

--- a/solution.py
+++ b/solution.py
@@ -72,33 +72,42 @@
     return jnp.concatenate(res + ims, axis=0).astype(jnp.bfloat16)
 
 
-def s_kernel(u_ref, v_ref, vr_ref, vi_ref, out):
+def s_kernel(u_ref, v_ref, vr_ref, vi_ref, taper_ref, g_ref, h_ref, out):
     small_u, big_u = kernel_tables(u_ref[...])
     small_v, big_v = kernel_tables(v_ref[...], (vr_ref[...], vi_ref[...]))
+    tp, g, h = taper_ref[...], g_ref[...], h_ref[...]
+    hp = lax.Precision.HIGHEST
+    f32 = jnp.float32
     for b in range(out.shape[0]):
         a = kernel_rows(small_u, big_u, b)
         bb = kernel_rows(small_v, big_v, b)
-        out[b] = lax.dot_general(
-            a, bb, (((1,), (1,)), ((), ())), preferred_element_type=jnp.float32
-        )
-
-
-def s_matrices(u_ang, v_ang, vis_re, vis_im):
+        sm = lax.dot_general(a, bb, (((1,), (1,)), ((), ())), preferred_element_type=f32)
+        x_re = tp * (sm[:32, :32] - sm[32:, 32:])
+        x_im = tp * (sm[:32, 32:] + sm[32:, :32])
+        x2 = jnp.concatenate([x_re, x_im], axis=0)
+        y2 = jnp.dot(g, x2, precision=hp, preferred_element_type=f32)
+        ycat = jnp.concatenate([y2[:32], y2[32:]], axis=1)
+        z2 = jnp.dot(ycat, h, precision=hp, preferred_element_type=f32)
+        out[b] = (z2 / 32.0).astype(out.dtype)
+
+
+def subgrid_patches(u_ang, v_ang, vis_re, vis_im, taper, left, right):
     n, kk = u_ang.shape
     per = 8
     spec = pl.BlockSpec((per, kk), lambda g: (g, 0))
+    whole = pl.BlockSpec((64, 64), lambda g: (0, 0))
     return pl.pallas_call(
         s_kernel,
         grid=(n // per,),
-        in_specs=[spec] * 4,
-        out_specs=pl.BlockSpec((per, 64, 64), lambda g: (g, 0, 0)),
-        out_shape=jax.ShapeDtypeStruct((n, 64, 64), jnp.float32),
+        in_specs=[spec] * 4 + [pl.BlockSpec((32, 32), lambda g: (0, 0)), whole, whole],
+        out_specs=pl.BlockSpec((per, 32, 64), lambda g: (g, 0, 0)),
+        out_shape=jax.ShapeDtypeStruct((n, 32, 64), jnp.bfloat16),
         cost_estimate=pl.CostEstimate(
-            flops=2 * n * 64 * 64 * kk + 24 * n * 64 * kk,
+            flops=2 * n * 64 * 64 * kk + 24 * n * 64 * kk + 24 * n * 64 * 64 * 32,
             transcendentals=4 * n * kk,
-            bytes_accessed=4 * n * 4 * kk + 4 * n * 64 * 64,
+            bytes_accessed=4 * n * 4 * kk + 2 * n * 32 * 64,
         ),
-    )(u_ang, v_ang, vis_re, vis_im)
+    )(u_ang, v_ang, vis_re, vis_im, taper, left, right)
 
 
 def make_subgrids(vis_b, coord_b, count_b, taper):
@@ -108,26 +117,18 @@
     vis_re = vis_b[:, 0, :].astype(jnp.float32) * live * scale_k
     vis_im = vis_b[:, 1, :].astype(jnp.float32) * live * scale_k
     step = -2.0 * math.pi / 32.0
-    bf = jnp.bfloat16
-    s_all = s_matrices(step * coord_b[:, 0, :], step * coord_b[:, 1, :], vis_re, vis_im)
-    s_re = s_all[:, :32, :32] - s_all[:, 32:, 32:]
-    s_im = s_all[:, :32, 32:] + s_all[:, 32:, :32]
-    x2 = jnp.concatenate([taper * s_re, taper * s_im], axis=1)
     centred = jnp.arange(32, dtype=jnp.float32) - 16.0
     angle = -2.0 * math.pi * centred[:, None] * centred[None, :] / 32.0
     f_re, f_im = (jnp.cos(angle), jnp.sin(angle))
-    hp = lax.Precision.HIGHEST
     left = jnp.concatenate(
         [jnp.concatenate([f_re, -f_im], 1), jnp.concatenate([f_im, f_re], 1)], 0
     )
-    y2 = jnp.einsum("ij,bjq->biq", left, x2, precision=hp)
-    ycat = jnp.concatenate([y2[:, :32], y2[:, 32:]], axis=2)
     right = jnp.concatenate(
         [jnp.concatenate([f_re, f_im], 1), jnp.concatenate([-f_im, f_re], 1)], 0
     )
-    z2 = jnp.einsum("baj,jk->bak", ycat, right, precision=hp)
-    z = z2.reshape(z2.shape[0], 32, 2, 32).transpose(0, 2, 1, 3)
-    return (z / 32.0).astype(jnp.bfloat16)
+    return subgrid_patches(
+        step * coord_b[:, 0, :], step * coord_b[:, 1, :], vis_re, vis_im, taper, left, right
+    )
 
 
 def taylor_weights(chan_local, freq_pos, channels):
@@ -142,7 +143,7 @@
     cells = jnp.arange(TILE, dtype=jnp.int32)
     small = jnp.arange(32, dtype=jnp.int32)
     col_hot = (small[None, :, None] + cols[:, None, None] == cells[None, None, :]).astype(bf)
-    spread = jnp.einsum("scab,sbq->scaq", patch, col_hot, preferred_element_type=f32).astype(bf)
+    spread = jnp.einsum("sacb,sbq->scaq", patch, col_hot, preferred_element_type=f32).astype(bf)
     row_hot = (cells[None, :, None] == rows[:, None, None] + small[None, None, :]).astype(f32)
     w_hi = weight.astype(bf)
     w_lo = (weight - w_hi.astype(f32)).astype(bf)
@@ -166,7 +167,7 @@
     def block_work(inputs):
         return make_subgrids(inputs[0], inputs[1], inputs[2], taper)
 
-    patches = lax.map(block_work, (vis_loc, coord_loc, count_loc)).reshape(sub_count, 2, 32, 32)
+    patches = lax.map(block_work, (vis_loc, coord_loc, count_loc)).reshape(sub_count, 32, 2, 32)
     dest = cover_tile[0, :, 0]
     row_off = offsets[0, :, 0]
     col_off = offsets[0, :, 1]
@@ -191,7 +192,7 @@
     valid = got_meta[:, 0].astype(jnp.float32)
     weight = taylor_weights(got_meta[:, 3], freq_pos, channels) * valid[:, None]
     local = place_all(
-        got_payload.reshape(slots, 2, 32, 32), weight, got_meta[:, 1], got_meta[:, 2]
+        got_payload.reshape(slots, 32, 2, 32), weight, got_meta[:, 1], got_meta[:, 2]
     )
     local = local.reshape(NT, 1, 2, TILE, TILE)
     total = gathered_total(local, "freq")

time: 103 us -> 108 us (1.049)
  Pallas kernels: 5.44 us -> 15.2 us
  matrix products: 5.89 us -> 2.5 us
  other arithmetic: 8.61 us -> 7.44 us
    pallas_call x1, Pallas kernels: 5.44 us -> 15.2 us  [subgrid_patches(): pl.pallas_call(s_kernel, grid=(n // per,), in_specs=[spec] * 4 + [pl.Bloc...]
    dot_general x3 -> x1, matrix products: 4.16 us -> 0.76 us  [place_all(): jnp.einsum('sacb,sbq->scaq', patch, col_hot, preferred_element_type=f32)]
    mul x1 -> x0, other arithmetic: 1.88 us -> none  [make_subgrids(): x2 = jnp.concatenate([taper * s_re, taper * s_im], axis=1)]
where the time goes in v7:
time: 108 us; the launch traced here: 107 us
  blocking collectives  55.5 us (51%)
  Pallas kernels  15.2 us (14%)
  starting transfers between devices  10.5 us (10%)
  waiting for transfers between devices  9.74 us (9%)
  other arithmetic  7.44 us (7%)
  local copies, waits for them, and re-layouts  6.02 us (6%)
  matrix products  2.5 us (2%)
    all_to_all x1, blocking collectives, gathered_total(): lax.all_to_all(flat.reshape(n, per // 128, 128), axis, 0, 0, tiled=True)  34.7 us
    all_to_all x1, blocking collectives, gathered_total(): whole = lax.all_to_all(spread, axis, 0, 0, tiled=True)  20.8 us
    pallas_call x1, Pallas kernels, subgrid_patches(): pl.pallas_call(s_kernel, grid=(n // per,), in_specs=[spec] * 4 + [pl.Bloc...  15.2 us
    all_to_all x1, starting transfers between devices, sent_together(): lax.all_to_all(both, axis, split_axis=split_dim, concat_axis=concat_dim,...  10.5 us
    all_to_all x1, waiting for transfers between devices, sent_together(): lax.all_to_all(both, axis, split_axis=split_dim, concat_axis=concat_dim,...  9.74 us
  transfers between devices with their start and end apart: 1, of which 1 were waited for; matrix products, arithmetic and copies ran while one was open for 0% of the time, Pallas kernels for 0%

profile of v7, /device:TPU:1, one launch (start us, length us, event | category | flops | bytes accessed | tf_op | source)
XLA Modules:
  0.0 107.0 jit_solution(13344473901985452493)
XLA Ops:
  0.0 0.7 convert.18
  0.7 0.7 convert_bitcast_fusion.1
  1.4 0.9 fusion.9
  2.2 0.7 fusion.31
  2.9 0.1 pad_maximum_fusion.5
  3.0 0.1 copy.22
  3.1 0.9 copy.41
  3.9 0.9 copy.40
  4.9 0.6 fusion.18
  5.5 0.1 fusion.30
  5.7 1.4 %fusion.20 = (f32[32,512]{1,0:T(8,128)}, f32[32,512]{1,0:T(8,128)}) fusion(bf16[32,2,512]{2,0,1:T(8,128)(2,1)S(1)} %bitcast.68, s32[32]{0:T(128)} %bitcast.72), kind=kLoop, calls=%fused_computation.30 | loop fusion | flops 114688 | bytes 196736 | tf_op jit(solution)/shard_map/while/body/eval_jaxpr/mul | solution.py:118
  7.1 0.7 fusion.23
  7.8 15.2 %eval_jaxpr.2 = bf16[32,32,64]{2,1,0:T(8,128)(2,1)} custom-call(f32[32,512]{1,0:T(8,128)} %get-tuple-element.17.u_ref, f32[32,512]{1,0:T(8,128)} %get-tuple-element.16.v_ref, f32[32,512]{1,0:T(8,128)} %get-tuple-element.26.vr_ref, f32[32,512]{1,0:T(8,128)} %get-tuple-element.24.vi_ref, f32[32,32]{1,0:T(8,128)} %taper_ref, f32[64,64]{1,0:T(8,128)} %get-tuple-element.29.g_ref, ...), custom_call_target="tpu_custom_call" | custom-call | flops 260046848 | bytes 393216 | tf_op jit(solution)/shard_map/while/body/eval_jaxpr/pallas_call | solution.py:99
  23.0 1.2 %reshape.349 = bf16[32,2048]{1,0:T(8,128)(2,1)S(1)} reshape(bf16[32,32,64]{2,1,0:T(8,128)(2,1)} %eval_jaxpr.2) | data formatting | bytes 262144 | tf_op jit(solution)/shard_map/reshape;reshape | solution.py:183
  24.2 0.7 scatter_custom_fusion.1
  24.9 0.9 scatter_custom_fusion
  25.7 0.2 reshape.337
  25.9 1.0 pad_maximum_fusion
  26.9 10.5 %all-to-all-start = ((bf16[32,2,2052]{2,1,0:T(2,128)(2,1)}), bf16[32,2,2052]{2,1,0:T(2,128)(2,1)S(1)}, u32[]{:S(2)}, u32[]{:S(2)}) async-start(bf16[32,2,2052]{2,1,0:T(2,128)(2,1)} %pad_maximum_fusion), calls=%async_computation | async-start | bytes 557056 | tf_op jit(solution)/shard_map/all_to_all | solution.py:17
  37.4 9.7 %all-to-all-done = bf16[32,2,2052]{2,1,0:T(2,128)(2,1)S(1)} async-done(((bf16[32,2,2052]{2,1,0:T(2,128)(2,1)}), bf16[32,2,2052]{2,1,0:T(2,128)(2,1)S(1)}, u32[]{:S(2)}, u32[]{:S(2)}) %all-to-all-start) | async-done | bytes 262688 | tf_op jit(solution)/shard_map/all_to_all | solution.py:17
  47.2 0.2 slice_reduce_fusion.1
  47.4 0.1 add_multiply_fusion
  47.5 0.1 copy.33
  47.6 0.1 iota_add_fusion.1
  47.6 0.1 iota_add_fusion
  47.7 0.2 split.9
  47.9 0.5 reshape.339
  48.4 0.3 fusion.14
  48.8 0.1 fusion.32
  48.9 0.8 fusion.5
  49.6 0.9 fusion.6
  50.5 0.1 copy.26
  50.7 34.7 %all_to_all.15 = f32[24,22,128]{2,1,0:T(8,128)S(1)} all-to-all(f32[24,22,128]{2,1,0:T(8,128)S(1)} %reshape.340), channel_id=1, replica_groups=mesh['span'=32,'freq'=24] {'freq'}, dimensions={0} | all-to-all | bytes 540672 | tf_op jit(solution)/shard_map/all_to_all | solution.py:27
  85.5 20.8 %all_to_all.16 = f32[24,22,128]{2,1,0:T(8,128)S(1)} all-to-all(f32[24,22,128]{2,1,0:T(8,128)S(1)} %broadcast_in_dim.33), channel_id=1, replica_groups=mesh['span'=32,'freq'=24] {'freq'}, dimensions={0} | all-to-all | bytes 540672 | tf_op jit(solution)/shard_map/all_to_all | solution.py:30
  106.3 0.7 slice_multiply_fusion
  (13 shorter events, 0.2 us)
Async XLA Ops:
  26.9 20.3 %all-to-all-start = ((bf16[32,2,2052]{2,1,0:T(2,128)(2,1)}), bf16[32,2,2052]{2,1,0:T(2,128)(2,1)S(1)}, u32[]{:S(2)}, u32[]{:S(2)}) async-start(bf16[32,2,2052]{2,1,0:T(2,128)(2,1)} %pad_maximum_fusion), calls=%async_computation | async-start | bytes 557056 | tf_op jit(solution)/shard_map/all_to_all | solution.py:17

commit v8 on v6

--- a/solution.py
+++ b/solution.py
@@ -178,14 +178,12 @@
     earlier = jnp.dot(lower, onehot, preferred_element_type=jnp.float32)
     rank = jnp.sum(earlier * onehot, axis=1).astype(jnp.int32)
     slot = dest * cap + rank
-    payload = (
-        jnp.zeros((n_span * cap, 2048), jnp.bfloat16).at[slot].set(patches.reshape(sub_count, 2048))
-    )
     info = jnp.stack([jnp.ones_like(dest), row_off, col_off, chan_loc], 1).astype(jnp.bfloat16)
-    meta = jnp.zeros((n_span * cap, 4), jnp.bfloat16).at[slot].set(info)
-    got_payload, got_meta = sent_together(
-        (payload.reshape(n_span, cap, 2048), meta.reshape(n_span, cap, 4)), "span", 0, 0, 2
-    )
+    rows = jnp.concatenate([patches.reshape(sub_count, 2048), info], axis=1)
+    pick = (slot[None, :] == jnp.arange(n_span * cap, dtype=jnp.int32)[:, None]).astype(jnp.bfloat16)
+    send = jnp.dot(pick, rows, preferred_element_type=jnp.float32).astype(jnp.bfloat16)
+    got = lax.all_to_all(send.reshape(n_span, cap, 2052), "span", 0, 0, tiled=True)
+    got_payload, got_meta = got[:, :, :2048], got[:, :, 2048:]
     slots = n_span * cap
     got_meta = got_meta.reshape(slots, 4).astype(jnp.int32)
     valid = got_meta[:, 0].astype(jnp.float32)

time: 103 us -> 101 us (0.981)
  other arithmetic: 8.61 us -> 7.57 us
    scatter x2 -> x0, local copies, waits for them, and re-layouts: 1.55 us -> none  [the longest x1 0.88 us: body(): jnp.zeros((n_span * cap, 2048), jnp.bfloat16).at[slot]]
where the time goes in v8:
time: 101 us; the launch traced here: 100 us
  blocking collectives  55.5 us (55%)
  starting transfers between devices  10.5 us (10%)
  waiting for transfers between devices  9.74 us (10%)
  other arithmetic  7.57 us (7%)
  matrix products  6.11 us (6%)
  Pallas kernels  5.44 us (5%)
  local copies, waits for them, and re-layouts  5.28 us (5%)
    all_to_all x1, blocking collectives, gathered_total(): lax.all_to_all(flat.reshape(n, per // 128, 128), axis, 0, 0, tiled=True)  34.7 us
    all_to_all x1, blocking collectives, gathered_total(): whole = lax.all_to_all(spread, axis, 0, 0, tiled=True)  20.8 us
    all_to_all x1, starting transfers between devices, body(): lax.all_to_all(send.reshape(n_span, cap, 2052), 'span', 0, 0, tiled=True)  10.5 us
    all_to_all x1, waiting for transfers between devices, body(): lax.all_to_all(send.reshape(n_span, cap, 2052), 'span', 0, 0, tiled=True)  9.74 us
    pallas_call x1, Pallas kernels, s_matrices(): pl.pallas_call(s_kernel, grid=(n // per,), in_specs=[spec] * 4, out_specs...  5.44 us
  transfers between devices with their start and end apart: 1, of which 1 were waited for; matrix products, arithmetic and copies ran while one was open for 0% of the time, Pallas kernels for 0%

profile of v8, /device:TPU:1, one launch (start us, length us, event | category | flops | bytes accessed | tf_op | source)
XLA Modules:
  0.0 100.3 jit_solution(499214626211850296)
XLA Ops:
  0.0 0.7 convert.18
  0.7 0.7 convert_bitcast_fusion.1
  1.4 0.9 fusion.10
  2.2 0.7 convert_add_fusion
  2.9 0.1 copy.41
  3.0 0.1 copy.42
  3.1 0.1 copy.40
  3.2 0.9 copy.62
  4.1 0.0 copy-start
  4.1 0.9 copy.61
  5.0 0.6 fusion.24
  5.7 0.1 fusion.43
  5.8 1.4 %fusion.26 = (f32[32,512]{1,0:T(8,128)}, f32[32,512]{1,0:T(8,128)}) fusion(bf16[32,2,512]{2,0,1:T(8,128)(2,1)S(1)} %bitcast.71, s32[32]{0:T(128)} %bitcast.74), kind=kLoop, calls=%fused_computation.39 | loop fusion | flops 114688 | bytes 196736 | tf_op jit(solution)/shard_map/while/body/eval_jaxpr/mul | solution.py:109
  7.2 5.4 %eval_jaxpr.2 = f32[32,64,64]{2,1,0:T(8,128)} custom-call(f32[32,512]{1,0:T(8,128)} %get-tuple-element.30.u_ref, f32[32,512]{1,0:T(8,128)} %get-tuple-element.29.v_ref, f32[32,512]{1,0:T(8,128)} %get-tuple-element.32.vr_ref, f32[32,512]{1,0:T(8,128)} %get-tuple-element.31.vi_ref), custom_call_target="tpu_custom_call" | custom-call | flops 159383552 | bytes 786432 | tf_op jit(solution)/shard_map/while/body/eval_jaxpr/pallas_call | solution.py:90
  12.6 0.0 copy-done
  12.6 1.9 %fusion.22 = (f32[32,32,32]{2,1,0:T(8,128)S(1)}, f32[32,32,32]{2,1,0:T(8,128)S(1)}) fusion(f32[32,64,64]{2,1,0:T(8,128)} %eval_jaxpr.2, f32[32,32]{1,0:T(8,128)S(1)} %copy-done), kind=kLoop, calls=%fused_computation.28 | loop fusion | flops 131072 | bytes 790528 | tf_op jit(solution)/shard_map/while/body/eval_jaxpr/mul | solution.py:115
  14.5 1.8 %convolution_bitcast_fusion = f32[32,64,32]{1,2,0:T(8,128)S(1)} fusion(f32[32,32,32]{2,1,0:T(8,128)S(1)} %get-tuple-element.24, f32[32,32,32]{2,1,0:T(8,128)S(1)} %get-tuple-element.17, f32[32,32]{1,0:T(8,128)S(1)} %get-tuple-element.39, f32[32,32]{1,0:T(8,128)S(1)} %get-tuple-element.38, f32[32,32]{1,0:T(8,128)S(1)} %get-tuple-element.37), kind=kOutput, calls=%fused_computation.10 | convolution fusion | flops 50409472 | bytes 536576 | tf_op jit(solution)/shard_map/while/body/eval_jaxpr/ij,bjq->biq/dot_general | solution.py:123
  16.3 0.2 fusion.47
  16.5 1.8 %fusion.9 = bf16[32,32,64]{2,1,0:T(8,128)(2,1)S(1)} fusion(f32[32,32,32]{1,2,0:T(8,128)S(1)} %get-tuple-element.28, f32[32,32,32]{1,2,0:T(8,128)S(1)} %get-tuple-element.26, f32[32,32]{1,0:T(8,128)S(1)} %get-tuple-element.39, f32[32,32]{1,0:T(8,128)S(1)} %get-tuple-element.37, f32[32,32]{1,0:T(8,128)S(1)} %get-tuple-element.38), kind=kOutput, calls=%fused_computation.11 | convolution fusion | flops 50540544 | bytes 405504 | tf_op jit(solution)/shard_map/while/body/eval_jaxpr/baj,jk->bak/dot_general | solution.py:128
  18.4 0.2 convert_element_type.112
  18.6 0.1 copy.60
  18.8 0.5 reshape_reshape.4
  19.3 0.1 concatenate.44
  19.4 0.2 convolution_convert_fusion
  19.6 0.8 reshape.317
  20.4 10.5 %all-to-all-start = ((bf16[32,2,2052]{2,1,0:T(2,128)(2,1)}), bf16[32,2,2052]{2,1,0:T(2,128)(2,1)S(1)}, u32[]{:S(2)}, u32[]{:S(2)}) async-start(bf16[32,2,2052]{2,1,0:T(2,128)(2,1)} %reshape.317), calls=%async_computation | async-start | bytes 557056 | tf_op jit(solution)/shard_map/all_to_all | solution.py:185
  31.0 9.7 %all-to-all-done = bf16[32,2,2052]{2,1,0:T(2,128)(2,1)S(1)} async-done(((bf16[32,2,2052]{2,1,0:T(2,128)(2,1)}), bf16[32,2,2052]{2,1,0:T(2,128)(2,1)S(1)}, u32[]{:S(2)}, u32[]{:S(2)}) %all-to-all-start) | async-done | bytes 262688 | tf_op jit(solution)/shard_map/all_to_all | solution.py:185
  40.7 0.2 slice_reduce_fusion.1
  40.9 0.1 add_multiply_fusion
  41.0 0.1 copy.54
  41.1 0.1 iota_add_fusion.1
  41.2 0.1 iota_add_fusion
  41.3 0.2 slice.109
  41.5 0.5 reshape.318
  42.0 0.3 fusion.20
  42.3 0.1 fusion.46
  42.4 0.5 fusion.5
  42.9 0.9 fusion.6
  43.8 0.1 copy.45
  44.0 34.7 %all_to_all.15 = f32[24,22,128]{2,1,0:T(8,128)S(1)} all-to-all(f32[24,22,128]{2,1,0:T(8,128)S(1)} %reshape.319), channel_id=1, replica_groups=mesh['span'=32,'freq'=24] {'freq'}, dimensions={0} | all-to-all | bytes 540672 | tf_op jit(solution)/shard_map/all_to_all | solution.py:27
  78.8 20.8 %all_to_all.16 = f32[24,22,128]{2,1,0:T(8,128)S(1)} all-to-all(f32[24,22,128]{2,1,0:T(8,128)S(1)} %broadcast_in_dim.26), channel_id=1, replica_groups=mesh['span'=32,'freq'=24] {'freq'}, dimensions={0} | all-to-all | bytes 540672 | tf_op jit(solution)/shard_map/all_to_all | solution.py:30
  99.6 0.7 slice_multiply_fusion
  (13 shorter events, 0.2 us)
Async XLA Ops:
  4.1 8.6 %copy-start = (f32[32,32]{1,0:T(8,128)S(1)}, f32[32,32]{1,0:T(8,128)}, u32[]{:S(2)}) copy-start(f32[32,32]{1,0:T(8,128)} %param.13) | copy-start | bytes 12292
  20.4 20.3 %all-to-all-start = ((bf16[32,2,2052]{2,1,0:T(2,128)(2,1)}), bf16[32,2,2052]{2,1,0:T(2,128)(2,1)S(1)}, u32[]{:S(2)}, u32[]{:S(2)}) async-start(bf16[32,2,2052]{2,1,0:T(2,128)(2,1)} %reshape.317), calls=%async_computation | async-start | bytes 557056 | tf_op jit(solution)/shard_map/all_to_all | solution.py:185

commit v9 on v8

--- a/solution.py
+++ b/solution.py
@@ -72,9 +72,17 @@
     return jnp.concatenate(res + ims, axis=0).astype(jnp.bfloat16)
 
 
-def s_kernel(u_ref, v_ref, vr_ref, vi_ref, out):
-    small_u, big_u = kernel_tables(u_ref[...])
-    small_v, big_v = kernel_tables(v_ref[...], (vr_ref[...], vi_ref[...]))
+def s_kernel(coord_ref, vis_ref, count_ref, out):
+    kk = coord_ref.shape[-1]
+    step = -2.0 * math.pi / 32.0
+    live = lax.broadcasted_iota(jnp.int32, (coord_ref.shape[0], kk), 1) < count_ref[...]
+    scale_k = 1.0 / math.sqrt(kk)
+    vis = vis_ref[...].astype(jnp.float32)
+    coord = coord_ref[...]
+    vr = jnp.where(live, vis[:, 0, :] * scale_k, 0.0)
+    vi = jnp.where(live, vis[:, 1, :] * scale_k, 0.0)
+    small_u, big_u = kernel_tables(step * coord[:, 0, :])
+    small_v, big_v = kernel_tables(step * coord[:, 1, :], (vr, vi))
     for b in range(out.shape[0]):
         a = kernel_rows(small_u, big_u, b)
         bb = kernel_rows(small_v, big_v, b)
@@ -83,33 +91,26 @@
         )
 
 
-def s_matrices(u_ang, v_ang, vis_re, vis_im):
-    n, kk = u_ang.shape
+def s_matrices(coords, vis, counts):
+    n, _, kk = coords.shape
     per = 8
-    spec = pl.BlockSpec((per, kk), lambda g: (g, 0))
+    both = pl.BlockSpec((per, 2, kk), lambda g: (g, 0, 0))
     return pl.pallas_call(
         s_kernel,
         grid=(n // per,),
-        in_specs=[spec] * 4,
+        in_specs=[both, both, pl.BlockSpec((per, 1), lambda g: (g, 0))],
         out_specs=pl.BlockSpec((per, 64, 64), lambda g: (g, 0, 0)),
         out_shape=jax.ShapeDtypeStruct((n, 64, 64), jnp.float32),
         cost_estimate=pl.CostEstimate(
             flops=2 * n * 64 * 64 * kk + 24 * n * 64 * kk,
             transcendentals=4 * n * kk,
-            bytes_accessed=4 * n * 4 * kk + 4 * n * 64 * 64,
+            bytes_accessed=6 * n * 2 * kk + 4 * n * 64 * 64,
         ),
-    )(u_ang, v_ang, vis_re, vis_im)
+    )(coords, vis, counts)
 
 
 def make_subgrids(vis_b, coord_b, count_b, taper):
-    kk = vis_b.shape[-1]
-    live = (jnp.arange(kk, dtype=jnp.int32)[None, :] < count_b[:, None]).astype(jnp.float32)
-    scale_k = 1.0 / math.sqrt(kk)
-    vis_re = vis_b[:, 0, :].astype(jnp.float32) * live * scale_k
-    vis_im = vis_b[:, 1, :].astype(jnp.float32) * live * scale_k
-    step = -2.0 * math.pi / 32.0
-    bf = jnp.bfloat16
-    s_all = s_matrices(step * coord_b[:, 0, :], step * coord_b[:, 1, :], vis_re, vis_im)
+    s_all = s_matrices(coord_b, vis_b, count_b.reshape(-1, 1))
     s_re = s_all[:, :32, :32] - s_all[:, 32:, 32:]
     s_im = s_all[:, :32, 32:] + s_all[:, 32:, :32]
     x2 = jnp.concatenate([taper * s_re, taper * s_im], axis=1)

time: 101 us -> 99.6 us (0.986)
  other arithmetic: 7.57 us -> 5.54 us
    mul x2 -> x0, other arithmetic: 2.03 us -> none  [the longest x1 1.39 us: make_subgrids(): vis_im = vis_b[:, 1, :].astype(jnp.float32) * live * scale_k]
    unnamed x5 -> x3, local copies, waits for them, and re-layouts: 1.87 us -> 0.07 us
    reshape x0 -> x1, local copies, waits for them, and re-layouts: none -> 1.35 us  [make_subgrids(): s_all = s_matrices(coord_b, vis_b, count_b.reshape(-1, 1))]
where the time goes in v9:
time: 99.6 us; the launch traced here: 98.5 us
  blocking collectives  55.5 us (56%)
  starting transfers between devices  10.5 us (11%)
  waiting for transfers between devices  9.74 us (10%)
  matrix products  6.11 us (6%)
  Pallas kernels  6.08 us (6%)
  other arithmetic  5.54 us (6%)
  local copies, waits for them, and re-layouts  4.84 us (5%)
    all_to_all x1, blocking collectives, gathered_total(): lax.all_to_all(flat.reshape(n, per // 128, 128), axis, 0, 0, tiled=True)  34.7 us
    all_to_all x1, blocking collectives, gathered_total(): whole = lax.all_to_all(spread, axis, 0, 0, tiled=True)  20.8 us
    all_to_all x1, starting transfers between devices, body(): lax.all_to_all(send.reshape(n_span, cap, 2052), 'span', 0, 0, tiled=True)  10.5 us
    all_to_all x1, waiting for transfers between devices, body(): lax.all_to_all(send.reshape(n_span, cap, 2052), 'span', 0, 0, tiled=True)  9.74 us
    pallas_call x1, Pallas kernels, s_matrices(): pl.pallas_call(s_kernel, grid=(n // per,), in_specs=[both, both, pl.Block...  6.08 us
  transfers between devices with their start and end apart: 1, of which 1 were waited for; matrix products, arithmetic and copies ran while one was open for 0% of the time, Pallas kernels for 0%

profile of v9, /device:TPU:1, one launch (start us, length us, event | category | flops | bytes accessed | tf_op | source)
XLA Modules:
  0.0 98.5 jit_solution(8997819934401751793)
XLA Ops:
  0.0 0.0 copy-start
  0.0 0.7 convert.16
  0.7 0.7 convert_bitcast_fusion.1
  1.4 0.9 fusion.10
  2.2 0.7 convert_add_fusion
  2.9 0.1 copy.37
  3.0 0.1 copy.38
  3.1 0.1 copy.36
  3.2 1.3 %copy.32.count_ref = s32[32,1]{1,0:T(8,128)} copy(s32[32,1]{0,1:T(1,128)} %bitcast.56) | data formatting | bytes 256 | tf_op jit(solution)/shard_map/while/body/eval_jaxpr/reshape | solution.py:113
  4.6 0.1 fusion.39
  4.7 6.1 %eval_jaxpr.2 = f32[32,64,64]{2,1,0:T(8,128)} custom-call(f32[32,2,512]{2,1,0:T(2,128)} %bitcast.52, bf16[32,2,512]{2,1,0:T(2,128)(2,1)} %bitcast.53, s32[32,1]{1,0:T(8,128)} %copy.32.count_ref), custom_call_target="tpu_custom_call" | custom-call | flops 159383552 | bytes 720896 | tf_op jit(solution)/shard_map/while/body/eval_jaxpr/pallas_call | solution.py:98
  10.8 0.0 copy-done
  10.8 1.9 %fusion.22 = (f32[32,32,32]{2,1,0:T(8,128)S(1)}, f32[32,32,32]{2,1,0:T(8,128)S(1)}) fusion(f32[32,64,64]{2,1,0:T(8,128)} %eval_jaxpr.2, f32[32,32]{1,0:T(8,128)S(1)} %copy-done), kind=kLoop, calls=%fused_computation.28 | loop fusion | flops 131072 | bytes 790528 | tf_op jit(solution)/shard_map/while/body/eval_jaxpr/mul | solution.py:116
  12.7 1.8 %convolution_bitcast_fusion = f32[32,64,32]{1,2,0:T(8,128)S(1)} fusion(f32[32,32,32]{2,1,0:T(8,128)S(1)} %get-tuple-element.24, f32[32,32,32]{2,1,0:T(8,128)S(1)} %get-tuple-element.17, f32[32,32]{1,0:T(8,128)S(1)} %get-tuple-element.35, f32[32,32]{1,0:T(8,128)S(1)} %get-tuple-element.34, f32[32,32]{1,0:T(8,128)S(1)} %get-tuple-element.33), kind=kOutput, calls=%fused_computation.10 | convolution fusion | flops 50409472 | bytes 536576 | tf_op jit(solution)/shard_map/while/body/eval_jaxpr/ij,bjq->biq/dot_general | solution.py:124
  14.5 0.2 fusion.43
  14.7 1.8 %fusion.9 = bf16[32,32,64]{2,1,0:T(8,128)(2,1)S(1)} fusion(f32[32,32,32]{1,2,0:T(8,128)S(1)} %get-tuple-element.28, f32[32,32,32]{1,2,0:T(8,128)S(1)} %get-tuple-element.26, f32[32,32]{1,0:T(8,128)S(1)} %get-tuple-element.35, f32[32,32]{1,0:T(8,128)S(1)} %get-tuple-element.33, f32[32,32]{1,0:T(8,128)S(1)} %get-tuple-element.34), kind=kOutput, calls=%fused_computation.11 | convolution fusion | flops 50540544 | bytes 405504 | tf_op jit(solution)/shard_map/while/body/eval_jaxpr/baj,jk->bak/dot_general | solution.py:129
  16.5 0.2 convert_element_type.92
  16.8 0.1 copy.54
  16.9 0.5 reshape_reshape.4
  17.5 0.1 concatenate.44
  17.6 0.2 convolution_convert_fusion
  17.8 0.8 reshape.312
  18.6 10.5 %all-to-all-start = ((bf16[32,2,2052]{2,1,0:T(2,128)(2,1)}), bf16[32,2,2052]{2,1,0:T(2,128)(2,1)S(1)}, u32[]{:S(2)}, u32[]{:S(2)}) async-start(bf16[32,2,2052]{2,1,0:T(2,128)(2,1)} %reshape.312), calls=%async_computation | async-start | bytes 557056 | tf_op jit(solution)/shard_map/all_to_all | solution.py:186
  29.1 9.7 %all-to-all-done = bf16[32,2,2052]{2,1,0:T(2,128)(2,1)S(1)} async-done(((bf16[32,2,2052]{2,1,0:T(2,128)(2,1)}), bf16[32,2,2052]{2,1,0:T(2,128)(2,1)S(1)}, u32[]{:S(2)}, u32[]{:S(2)}) %all-to-all-start) | async-done | bytes 262688 | tf_op jit(solution)/shard_map/all_to_all | solution.py:186
  38.9 0.2 slice_reduce_fusion.1
  39.1 0.1 add_multiply_fusion
  39.2 0.1 copy.50
  39.3 0.1 iota_add_fusion.1
  39.3 0.1 iota_add_fusion
  39.4 0.2 slice.85
  39.6 0.5 reshape.313
  40.1 0.3 fusion.20
  40.5 0.1 fusion.42
  40.6 0.5 fusion.5
  41.1 0.9 fusion.6
  42.0 0.1 copy.41
  42.2 34.7 %all_to_all.15 = f32[24,22,128]{2,1,0:T(8,128)S(1)} all-to-all(f32[24,22,128]{2,1,0:T(8,128)S(1)} %reshape.314), channel_id=1, replica_groups=mesh['span'=32,'freq'=24] {'freq'}, dimensions={0} | all-to-all | bytes 540672 | tf_op jit(solution)/shard_map/all_to_all | solution.py:27
  77.0 20.8 %all_to_all.16 = f32[24,22,128]{2,1,0:T(8,128)S(1)} all-to-all(f32[24,22,128]{2,1,0:T(8,128)S(1)} %broadcast_in_dim.22), channel_id=1, replica_groups=mesh['span'=32,'freq'=24] {'freq'}, dimensions={0} | all-to-all | bytes 540672 | tf_op jit(solution)/shard_map/all_to_all | solution.py:30
  97.7 0.7 slice_multiply_fusion
  (13 shorter events, 0.2 us)
Async XLA Ops:
  0.0 10.8 %copy-start = (f32[32,32]{1,0:T(8,128)S(1)}, f32[32,32]{1,0:T(8,128)}, u32[]{:S(2)}) copy-start(f32[32,32]{1,0:T(8,128)} %param.13) | copy-start | bytes 12292
  18.6 20.3 %all-to-all-start = ((bf16[32,2,2052]{2,1,0:T(2,128)(2,1)}), bf16[32,2,2052]{2,1,0:T(2,128)(2,1)S(1)}, u32[]{:S(2)}, u32[]{:S(2)}) async-start(bf16[32,2,2052]{2,1,0:T(2,128)(2,1)} %reshape.312), calls=%async_computation | async-start | bytes 557056 | tf_op jit(solution)/shard_map/all_to_all | solution.py:186

commit v10 on v9

--- a/solution.py
+++ b/solution.py
@@ -4,6 +4,7 @@
 import jax.numpy as jnp
 from jax import lax
 from jax.experimental import pallas as pl
+from jax.experimental.pallas import tpu as pltpu
 from jax.sharding import PartitionSpec as P
 
 TILE = 128
@@ -75,7 +76,12 @@
 def s_kernel(coord_ref, vis_ref, count_ref, out):
     kk = coord_ref.shape[-1]
     step = -2.0 * math.pi / 32.0
-    live = lax.broadcasted_iota(jnp.int32, (coord_ref.shape[0], kk), 1) < count_ref[...]
+    per = coord_ref.shape[0]
+    sub = lax.broadcasted_iota(jnp.int32, (per, kk), 0)
+    limit = jnp.zeros((per, kk), jnp.int32)
+    for b in range(per):
+        limit = jnp.where(sub == b, count_ref[0, pl.program_id(0) * per + b], limit)
+    live = lax.broadcasted_iota(jnp.int32, (per, kk), 1) < limit
     scale_k = 1.0 / math.sqrt(kk)
     vis = vis_ref[...].astype(jnp.float32)
     coord = coord_ref[...]
@@ -98,7 +104,7 @@
     return pl.pallas_call(
         s_kernel,
         grid=(n // per,),
-        in_specs=[both, both, pl.BlockSpec((per, 1), lambda g: (g, 0))],
+        in_specs=[both, both, pl.BlockSpec(memory_space=pltpu.SMEM)],
         out_specs=pl.BlockSpec((per, 64, 64), lambda g: (g, 0, 0)),
         out_shape=jax.ShapeDtypeStruct((n, 64, 64), jnp.float32),
         cost_estimate=pl.CostEstimate(
@@ -110,7 +116,7 @@
 
 
 def make_subgrids(vis_b, coord_b, count_b, taper):
-    s_all = s_matrices(coord_b, vis_b, count_b.reshape(-1, 1))
+    s_all = s_matrices(coord_b, vis_b, count_b.reshape(1, -1))
     s_re = s_all[:, :32, :32] - s_all[:, 32:, 32:]
     s_im = s_all[:, :32, 32:] + s_all[:, 32:, :32]
     x2 = jnp.concatenate([taper * s_re, taper * s_im], axis=1)

time: 99.6 us -> 98.3 us (0.987)
  local copies, waits for them, and re-layouts: 4.84 us -> 3.49 us
    reshape x1 -> x0, local copies, waits for them, and re-layouts: 1.35 us -> none  [make_subgrids(): s_all = s_matrices(coord_b, vis_b, count_b.reshape(-1, 1))]
where the time goes in v10:
time: 98.3 us; the launch traced here: 97.1 us
  blocking collectives  55.5 us (56%)
  starting transfers between devices  10.5 us (11%)
  waiting for transfers between devices  9.74 us (10%)
  matrix products  6.11 us (6%)
  Pallas kernels  6.07 us (6%)
  other arithmetic  5.54 us (6%)
  local copies, waits for them, and re-layouts  3.49 us (4%)
    all_to_all x1, blocking collectives, gathered_total(): lax.all_to_all(flat.reshape(n, per // 128, 128), axis, 0, 0, tiled=True)  34.7 us
    all_to_all x1, blocking collectives, gathered_total(): whole = lax.all_to_all(spread, axis, 0, 0, tiled=True)  20.8 us
    all_to_all x1, starting transfers between devices, body(): lax.all_to_all(send.reshape(n_span, cap, 2052), 'span', 0, 0, tiled=True)  10.5 us
    all_to_all x1, waiting for transfers between devices, body(): lax.all_to_all(send.reshape(n_span, cap, 2052), 'span', 0, 0, tiled=True)  9.74 us
    pallas_call x1, Pallas kernels, s_matrices(): pl.pallas_call(s_kernel, grid=(n // per,), in_specs=[both, both, pl.Block...  6.07 us
  transfers between devices with their start and end apart: 1, of which 1 were waited for; matrix products, arithmetic and copies ran while one was open for 0% of the time, Pallas kernels for 0%

profile of v10, /device:TPU:1, one launch (start us, length us, event | category | flops | bytes accessed | tf_op | source)
XLA Modules:
  0.0 97.1 jit_solution(784935873774034943)
XLA Ops:
  0.0 0.0 copy-start
  0.0 0.7 convert.16
  0.7 0.7 convert_bitcast_fusion.1
  1.4 0.9 fusion.10
  2.2 0.7 convert_add_fusion
  2.9 0.1 copy.33
  3.0 0.1 copy.34
  3.1 0.1 copy.32
  3.2 0.1 fusion.39
  3.4 6.1 %eval_jaxpr.2 = f32[32,64,64]{2,1,0:T(8,128)} custom-call(f32[32,2,512]{2,1,0:T(2,128)} %bitcast.51, bf16[32,2,512]{2,1,0:T(2,128)(2,1)} %bitcast.52, s32[1,32]{1,0:T(1,128)} %count_ref), custom_call_target="tpu_custom_call" | custom-call | flops 159383552 | bytes 720896 | tf_op jit(solution)/shard_map/while/body/eval_jaxpr/pallas_call | solution.py:104
  9.4 0.0 copy-done
  9.4 1.9 %fusion.22 = (f32[32,32,32]{2,1,0:T(8,128)S(1)}, f32[32,32,32]{2,1,0:T(8,128)S(1)}) fusion(f32[32,64,64]{2,1,0:T(8,128)} %eval_jaxpr.2, f32[32,32]{1,0:T(8,128)S(1)} %copy-done), kind=kLoop, calls=%fused_computation.28 | loop fusion | flops 131072 | bytes 790528 | tf_op jit(solution)/shard_map/while/body/eval_jaxpr/mul | solution.py:122
  11.3 1.8 %convolution_bitcast_fusion = f32[32,64,32]{1,2,0:T(8,128)S(1)} fusion(f32[32,32,32]{2,1,0:T(8,128)S(1)} %get-tuple-element.24, f32[32,32,32]{2,1,0:T(8,128)S(1)} %get-tuple-element.17, f32[32,32]{1,0:T(8,128)S(1)} %get-tuple-element.35, f32[32,32]{1,0:T(8,128)S(1)} %get-tuple-element.34, f32[32,32]{1,0:T(8,128)S(1)} %get-tuple-element.33), kind=kOutput, calls=%fused_computation.10 | convolution fusion | flops 50409472 | bytes 536576 | tf_op jit(solution)/shard_map/while/body/eval_jaxpr/ij,bjq->biq/dot_general | solution.py:130
  13.1 0.2 fusion.43
  13.3 1.8 %fusion.9 = bf16[32,32,64]{2,1,0:T(8,128)(2,1)S(1)} fusion(f32[32,32,32]{1,2,0:T(8,128)S(1)} %get-tuple-element.28, f32[32,32,32]{1,2,0:T(8,128)S(1)} %get-tuple-element.26, f32[32,32]{1,0:T(8,128)S(1)} %get-tuple-element.35, f32[32,32]{1,0:T(8,128)S(1)} %get-tuple-element.33, f32[32,32]{1,0:T(8,128)S(1)} %get-tuple-element.34), kind=kOutput, calls=%fused_computation.11 | convolution fusion | flops 50540544 | bytes 405504 | tf_op jit(solution)/shard_map/while/body/eval_jaxpr/baj,jk->bak/dot_general | solution.py:135
  15.2 0.2 convert_element_type.92
  15.4 0.1 copy.50
  15.6 0.5 reshape_reshape.4
  16.1 0.1 concatenate.44
  16.2 0.2 convolution_convert_fusion
  16.4 0.8 reshape.308
  17.2 10.5 %all-to-all-start = ((bf16[32,2,2052]{2,1,0:T(2,128)(2,1)}), bf16[32,2,2052]{2,1,0:T(2,128)(2,1)S(1)}, u32[]{:S(2)}, u32[]{:S(2)}) async-start(bf16[32,2,2052]{2,1,0:T(2,128)(2,1)} %reshape.308), calls=%async_computation | async-start | bytes 557056 | tf_op jit(solution)/shard_map/all_to_all | solution.py:192
  27.8 9.7 %all-to-all-done = bf16[32,2,2052]{2,1,0:T(2,128)(2,1)S(1)} async-done(((bf16[32,2,2052]{2,1,0:T(2,128)(2,1)}), bf16[32,2,2052]{2,1,0:T(2,128)(2,1)S(1)}, u32[]{:S(2)}, u32[]{:S(2)}) %all-to-all-start) | async-done | bytes 262688 | tf_op jit(solution)/shard_map/all_to_all | solution.py:192
  37.5 0.2 slice_reduce_fusion.1
  37.7 0.1 add_multiply_fusion
  37.8 0.1 copy.46
  37.9 0.1 iota_add_fusion.1
  38.0 0.1 iota_add_fusion
  38.1 0.2 slice.85
  38.3 0.5 reshape.309
  38.8 0.3 fusion.20
  39.1 0.1 fusion.42
  39.2 0.5 fusion.5
  39.7 0.9 fusion.6
  40.6 0.1 copy.37
  40.8 34.7 %all_to_all.15 = f32[24,22,128]{2,1,0:T(8,128)S(1)} all-to-all(f32[24,22,128]{2,1,0:T(8,128)S(1)} %reshape.310), channel_id=1, replica_groups=mesh['span'=32,'freq'=24] {'freq'}, dimensions={0} | all-to-all | bytes 540672 | tf_op jit(solution)/shard_map/all_to_all | solution.py:28
  75.6 20.8 %all_to_all.16 = f32[24,22,128]{2,1,0:T(8,128)S(1)} all-to-all(f32[24,22,128]{2,1,0:T(8,128)S(1)} %broadcast_in_dim.22), channel_id=1, replica_groups=mesh['span'=32,'freq'=24] {'freq'}, dimensions={0} | all-to-all | bytes 540672 | tf_op jit(solution)/shard_map/all_to_all | solution.py:31
  96.4 0.7 slice_multiply_fusion
  (13 shorter events, 0.2 us)
Async XLA Ops:
  0.0 9.4 %copy-start = (f32[32,32]{1,0:T(8,128)S(1)}, f32[32,32]{1,0:T(8,128)}, u32[]{:S(2)}) copy-start(f32[32,32]{1,0:T(8,128)} %param.13) | copy-start | bytes 12292
  17.2 20.3 %all-to-all-start = ((bf16[32,2,2052]{2,1,0:T(2,128)(2,1)}), bf16[32,2,2052]{2,1,0:T(2,128)(2,1)S(1)}, u32[]{:S(2)}, u32[]{:S(2)}) async-start(bf16[32,2,2052]{2,1,0:T(2,128)(2,1)} %reshape.308), calls=%async_computation | async-start | bytes 557056 | tf_op jit(solution)/shard_map/all_to_all | solution.py:192

commit v11 on v10

--- a/solution.py
+++ b/solution.py
@@ -179,11 +179,9 @@
     col_off = offsets[0, :, 1]
     chan_loc = channel[0]
     cap = 2 * sub_count // n_span
-    onehot = (dest[:, None] == jnp.arange(n_span, dtype=jnp.int32)[None, :]).astype(jnp.float32)
     order = jnp.arange(sub_count, dtype=jnp.int32)
-    lower = (order[:, None] > order[None, :]).astype(jnp.float32)
-    earlier = jnp.dot(lower, onehot, preferred_element_type=jnp.float32)
-    rank = jnp.sum(earlier * onehot, axis=1).astype(jnp.int32)
+    before = (dest[:, None] == dest[None, :]) & (order[:, None] > order[None, :])
+    rank = jnp.sum(before.astype(jnp.int32), axis=1)
     slot = dest * cap + rank
     info = jnp.stack([jnp.ones_like(dest), row_off, col_off, chan_loc], 1).astype(jnp.bfloat16)
     rows = jnp.concatenate([patches.reshape(sub_count, 2048), info], axis=1)

time: 98.3 us -> 98.3 us (level)
  no operation moved by 1% of the time
where the time goes in v11:
time: 98.3 us; the launch traced here: 97.2 us
  blocking collectives  55.5 us (56%)
  starting transfers between devices  10.5 us (11%)
  waiting for transfers between devices  9.74 us (10%)
  other arithmetic  6.45 us (7%)
  Pallas kernels  6.07 us (6%)
  matrix products  5.24 us (5%)
  local copies, waits for them, and re-layouts  3.49 us (4%)
    all_to_all x1, blocking collectives, gathered_total(): lax.all_to_all(flat.reshape(n, per // 128, 128), axis, 0, 0, tiled=True)  34.7 us
    all_to_all x1, blocking collectives, gathered_total(): whole = lax.all_to_all(spread, axis, 0, 0, tiled=True)  20.8 us
    all_to_all x1, starting transfers between devices, body(): lax.all_to_all(send.reshape(n_span, cap, 2052), 'span', 0, 0, tiled=True)  10.5 us
    all_to_all x1, waiting for transfers between devices, body(): lax.all_to_all(send.reshape(n_span, cap, 2052), 'span', 0, 0, tiled=True)  9.74 us
    pallas_call x1, Pallas kernels, s_matrices(): pl.pallas_call(s_kernel, grid=(n // per,), in_specs=[both, both, pl.Block...  6.07 us
  transfers between devices with their start and end apart: 1, of which 1 were waited for; matrix products, arithmetic and copies ran while one was open for 0% of the time, Pallas kernels for 0%

profile of v11, /device:TPU:1, one launch (start us, length us, event | category | flops | bytes accessed | tf_op | source)
XLA Modules:
  0.0 97.2 jit_solution(6815153994830996564)
XLA Ops:
  0.0 0.0 copy-start
  0.0 0.7 convert.16
  0.7 0.7 convert_bitcast_fusion.1
  1.4 0.9 convert_reduce_fusion
  2.3 0.7 multiply_add_fusion
  2.9 0.1 copy.41
  3.0 0.1 copy.42
  3.1 0.1 copy.40
  3.2 0.1 fusion.38
  3.4 6.1 %eval_jaxpr.2 = f32[32,64,64]{2,1,0:T(8,128)} custom-call(f32[32,2,512]{2,1,0:T(2,128)} %bitcast.51, bf16[32,2,512]{2,1,0:T(2,128)(2,1)} %bitcast.52, s32[1,32]{1,0:T(1,128)} %count_ref), custom_call_target="tpu_custom_call" | custom-call | flops 159383552 | bytes 720896 | tf_op jit(solution)/shard_map/while/body/eval_jaxpr/pallas_call | solution.py:104
  9.5 0.0 copy-done
  9.5 1.9 %fusion.21 = (f32[32,32,32]{2,1,0:T(8,128)S(1)}, f32[32,32,32]{2,1,0:T(8,128)S(1)}) fusion(f32[32,64,64]{2,1,0:T(8,128)} %eval_jaxpr.2, f32[32,32]{1,0:T(8,128)S(1)} %copy-done), kind=kLoop, calls=%fused_computation.26 | loop fusion | flops 131072 | bytes 790528 | tf_op jit(solution)/shard_map/while/body/eval_jaxpr/mul | solution.py:122
  11.3 1.8 %convolution_bitcast_fusion = f32[32,64,32]{1,2,0:T(8,128)S(1)} fusion(f32[32,32,32]{2,1,0:T(8,128)S(1)} %get-tuple-element.24, f32[32,32,32]{2,1,0:T(8,128)S(1)} %get-tuple-element.17, f32[32,32]{1,0:T(8,128)S(1)} %get-tuple-element.35, f32[32,32]{1,0:T(8,128)S(1)} %get-tuple-element.34, f32[32,32]{1,0:T(8,128)S(1)} %get-tuple-element.33), kind=kOutput, calls=%fused_computation.10 | convolution fusion | flops 50409472 | bytes 536576 | tf_op jit(solution)/shard_map/while/body/eval_jaxpr/ij,bjq->biq/dot_general | solution.py:130
  13.2 0.2 fusion.42
  13.4 1.8 %fusion.9 = bf16[32,32,64]{2,1,0:T(8,128)(2,1)S(1)} fusion(f32[32,32,32]{1,2,0:T(8,128)S(1)} %get-tuple-element.28, f32[32,32,32]{1,2,0:T(8,128)S(1)} %get-tuple-element.26, f32[32,32]{1,0:T(8,128)S(1)} %get-tuple-element.35, f32[32,32]{1,0:T(8,128)S(1)} %get-tuple-element.33, f32[32,32]{1,0:T(8,128)S(1)} %get-tuple-element.34), kind=kOutput, calls=%fused_computation.11 | convolution fusion | flops 50540544 | bytes 405504 | tf_op jit(solution)/shard_map/while/body/eval_jaxpr/baj,jk->bak/dot_general | solution.py:135
  15.2 0.2 convert_element_type.86
  15.5 0.1 copy.58
  15.6 0.5 reshape_reshape.4
  16.1 0.1 concatenate.44
  16.2 0.2 convolution_convert_fusion
  16.5 0.8 reshape.308
  17.3 10.5 %all-to-all-start = ((bf16[32,2,2052]{2,1,0:T(2,128)(2,1)}), bf16[32,2,2052]{2,1,0:T(2,128)(2,1)S(1)}, u32[]{:S(2)}, u32[]{:S(2)}) async-start(bf16[32,2,2052]{2,1,0:T(2,128)(2,1)} %reshape.308), calls=%async_computation | async-start | bytes 557056 | tf_op jit(solution)/shard_map/all_to_all | solution.py:190
  27.8 9.7 %all-to-all-done = bf16[32,2,2052]{2,1,0:T(2,128)(2,1)S(1)} async-done(((bf16[32,2,2052]{2,1,0:T(2,128)(2,1)}), bf16[32,2,2052]{2,1,0:T(2,128)(2,1)S(1)}, u32[]{:S(2)}, u32[]{:S(2)}) %all-to-all-start) | async-done | bytes 262688 | tf_op jit(solution)/shard_map/all_to_all | solution.py:190
  37.6 0.2 slice_reduce_fusion.1
  37.8 0.1 add_multiply_fusion
  37.9 0.1 copy.54
  37.9 0.1 iota_add_fusion.1
  38.0 0.1 iota_add_fusion
  38.1 0.2 slice.85
  38.3 0.5 reshape.309
  38.8 0.3 fusion.19
  39.2 0.1 fusion.41
  39.2 0.5 fusion.5
  39.7 0.9 fusion.6
  40.7 0.1 copy.45
  40.9 34.7 %all_to_all.15 = f32[24,22,128]{2,1,0:T(8,128)S(1)} all-to-all(f32[24,22,128]{2,1,0:T(8,128)S(1)} %reshape.310), channel_id=1, replica_groups=mesh['span'=32,'freq'=24] {'freq'}, dimensions={0} | all-to-all | bytes 540672 | tf_op jit(solution)/shard_map/all_to_all | solution.py:28
  75.6 20.8 %all_to_all.16 = f32[24,22,128]{2,1,0:T(8,128)S(1)} all-to-all(f32[24,22,128]{2,1,0:T(8,128)S(1)} %broadcast_in_dim.26), channel_id=1, replica_groups=mesh['span'=32,'freq'=24] {'freq'}, dimensions={0} | all-to-all | bytes 540672 | tf_op jit(solution)/shard_map/all_to_all | solution.py:31
  96.4 0.7 slice_multiply_fusion
  (13 shorter events, 0.2 us)
Async XLA Ops:
  0.0 9.5 %copy-start = (f32[32,32]{1,0:T(8,128)S(1)}, f32[32,32]{1,0:T(8,128)}, u32[]{:S(2)}) copy-start(f32[32,32]{1,0:T(8,128)} %param.13) | copy-start | bytes 12292
  17.3 20.3 %all-to-all-start = ((bf16[32,2,2052]{2,1,0:T(2,128)(2,1)}), bf16[32,2,2052]{2,1,0:T(2,128)(2,1)S(1)}, u32[]{:S(2)}, u32[]{:S(2)}) async-start(bf16[32,2,2052]{2,1,0:T(2,128)(2,1)} %reshape.308), calls=%async_computation | async-start | bytes 557056 | tf_op jit(solution)/shard_map/all_to_all | solution.py:190

commit v12 on v11

--- a/solution.py
+++ b/solution.py
@@ -73,7 +73,7 @@
     return jnp.concatenate(res + ims, axis=0).astype(jnp.bfloat16)
 
 
-def s_kernel(coord_ref, vis_ref, count_ref, out):
+def s_kernel(coord_ref, vis_ref, count_ref, taper_ref, out):
     kk = coord_ref.shape[-1]
     step = -2.0 * math.pi / 32.0
     per = coord_ref.shape[0]
@@ -89,37 +89,41 @@
     vi = jnp.where(live, vis[:, 1, :] * scale_k, 0.0)
     small_u, big_u = kernel_tables(step * coord[:, 0, :])
     small_v, big_v = kernel_tables(step * coord[:, 1, :], (vr, vi))
+    tp = taper_ref[...]
     for b in range(out.shape[0]):
         a = kernel_rows(small_u, big_u, b)
         bb = kernel_rows(small_v, big_v, b)
-        out[b] = lax.dot_general(
-            a, bb, (((1,), (1,)), ((), ())), preferred_element_type=jnp.float32
-        )
-
-
-def s_matrices(coords, vis, counts):
+        sm = lax.dot_general(a, bb, (((1,), (1,)), ((), ())), preferred_element_type=jnp.float32)
+        x_re = tp * (sm[:32, :32] - sm[32:, 32:])
+        x_im = tp * (sm[:32, 32:] + sm[32:, :32])
+        out[b] = jnp.concatenate([x_re, x_im], axis=0)
+
+
+def s_matrices(coords, vis, counts, taper):
     n, _, kk = coords.shape
     per = 8
     both = pl.BlockSpec((per, 2, kk), lambda g: (g, 0, 0))
     return pl.pallas_call(
         s_kernel,
         grid=(n // per,),
-        in_specs=[both, both, pl.BlockSpec(memory_space=pltpu.SMEM)],
-        out_specs=pl.BlockSpec((per, 64, 64), lambda g: (g, 0, 0)),
-        out_shape=jax.ShapeDtypeStruct((n, 64, 64), jnp.float32),
+        in_specs=[
+            both,
+            both,
+            pl.BlockSpec(memory_space=pltpu.SMEM),
+            pl.BlockSpec((32, 32), lambda g: (0, 0)),
+        ],
+        out_specs=pl.BlockSpec((per, 64, 32), lambda g: (g, 0, 0)),
+        out_shape=jax.ShapeDtypeStruct((n, 64, 32), jnp.float32),
         cost_estimate=pl.CostEstimate(
             flops=2 * n * 64 * 64 * kk + 24 * n * 64 * kk,
             transcendentals=4 * n * kk,
             bytes_accessed=6 * n * 2 * kk + 4 * n * 64 * 64,
         ),
-    )(coords, vis, counts)
+    )(coords, vis, counts, taper)
 
 
 def make_subgrids(vis_b, coord_b, count_b, taper):
-    s_all = s_matrices(coord_b, vis_b, count_b.reshape(1, -1))
-    s_re = s_all[:, :32, :32] - s_all[:, 32:, 32:]
-    s_im = s_all[:, :32, 32:] + s_all[:, 32:, :32]
-    x2 = jnp.concatenate([taper * s_re, taper * s_im], axis=1)
+    x2 = s_matrices(coord_b, vis_b, count_b.reshape(1, -1), taper)
     centred = jnp.arange(32, dtype=jnp.float32) - 16.0
     angle = -2.0 * math.pi * centred[:, None] * centred[None, :] / 32.0
     f_re, f_im = (jnp.cos(angle), jnp.sin(angle))

time: 98.3 us -> 98.2 us (level)
  other arithmetic: 6.45 us -> 4.57 us
  matrix products: 5.24 us -> 6.46 us
    mul x1 -> x0, other arithmetic: 1.88 us -> none  [make_subgrids(): x2 = jnp.concatenate([taper * s_re, taper * s_im], axis=1)]
    dot_general x1, matrix products: 1.83 us -> 3.05 us  [make_subgrids(): y2 = jnp.einsum('ij,bjq->biq', left, x2, precision=hp)]
where the time goes in v12:
time: 98.2 us; the launch traced here: 97 us
  blocking collectives  55.5 us (57%)
  starting transfers between devices  10.5 us (11%)
  waiting for transfers between devices  9.74 us (10%)
  Pallas kernels  6.63 us (7%)
  matrix products  6.46 us (7%)
  other arithmetic  4.57 us (5%)
  local copies, waits for them, and re-layouts  3.49 us (4%)
    all_to_all x1, blocking collectives, gathered_total(): lax.all_to_all(flat.reshape(n, per // 128, 128), axis, 0, 0, tiled=True)  34.7 us
    all_to_all x1, blocking collectives, gathered_total(): whole = lax.all_to_all(spread, axis, 0, 0, tiled=True)  20.8 us
    all_to_all x1, starting transfers between devices, body(): lax.all_to_all(send.reshape(n_span, cap, 2052), 'span', 0, 0, tiled=True)  10.5 us
    all_to_all x1, waiting for transfers between devices, body(): lax.all_to_all(send.reshape(n_span, cap, 2052), 'span', 0, 0, tiled=True)  9.74 us
    pallas_call x1, Pallas kernels, s_matrices(): pl.pallas_call(s_kernel, grid=(n // per,), in_specs=[both, both, pl.Block...  6.63 us
    dot_general x1, matrix products, make_subgrids(): y2 = jnp.einsum('ij,bjq->biq', left, x2, precision=hp)  3.05 us
  transfers between devices with their start and end apart: 1, of which 1 were waited for; matrix products, arithmetic and copies ran while one was open for 0% of the time, Pallas kernels for 0%

profile of v12, /device:TPU:1, one launch (start us, length us, event | category | flops | bytes accessed | tf_op | source)
XLA Modules:
  0.0 97.0 jit_solution(15391700552414886828)
XLA Ops:
  0.0 0.7 convert.16
  0.7 0.7 convert_bitcast_fusion.1
  1.4 0.9 convert_reduce_fusion
  2.3 0.7 multiply_add_fusion
  2.9 0.1 copy.41
  3.0 0.1 copy.42
  3.1 0.1 copy.40
  3.2 0.1 fusion.33
  3.4 6.6 %eval_jaxpr.2 = f32[32,64,32]{2,1,0:T(8,128)} custom-call(f32[32,2,512]{2,1,0:T(2,128)} %bitcast.52, bf16[32,2,512]{2,1,0:T(2,128)(2,1)} %bitcast.53, s32[1,32]{1,0:T(1,128)} %count_ref, f32[32,32]{1,0:T(8,128)} %taper_ref), custom_call_target="tpu_custom_call" | custom-call | flops 159383552 | bytes 720896 | tf_op jit(solution)/shard_map/while/body/eval_jaxpr/pallas_call | solution.py:106
  10.0 3.0 %convolution_bitcast_fusion = f32[32,64,32]{1,2,0:T(8,128)S(1)} fusion(f32[32,64,32]{2,1,0:T(8,128)} %eval_jaxpr.2, f32[32,32]{1,0:T(8,128)S(1)} %get-tuple-element.32, f32[32,32]{1,0:T(8,128)S(1)} %get-tuple-element.31, f32[32,32]{1,0:T(8,128)S(1)} %get-tuple-element.30), kind=kOutput, calls=%fused_computation.10 | convolution fusion | flops 50343936 | bytes 536576 | tf_op jit(solution)/shard_map/while/body/eval_jaxpr/ij,bjq->biq/dot_general | solution.py:134
  13.1 0.2 fusion.37
  13.3 1.8 %fusion.9 = bf16[32,32,64]{2,1,0:T(8,128)(2,1)S(1)} fusion(f32[32,32,32]{1,2,0:T(8,128)S(1)} %get-tuple-element.17, f32[32,32,32]{1,2,0:T(8,128)S(1)} %get-tuple-element.16, f32[32,32]{1,0:T(8,128)S(1)} %get-tuple-element.32, f32[32,32]{1,0:T(8,128)S(1)} %get-tuple-element.30, f32[32,32]{1,0:T(8,128)S(1)} %get-tuple-element.31), kind=kOutput, calls=%fused_computation.11 | convolution fusion | flops 50540544 | bytes 405504 | tf_op jit(solution)/shard_map/while/body/eval_jaxpr/baj,jk->bak/dot_general | solution.py:139
  15.1 0.2 convert_element_type.86
  15.4 0.1 copy.58
  15.5 0.5 reshape_reshape.4
  16.0 0.1 concatenate.39
  16.1 0.2 convolution_convert_fusion
  16.4 0.8 reshape.307
  17.2 10.5 %all-to-all-start = ((bf16[32,2,2052]{2,1,0:T(2,128)(2,1)}), bf16[32,2,2052]{2,1,0:T(2,128)(2,1)S(1)}, u32[]{:S(2)}, u32[]{:S(2)}) async-start(bf16[32,2,2052]{2,1,0:T(2,128)(2,1)} %reshape.307), calls=%async_computation | async-start | bytes 557056 | tf_op jit(solution)/shard_map/all_to_all | solution.py:194
  27.7 9.7 %all-to-all-done = bf16[32,2,2052]{2,1,0:T(2,128)(2,1)S(1)} async-done(((bf16[32,2,2052]{2,1,0:T(2,128)(2,1)}), bf16[32,2,2052]{2,1,0:T(2,128)(2,1)S(1)}, u32[]{:S(2)}, u32[]{:S(2)}) %all-to-all-start) | async-done | bytes 262688 | tf_op jit(solution)/shard_map/all_to_all | solution.py:194
  37.5 0.2 slice_reduce_fusion.1
  37.7 0.1 add_multiply_fusion
  37.8 0.1 copy.54
  37.8 0.1 iota_add_fusion.1
  37.9 0.1 iota_add_fusion
  38.0 0.2 slice.61
  38.2 0.5 reshape.308
  38.7 0.3 fusion.16
  39.1 0.1 fusion.36
  39.1 0.5 fusion.5
  39.6 0.9 fusion.6
  40.6 0.1 copy.45
  40.8 34.7 %all_to_all.15 = f32[24,22,128]{2,1,0:T(8,128)S(1)} all-to-all(f32[24,22,128]{2,1,0:T(8,128)S(1)} %reshape.309), channel_id=1, replica_groups=mesh['span'=32,'freq'=24] {'freq'}, dimensions={0} | all-to-all | bytes 540672 | tf_op jit(solution)/shard_map/all_to_all | solution.py:28
  75.5 20.8 %all_to_all.16 = f32[24,22,128]{2,1,0:T(8,128)S(1)} all-to-all(f32[24,22,128]{2,1,0:T(8,128)S(1)} %broadcast_in_dim.23), channel_id=1, replica_groups=mesh['span'=32,'freq'=24] {'freq'}, dimensions={0} | all-to-all | bytes 540672 | tf_op jit(solution)/shard_map/all_to_all | solution.py:31
  96.3 0.7 slice_multiply_fusion
  (13 shorter events, 0.2 us)
Async XLA Ops:
  17.2 20.3 %all-to-all-start = ((bf16[32,2,2052]{2,1,0:T(2,128)(2,1)}), bf16[32,2,2052]{2,1,0:T(2,128)(2,1)S(1)}, u32[]{:S(2)}, u32[]{:S(2)}) async-start(bf16[32,2,2052]{2,1,0:T(2,128)(2,1)} %reshape.307), calls=%async_computation | async-start | bytes 557056 | tf_op jit(solution)/shard_map/all_to_all | solution.py:194

commit v13 on v11

--- a/solution.py
+++ b/solution.py
@@ -27,8 +27,8 @@
     flat = jnp.pad(flat, (0, per * n - size))
     got = lax.all_to_all(flat.reshape(n, per // 128, 128), axis, 0, 0, tiled=True)
     part = got.sum(axis=0)
-    spread = jnp.broadcast_to(part[None], (n, per // 128, 128))
-    whole = lax.all_to_all(spread, axis, 0, 0, tiled=True)
+    spread = jnp.broadcast_to(part.astype(jnp.bfloat16)[None], (n, per // 128, 128))
+    whole = lax.all_to_all(spread, axis, 0, 0, tiled=True).astype(jnp.float32)
     return whole.reshape(-1)[:size].reshape(shard.shape)
 
 

time: 98.3 us -> 94.2 us (0.958)
  blocking collectives: 55.5 us -> 52.1 us
    all_to_all x1, blocking collectives: 20.8 us -> 17.3 us  [gathered_total(): whole = lax.all_to_all(spread, axis, 0, 0, tiled=True).astype(jnp.float32)]
where the time goes in v13:
time: 94.2 us; the launch traced here: 93.8 us
  blocking collectives  52.1 us (55%)
  starting transfers between devices  10.5 us (11%)
  waiting for transfers between devices  9.74 us (10%)
  other arithmetic  6.45 us (7%)
  Pallas kernels  6.07 us (6%)
  matrix products  5.24 us (6%)
  local copies, waits for them, and re-layouts  3.52 us (4%)
    all_to_all x1, blocking collectives, gathered_total(): lax.all_to_all(flat.reshape(n, per // 128, 128), axis, 0, 0, tiled=True)  34.7 us
    all_to_all x1, blocking collectives, gathered_total(): whole = lax.all_to_all(spread, axis, 0, 0, tiled=True).astype(jnp.float32)  17.3 us
    all_to_all x1, starting transfers between devices, body(): lax.all_to_all(send.reshape(n_span, cap, 2052), 'span', 0, 0, tiled=True)  10.5 us
    all_to_all x1, waiting for transfers between devices, body(): lax.all_to_all(send.reshape(n_span, cap, 2052), 'span', 0, 0, tiled=True)  9.74 us
    pallas_call x1, Pallas kernels, s_matrices(): pl.pallas_call(s_kernel, grid=(n // per,), in_specs=[both, both, pl.Block...  6.07 us
  transfers between devices with their start and end apart: 1, of which 1 were waited for; matrix products, arithmetic and copies ran while one was open for 0% of the time, Pallas kernels for 0%

profile of v13, /device:TPU:1, one launch (start us, length us, event | category | flops | bytes accessed | tf_op | source)
XLA Modules:
  0.0 93.8 jit_solution(17713457730592850716)
XLA Ops:
  0.0 0.0 copy-start
  0.0 0.7 convert.18
  0.7 0.7 convert_bitcast_fusion.1
  1.4 0.9 convert_reduce_fusion
  2.3 0.7 multiply_add_fusion
  2.9 0.1 copy.41
  3.0 0.1 copy.42
  3.1 0.1 copy.40
  3.2 0.1 fusion.38
  3.4 6.1 %eval_jaxpr.2 = f32[32,64,64]{2,1,0:T(8,128)} custom-call(f32[32,2,512]{2,1,0:T(2,128)} %bitcast.51, bf16[32,2,512]{2,1,0:T(2,128)(2,1)} %bitcast.52, s32[1,32]{1,0:T(1,128)} %count_ref), custom_call_target="tpu_custom_call" | custom-call | flops 159383552 | bytes 720896 | tf_op jit(solution)/shard_map/while/body/eval_jaxpr/pallas_call | solution.py:104
  9.5 0.0 copy-done
  9.5 1.9 %fusion.21 = (f32[32,32,32]{2,1,0:T(8,128)S(1)}, f32[32,32,32]{2,1,0:T(8,128)S(1)}) fusion(f32[32,64,64]{2,1,0:T(8,128)} %eval_jaxpr.2, f32[32,32]{1,0:T(8,128)S(1)} %copy-done), kind=kLoop, calls=%fused_computation.26 | loop fusion | flops 131072 | bytes 790528 | tf_op jit(solution)/shard_map/while/body/eval_jaxpr/mul | solution.py:122
  11.3 1.8 %convolution_bitcast_fusion = f32[32,64,32]{1,2,0:T(8,128)S(1)} fusion(f32[32,32,32]{2,1,0:T(8,128)S(1)} %get-tuple-element.24, f32[32,32,32]{2,1,0:T(8,128)S(1)} %get-tuple-element.17, f32[32,32]{1,0:T(8,128)S(1)} %get-tuple-element.35, f32[32,32]{1,0:T(8,128)S(1)} %get-tuple-element.34, f32[32,32]{1,0:T(8,128)S(1)} %get-tuple-element.33), kind=kOutput, calls=%fused_computation.10 | convolution fusion | flops 50409472 | bytes 536576 | tf_op jit(solution)/shard_map/while/body/eval_jaxpr/ij,bjq->biq/dot_general | solution.py:130
  13.2 0.2 fusion.42
  13.4 1.8 %fusion.9 = bf16[32,32,64]{2,1,0:T(8,128)(2,1)S(1)} fusion(f32[32,32,32]{1,2,0:T(8,128)S(1)} %get-tuple-element.28, f32[32,32,32]{1,2,0:T(8,128)S(1)} %get-tuple-element.26, f32[32,32]{1,0:T(8,128)S(1)} %get-tuple-element.35, f32[32,32]{1,0:T(8,128)S(1)} %get-tuple-element.33, f32[32,32]{1,0:T(8,128)S(1)} %get-tuple-element.34), kind=kOutput, calls=%fused_computation.11 | convolution fusion | flops 50540544 | bytes 405504 | tf_op jit(solution)/shard_map/while/body/eval_jaxpr/baj,jk->bak/dot_general | solution.py:135
  15.2 0.2 convert_element_type.94
  15.5 0.1 copy.58
  15.6 0.5 reshape_reshape.4
  16.1 0.1 concatenate.44
  16.2 0.2 convolution_convert_fusion
  16.5 0.8 reshape.311
  17.3 10.5 %all-to-all-start = ((bf16[32,2,2052]{2,1,0:T(2,128)(2,1)}), bf16[32,2,2052]{2,1,0:T(2,128)(2,1)S(1)}, u32[]{:S(2)}, u32[]{:S(2)}) async-start(bf16[32,2,2052]{2,1,0:T(2,128)(2,1)} %reshape.311), calls=%async_computation | async-start | bytes 557056 | tf_op jit(solution)/shard_map/all_to_all | solution.py:190
  27.8 9.7 %all-to-all-done = bf16[32,2,2052]{2,1,0:T(2,128)(2,1)S(1)} async-done(((bf16[32,2,2052]{2,1,0:T(2,128)(2,1)}), bf16[32,2,2052]{2,1,0:T(2,128)(2,1)S(1)}, u32[]{:S(2)}, u32[]{:S(2)}) %all-to-all-start) | async-done | bytes 262688 | tf_op jit(solution)/shard_map/all_to_all | solution.py:190
  37.6 0.2 slice_reduce_fusion.1
  37.8 0.1 add_multiply_fusion
  37.9 0.1 copy.54
  37.9 0.1 iota_add_fusion.1
  38.0 0.1 iota_add_fusion
  38.1 0.2 slice.89
  38.3 0.5 reshape.312
  38.8 0.3 fusion.19
  39.2 0.1 fusion.41
  39.2 0.5 fusion.5
  39.7 0.9 fusion.6
  40.7 0.1 copy.45
  40.9 34.7 %all_to_all.15 = f32[24,22,128]{2,1,0:T(8,128)S(1)} all-to-all(f32[24,22,128]{2,1,0:T(8,128)S(1)} %reshape.313), channel_id=1, replica_groups=mesh['span'=32,'freq'=24] {'freq'}, dimensions={0} | all-to-all | bytes 540672 | tf_op jit(solution)/shard_map/all_to_all | solution.py:28
  75.6 17.3 %all_to_all.16 = bf16[24,22,128]{2,1,0:T(8,128)(2,1)S(1)} all-to-all(bf16[24,22,128]{2,1,0:T(8,128)(2,1)S(1)} %broadcast_in_dim.26), channel_id=1, replica_groups=mesh['span'=32,'freq'=24] {'freq'}, dimensions={0} | all-to-all | bytes 270336 | tf_op jit(solution)/shard_map/all_to_all | solution.py:31
  93.0 0.7 convert_multiply_fusion
  (13 shorter events, 0.2 us)
Async XLA Ops:
  0.0 9.5 %copy-start = (f32[32,32]{1,0:T(8,128)S(1)}, f32[32,32]{1,0:T(8,128)}, u32[]{:S(2)}) copy-start(f32[32,32]{1,0:T(8,128)} %param.13) | copy-start | bytes 12292
  17.3 20.3 %all-to-all-start = ((bf16[32,2,2052]{2,1,0:T(2,128)(2,1)}), bf16[32,2,2052]{2,1,0:T(2,128)(2,1)S(1)}, u32[]{:S(2)}, u32[]{:S(2)}) async-start(bf16[32,2,2052]{2,1,0:T(2,128)(2,1)} %reshape.311), calls=%async_computation | async-start | bytes 557056 | tf_op jit(solution)/shard_map/all_to_all | solution.py:190

commit v14 on v13

--- a/solution.py
+++ b/solution.py
@@ -123,7 +123,7 @@
     centred = jnp.arange(32, dtype=jnp.float32) - 16.0
     angle = -2.0 * math.pi * centred[:, None] * centred[None, :] / 32.0
     f_re, f_im = (jnp.cos(angle), jnp.sin(angle))
-    hp = lax.Precision.HIGHEST
+    hp = lax.Precision.HIGH
     left = jnp.concatenate(
         [jnp.concatenate([f_re, -f_im], 1), jnp.concatenate([f_im, f_re], 1)], 0
     )

time: 94.2 us -> 92.6 us (0.983)
  matrix products: 5.24 us -> 3.62 us
where the time goes in v14:
time: 92.6 us; the launch traced here: 92.1 us
  blocking collectives  52.1 us (56%)
  starting transfers between devices  10.5 us (11%)
  waiting for transfers between devices  9.74 us (11%)
  other arithmetic  6.45 us (7%)
  Pallas kernels  6.07 us (7%)
  matrix products  3.62 us (4%)
  local copies, waits for them, and re-layouts  3.52 us (4%)
    all_to_all x1, blocking collectives, gathered_total(): lax.all_to_all(flat.reshape(n, per // 128, 128), axis, 0, 0, tiled=True)  34.7 us
    all_to_all x1, blocking collectives, gathered_total(): whole = lax.all_to_all(spread, axis, 0, 0, tiled=True).astype(jnp.float32)  17.3 us
    all_to_all x1, starting transfers between devices, body(): lax.all_to_all(send.reshape(n_span, cap, 2052), 'span', 0, 0, tiled=True)  10.5 us
    all_to_all x1, waiting for transfers between devices, body(): lax.all_to_all(send.reshape(n_span, cap, 2052), 'span', 0, 0, tiled=True)  9.74 us
    pallas_call x1, Pallas kernels, s_matrices(): pl.pallas_call(s_kernel, grid=(n // per,), in_specs=[both, both, pl.Block...  6.07 us
    mul x1, other arithmetic, make_subgrids(): x2 = jnp.concatenate([taper * s_re, taper * s_im], axis=1)  1.88 us
  transfers between devices with their start and end apart: 1, of which 1 were waited for; matrix products, arithmetic and copies ran while one was open for 0% of the time, Pallas kernels for 0%

profile of v14, /device:TPU:1, one launch (start us, length us, event | category | flops | bytes accessed | tf_op | source)
XLA Modules:
  0.0 92.1 jit_solution(17232985221184429609)
XLA Ops:
  0.0 0.0 copy-start
  0.0 0.7 convert.18
  0.7 0.7 convert_bitcast_fusion.1
  1.4 0.9 convert_reduce_fusion
  2.3 0.7 multiply_add_fusion
  2.9 0.1 copy.41
  3.0 0.1 copy.42
  3.1 0.1 copy.40
  3.2 0.1 fusion.38
  3.4 6.1 %eval_jaxpr.2 = f32[32,64,64]{2,1,0:T(8,128)} custom-call(f32[32,2,512]{2,1,0:T(2,128)} %bitcast.51, bf16[32,2,512]{2,1,0:T(2,128)(2,1)} %bitcast.52, s32[1,32]{1,0:T(1,128)} %count_ref), custom_call_target="tpu_custom_call" | custom-call | flops 159383552 | bytes 720896 | tf_op jit(solution)/shard_map/while/body/eval_jaxpr/pallas_call | solution.py:104
  9.5 0.0 copy-done
  9.5 1.9 %fusion.21 = (f32[32,32,32]{2,1,0:T(8,128)S(1)}, f32[32,32,32]{2,1,0:T(8,128)S(1)}) fusion(f32[32,64,64]{2,1,0:T(8,128)} %eval_jaxpr.2, f32[32,32]{1,0:T(8,128)S(1)} %copy-done), kind=kLoop, calls=%fused_computation.26 | loop fusion | flops 131072 | bytes 790528 | tf_op jit(solution)/shard_map/while/body/eval_jaxpr/mul | solution.py:122
  11.3 1.0 %convolution_bitcast_fusion = f32[32,64,32]{1,2,0:T(8,128)S(1)} fusion(f32[32,32,32]{2,1,0:T(8,128)S(1)} %get-tuple-element.24, f32[32,32,32]{2,1,0:T(8,128)S(1)} %get-tuple-element.17, f32[32,32]{1,0:T(8,128)S(1)} %get-tuple-element.35, f32[32,32]{1,0:T(8,128)S(1)} %get-tuple-element.34, f32[32,32]{1,0:T(8,128)S(1)} %get-tuple-element.33), kind=kOutput, calls=%fused_computation.10 | convolution fusion | flops 25243648 | bytes 536576 | tf_op jit(solution)/shard_map/while/body/eval_jaxpr/ij,bjq->biq/dot_general | solution.py:130
  12.4 0.2 fusion.42
  12.6 1.0 %fusion.9 = bf16[32,32,64]{2,1,0:T(8,128)(2,1)S(1)} fusion(f32[32,32,32]{1,2,0:T(8,128)S(1)} %get-tuple-element.28, f32[32,32,32]{1,2,0:T(8,128)S(1)} %get-tuple-element.26, f32[32,32]{1,0:T(8,128)S(1)} %get-tuple-element.35, f32[32,32]{1,0:T(8,128)S(1)} %get-tuple-element.33, f32[32,32]{1,0:T(8,128)S(1)} %get-tuple-element.34), kind=kOutput, calls=%fused_computation.11 | convolution fusion | flops 25374720 | bytes 405504 | tf_op jit(solution)/shard_map/while/body/eval_jaxpr/baj,jk->bak/dot_general | solution.py:135
  13.6 0.2 convert_element_type.94
  13.9 0.1 copy.58
  14.0 0.5 reshape_reshape.4
  14.5 0.1 concatenate.44
  14.6 0.2 convolution_convert_fusion
  14.9 0.8 reshape.311
  15.7 10.5 %all-to-all-start = ((bf16[32,2,2052]{2,1,0:T(2,128)(2,1)}), bf16[32,2,2052]{2,1,0:T(2,128)(2,1)S(1)}, u32[]{:S(2)}, u32[]{:S(2)}) async-start(bf16[32,2,2052]{2,1,0:T(2,128)(2,1)} %reshape.311), calls=%async_computation | async-start | bytes 557056 | tf_op jit(solution)/shard_map/all_to_all | solution.py:190
  26.2 9.7 %all-to-all-done = bf16[32,2,2052]{2,1,0:T(2,128)(2,1)S(1)} async-done(((bf16[32,2,2052]{2,1,0:T(2,128)(2,1)}), bf16[32,2,2052]{2,1,0:T(2,128)(2,1)S(1)}, u32[]{:S(2)}, u32[]{:S(2)}) %all-to-all-start) | async-done | bytes 262688 | tf_op jit(solution)/shard_map/all_to_all | solution.py:190
  36.0 0.2 slice_reduce_fusion.1
  36.1 0.1 add_multiply_fusion
  36.3 0.1 copy.54
  36.3 0.1 iota_add_fusion.1
  36.4 0.1 iota_add_fusion
  36.5 0.2 slice.89
  36.7 0.5 reshape.312
  37.2 0.3 fusion.19
  37.5 0.1 fusion.41
  37.6 0.5 fusion.5
  38.1 0.9 fusion.6
  39.0 0.1 copy.45
  39.2 34.7 %all_to_all.15 = f32[24,22,128]{2,1,0:T(8,128)S(1)} all-to-all(f32[24,22,128]{2,1,0:T(8,128)S(1)} %reshape.313), channel_id=1, replica_groups=mesh['span'=32,'freq'=24] {'freq'}, dimensions={0} | all-to-all | bytes 540672 | tf_op jit(solution)/shard_map/all_to_all | solution.py:28
  74.0 17.3 %all_to_all.16 = bf16[24,22,128]{2,1,0:T(8,128)(2,1)S(1)} all-to-all(bf16[24,22,128]{2,1,0:T(8,128)(2,1)S(1)} %broadcast_in_dim.26), channel_id=1, replica_groups=mesh['span'=32,'freq'=24] {'freq'}, dimensions={0} | all-to-all | bytes 270336 | tf_op jit(solution)/shard_map/all_to_all | solution.py:31
  91.4 0.7 convert_multiply_fusion
  (13 shorter events, 0.2 us)
Async XLA Ops:
  0.0 9.5 %copy-start = (f32[32,32]{1,0:T(8,128)S(1)}, f32[32,32]{1,0:T(8,128)}, u32[]{:S(2)}) copy-start(f32[32,32]{1,0:T(8,128)} %param.13) | copy-start | bytes 12292
  15.7 20.3 %all-to-all-start = ((bf16[32,2,2052]{2,1,0:T(2,128)(2,1)}), bf16[32,2,2052]{2,1,0:T(2,128)(2,1)S(1)}, u32[]{:S(2)}, u32[]{:S(2)}) async-start(bf16[32,2,2052]{2,1,0:T(2,128)(2,1)} %reshape.311), calls=%async_computation | async-start | bytes 557056 | tf_op jit(solution)/shard_map/all_to_all | solution.py:190

commit v15 on v14

--- a/solution.py
+++ b/solution.py
@@ -99,7 +99,7 @@
 
 def s_matrices(coords, vis, counts):
     n, _, kk = coords.shape
-    per = 8
+    per = 16
     both = pl.BlockSpec((per, 2, kk), lambda g: (g, 0, 0))
     return pl.pallas_call(
         s_kernel,

time: 92.6 us -> 92.6 us (level)
  no operation moved by 1% of the time
where the time goes in v15:
time: 92.6 us; the launch traced here: 92.2 us
  blocking collectives  52.1 us (56%)
  starting transfers between devices  10.5 us (11%)
  waiting for transfers between devices  9.74 us (11%)
  other arithmetic  6.45 us (7%)
  Pallas kernels  6.14 us (7%)
  matrix products  3.62 us (4%)
  local copies, waits for them, and re-layouts  3.52 us (4%)
    all_to_all x1, blocking collectives, gathered_total(): lax.all_to_all(flat.reshape(n, per // 128, 128), axis, 0, 0, tiled=True)  34.7 us
    all_to_all x1, blocking collectives, gathered_total(): whole = lax.all_to_all(spread, axis, 0, 0, tiled=True).astype(jnp.float32)  17.3 us
    all_to_all x1, starting transfers between devices, body(): lax.all_to_all(send.reshape(n_span, cap, 2052), 'span', 0, 0, tiled=True)  10.5 us
    all_to_all x1, waiting for transfers between devices, body(): lax.all_to_all(send.reshape(n_span, cap, 2052), 'span', 0, 0, tiled=True)  9.74 us
    pallas_call x1, Pallas kernels, s_matrices(): pl.pallas_call(s_kernel, grid=(n // per,), in_specs=[both, both, pl.Block...  6.14 us
    mul x1, other arithmetic, make_subgrids(): x2 = jnp.concatenate([taper * s_re, taper * s_im], axis=1)  1.88 us
  transfers between devices with their start and end apart: 1, of which 1 were waited for; matrix products, arithmetic and copies ran while one was open for 0% of the time, Pallas kernels for 0%

profile of v15, /device:TPU:1, one launch (start us, length us, event | category | flops | bytes accessed | tf_op | source)
XLA Modules:
  0.0 92.2 jit_solution(2139367439917986599)
XLA Ops:
  0.0 0.0 copy-start
  0.0 0.7 convert.18
  0.7 0.7 convert_bitcast_fusion.1
  1.4 0.9 convert_reduce_fusion
  2.3 0.7 multiply_add_fusion
  2.9 0.1 copy.41
  3.0 0.1 copy.42
  3.1 0.1 copy.40
  3.2 0.1 fusion.38
  3.4 6.1 %eval_jaxpr.2 = f32[32,64,64]{2,1,0:T(8,128)} custom-call(f32[32,2,512]{2,1,0:T(2,128)} %bitcast.51, bf16[32,2,512]{2,1,0:T(2,128)(2,1)} %bitcast.52, s32[1,32]{1,0:T(1,128)} %count_ref), custom_call_target="tpu_custom_call" | custom-call | flops 159383552 | bytes 720896 | tf_op jit(solution)/shard_map/while/body/eval_jaxpr/pallas_call | solution.py:104
  9.5 0.0 copy-done
  9.5 1.9 %fusion.21 = (f32[32,32,32]{2,1,0:T(8,128)S(1)}, f32[32,32,32]{2,1,0:T(8,128)S(1)}) fusion(f32[32,64,64]{2,1,0:T(8,128)} %eval_jaxpr.2, f32[32,32]{1,0:T(8,128)S(1)} %copy-done), kind=kLoop, calls=%fused_computation.26 | loop fusion | flops 131072 | bytes 790528 | tf_op jit(solution)/shard_map/while/body/eval_jaxpr/mul | solution.py:122
  11.4 1.0 %convolution_bitcast_fusion = f32[32,64,32]{1,2,0:T(8,128)S(1)} fusion(f32[32,32,32]{2,1,0:T(8,128)S(1)} %get-tuple-element.24, f32[32,32,32]{2,1,0:T(8,128)S(1)} %get-tuple-element.17, f32[32,32]{1,0:T(8,128)S(1)} %get-tuple-element.35, f32[32,32]{1,0:T(8,128)S(1)} %get-tuple-element.34, f32[32,32]{1,0:T(8,128)S(1)} %get-tuple-element.33), kind=kOutput, calls=%fused_computation.10 | convolution fusion | flops 25243648 | bytes 536576 | tf_op jit(solution)/shard_map/while/body/eval_jaxpr/ij,bjq->biq/dot_general | solution.py:130
  12.4 0.2 fusion.42
  12.6 1.0 %fusion.9 = bf16[32,32,64]{2,1,0:T(8,128)(2,1)S(1)} fusion(f32[32,32,32]{1,2,0:T(8,128)S(1)} %get-tuple-element.28, f32[32,32,32]{1,2,0:T(8,128)S(1)} %get-tuple-element.26, f32[32,32]{1,0:T(8,128)S(1)} %get-tuple-element.35, f32[32,32]{1,0:T(8,128)S(1)} %get-tuple-element.33, f32[32,32]{1,0:T(8,128)S(1)} %get-tuple-element.34), kind=kOutput, calls=%fused_computation.11 | convolution fusion | flops 25374720 | bytes 405504 | tf_op jit(solution)/shard_map/while/body/eval_jaxpr/baj,jk->bak/dot_general | solution.py:135
  13.7 0.2 convert_element_type.94
  13.9 0.1 copy.58
  14.0 0.5 reshape_reshape.4
  14.6 0.1 concatenate.44
  14.7 0.2 convolution_convert_fusion
  14.9 0.8 reshape.311
  15.7 10.5 %all-to-all-start = ((bf16[32,2,2052]{2,1,0:T(2,128)(2,1)}), bf16[32,2,2052]{2,1,0:T(2,128)(2,1)S(1)}, u32[]{:S(2)}, u32[]{:S(2)}) async-start(bf16[32,2,2052]{2,1,0:T(2,128)(2,1)} %reshape.311), calls=%async_computation | async-start | bytes 557056 | tf_op jit(solution)/shard_map/all_to_all | solution.py:190
  26.3 9.7 %all-to-all-done = bf16[32,2,2052]{2,1,0:T(2,128)(2,1)S(1)} async-done(((bf16[32,2,2052]{2,1,0:T(2,128)(2,1)}), bf16[32,2,2052]{2,1,0:T(2,128)(2,1)S(1)}, u32[]{:S(2)}, u32[]{:S(2)}) %all-to-all-start) | async-done | bytes 262688 | tf_op jit(solution)/shard_map/all_to_all | solution.py:190
  36.0 0.2 slice_reduce_fusion.1
  36.2 0.1 add_multiply_fusion
  36.3 0.1 copy.54
  36.4 0.1 iota_add_fusion.1
  36.5 0.1 iota_add_fusion
  36.6 0.2 slice.89
  36.8 0.5 reshape.312
  37.3 0.3 fusion.19
  37.6 0.1 fusion.41
  37.7 0.5 fusion.5
  38.2 0.9 fusion.6
  39.1 0.1 copy.45
  39.3 34.7 %all_to_all.15 = f32[24,22,128]{2,1,0:T(8,128)S(1)} all-to-all(f32[24,22,128]{2,1,0:T(8,128)S(1)} %reshape.313), channel_id=1, replica_groups=mesh['span'=32,'freq'=24] {'freq'}, dimensions={0} | all-to-all | bytes 540672 | tf_op jit(solution)/shard_map/all_to_all | solution.py:28
  74.1 17.3 %all_to_all.16 = bf16[24,22,128]{2,1,0:T(8,128)(2,1)S(1)} all-to-all(bf16[24,22,128]{2,1,0:T(8,128)(2,1)S(1)} %broadcast_in_dim.26), channel_id=1, replica_groups=mesh['span'=32,'freq'=24] {'freq'}, dimensions={0} | all-to-all | bytes 270336 | tf_op jit(solution)/shard_map/all_to_all | solution.py:31
  91.5 0.7 convert_multiply_fusion
  (13 shorter events, 0.2 us)
Async XLA Ops:
  0.0 9.5 %copy-start = (f32[32,32]{1,0:T(8,128)S(1)}, f32[32,32]{1,0:T(8,128)}, u32[]{:S(2)}) copy-start(f32[32,32]{1,0:T(8,128)} %param.13) | copy-start | bytes 12292
  15.7 20.3 %all-to-all-start = ((bf16[32,2,2052]{2,1,0:T(2,128)(2,1)}), bf16[32,2,2052]{2,1,0:T(2,128)(2,1)S(1)}, u32[]{:S(2)}, u32[]{:S(2)}) async-start(bf16[32,2,2052]{2,1,0:T(2,128)(2,1)} %reshape.311), calls=%async_computation | async-start | bytes 557056 | tf_op jit(solution)/shard_map/all_to_all | solution.py:190

commit v16 on v14

--- a/solution.py
+++ b/solution.py
@@ -19,7 +19,7 @@
     return tuple(jnp.split(whole, [sum(widths[:k]) for k in range(1, len(widths))], axis=along))
 
 
-def gathered_total(shard, axis):
+def gathered_total(shard, axis, scale):
     n = lax.axis_size(axis)
     flat = shard.reshape(-1)
     size = flat.shape[0]
@@ -27,7 +27,7 @@
     flat = jnp.pad(flat, (0, per * n - size))
     got = lax.all_to_all(flat.reshape(n, per // 128, 128), axis, 0, 0, tiled=True)
     part = got.sum(axis=0)
-    spread = jnp.broadcast_to(part.astype(jnp.bfloat16)[None], (n, per // 128, 128))
+    spread = jnp.broadcast_to((part * scale).astype(jnp.bfloat16)[None], (n, per // 128, 128))
     whole = lax.all_to_all(spread, axis, 0, 0, tiled=True).astype(jnp.float32)
     return whole.reshape(-1)[:size].reshape(shard.shape)
 
@@ -197,9 +197,8 @@
         got_payload.reshape(slots, 2, 32, 32), weight, got_meta[:, 1], got_meta[:, 2]
     )
     local = local.reshape(NT, 1, 2, TILE, TILE)
-    total = gathered_total(local, "freq")
     scale = TILE / (32.0 * math.sqrt(n_freq * sub_count))
-    return total * scale
+    return gathered_total(local, "freq", scale)
 
 
 def solution(mesh):

time: 92.6 us -> 92.6 us (level)
  no operation moved by 1% of the time
where the time goes in v16:
time: 92.6 us; the launch traced here: 92.2 us
  blocking collectives  52.1 us (56%)
  starting transfers between devices  10.5 us (11%)
  waiting for transfers between devices  9.74 us (11%)
  other arithmetic  6.45 us (7%)
  Pallas kernels  6.07 us (7%)
  matrix products  3.62 us (4%)
  local copies, waits for them, and re-layouts  3.53 us (4%)
    all_to_all x1, blocking collectives, gathered_total(): lax.all_to_all(flat.reshape(n, per // 128, 128), axis, 0, 0, tiled=True)  34.7 us
    all_to_all x1, blocking collectives, gathered_total(): whole = lax.all_to_all(spread, axis, 0, 0, tiled=True).astype(jnp.float32)  17.3 us
    all_to_all x1, starting transfers between devices, body(): lax.all_to_all(send.reshape(n_span, cap, 2052), 'span', 0, 0, tiled=True)  10.5 us
    all_to_all x1, waiting for transfers between devices, body(): lax.all_to_all(send.reshape(n_span, cap, 2052), 'span', 0, 0, tiled=True)  9.74 us
    pallas_call x1, Pallas kernels, s_matrices(): pl.pallas_call(s_kernel, grid=(n // per,), in_specs=[both, both, pl.Block...  6.07 us
    mul x1, other arithmetic, make_subgrids(): x2 = jnp.concatenate([taper * s_re, taper * s_im], axis=1)  1.88 us
  transfers between devices with their start and end apart: 1, of which 1 were waited for; matrix products, arithmetic and copies ran while one was open for 0% of the time, Pallas kernels for 0%

profile of v16, /device:TPU:1, one launch (start us, length us, event | category | flops | bytes accessed | tf_op | source)
XLA Modules:
  0.0 92.2 jit_solution(16809239434028878991)
XLA Ops:
  0.0 0.0 copy-start
  0.0 0.7 convert.19
  0.7 0.7 convert_bitcast_fusion.1
  1.4 0.9 convert_reduce_fusion
  2.3 0.7 multiply_add_fusion
  2.9 0.1 copy.41
  3.0 0.1 copy.42
  3.1 0.1 copy.40
  3.2 0.1 fusion.38
  3.4 6.1 %eval_jaxpr.2 = f32[32,64,64]{2,1,0:T(8,128)} custom-call(f32[32,2,512]{2,1,0:T(2,128)} %bitcast.53, bf16[32,2,512]{2,1,0:T(2,128)(2,1)} %bitcast.54, s32[1,32]{1,0:T(1,128)} %count_ref), custom_call_target="tpu_custom_call" | custom-call | flops 159383552 | bytes 720896 | tf_op jit(solution)/shard_map/while/body/eval_jaxpr/pallas_call | solution.py:104
  9.5 0.0 copy-done
  9.5 1.9 %fusion.21 = (f32[32,32,32]{2,1,0:T(8,128)S(1)}, f32[32,32,32]{2,1,0:T(8,128)S(1)}) fusion(f32[32,64,64]{2,1,0:T(8,128)} %eval_jaxpr.2, f32[32,32]{1,0:T(8,128)S(1)} %copy-done), kind=kLoop, calls=%fused_computation.26 | loop fusion | flops 131072 | bytes 790528 | tf_op jit(solution)/shard_map/while/body/eval_jaxpr/mul | solution.py:122
  11.3 1.0 %convolution_bitcast_fusion = f32[32,64,32]{1,2,0:T(8,128)S(1)} fusion(f32[32,32,32]{2,1,0:T(8,128)S(1)} %get-tuple-element.24, f32[32,32,32]{2,1,0:T(8,128)S(1)} %get-tuple-element.17, f32[32,32]{1,0:T(8,128)S(1)} %get-tuple-element.35, f32[32,32]{1,0:T(8,128)S(1)} %get-tuple-element.34, f32[32,32]{1,0:T(8,128)S(1)} %get-tuple-element.33), kind=kOutput, calls=%fused_computation.10 | convolution fusion | flops 25243648 | bytes 536576 | tf_op jit(solution)/shard_map/while/body/eval_jaxpr/ij,bjq->biq/dot_general | solution.py:130
  12.4 0.2 fusion.42
  12.6 1.0 %fusion.9 = bf16[32,32,64]{2,1,0:T(8,128)(2,1)S(1)} fusion(f32[32,32,32]{1,2,0:T(8,128)S(1)} %get-tuple-element.28, f32[32,32,32]{1,2,0:T(8,128)S(1)} %get-tuple-element.26, f32[32,32]{1,0:T(8,128)S(1)} %get-tuple-element.35, f32[32,32]{1,0:T(8,128)S(1)} %get-tuple-element.33, f32[32,32]{1,0:T(8,128)S(1)} %get-tuple-element.34), kind=kOutput, calls=%fused_computation.11 | convolution fusion | flops 25374720 | bytes 405504 | tf_op jit(solution)/shard_map/while/body/eval_jaxpr/baj,jk->bak/dot_general | solution.py:135
  13.6 0.2 convert_element_type.94
  13.9 0.1 copy.58
  14.0 0.5 reshape_reshape.4
  14.5 0.1 concatenate.44
  14.6 0.2 convolution_convert_fusion
  14.9 0.8 reshape.303
  15.7 10.5 %all-to-all-start = ((bf16[32,2,2052]{2,1,0:T(2,128)(2,1)}), bf16[32,2,2052]{2,1,0:T(2,128)(2,1)S(1)}, u32[]{:S(2)}, u32[]{:S(2)}) async-start(bf16[32,2,2052]{2,1,0:T(2,128)(2,1)} %reshape.303), calls=%async_computation | async-start | bytes 557056 | tf_op jit(solution)/shard_map/all_to_all | solution.py:190
  26.2 9.7 %all-to-all-done = bf16[32,2,2052]{2,1,0:T(2,128)(2,1)S(1)} async-done(((bf16[32,2,2052]{2,1,0:T(2,128)(2,1)}), bf16[32,2,2052]{2,1,0:T(2,128)(2,1)S(1)}, u32[]{:S(2)}, u32[]{:S(2)}) %all-to-all-start) | async-done | bytes 262688 | tf_op jit(solution)/shard_map/all_to_all | solution.py:190
  36.0 0.2 slice_reduce_fusion.1
  36.1 0.1 add_multiply_fusion
  36.3 0.1 copy.54
  36.3 0.1 iota_add_fusion.1
  36.4 0.1 iota_add_fusion
  36.5 0.2 slice.86
  36.7 0.5 reshape.304
  37.2 0.3 fusion.19
  37.5 0.1 fusion.41
  37.6 0.5 fusion.5
  38.1 0.9 fusion.6
  39.0 0.1 copy.45
  39.2 34.7 %all_to_all.15 = f32[24,22,128]{2,1,0:T(8,128)S(1)} all-to-all(f32[24,22,128]{2,1,0:T(8,128)S(1)} %reshape.305), channel_id=1, replica_groups=mesh['span'=32,'freq'=24] {'freq'}, dimensions={0} | all-to-all | bytes 540672 | tf_op jit(solution)/shard_map/all_to_all | solution.py:28
  74.0 17.3 %all_to_all.16 = bf16[24,22,128]{2,1,0:T(8,128)(2,1)S(1)} all-to-all(bf16[24,22,128]{2,1,0:T(8,128)(2,1)S(1)} %broadcast_in_dim.26), channel_id=1, replica_groups=mesh['span'=32,'freq'=24] {'freq'}, dimensions={0} | all-to-all | bytes 270336 | tf_op jit(solution)/shard_map/all_to_all | solution.py:31
  91.4 0.7 convert.22
  (15 shorter events, 0.3 us)
Async XLA Ops:
  0.0 9.5 %copy-start = (f32[32,32]{1,0:T(8,128)S(1)}, f32[32,32]{1,0:T(8,128)}, u32[]{:S(2)}) copy-start(f32[32,32]{1,0:T(8,128)} %param.13) | copy-start | bytes 12292
  15.7 20.3 %all-to-all-start = ((bf16[32,2,2052]{2,1,0:T(2,128)(2,1)}), bf16[32,2,2052]{2,1,0:T(2,128)(2,1)S(1)}, u32[]{:S(2)}, u32[]{:S(2)}) async-start(bf16[32,2,2052]{2,1,0:T(2,128)(2,1)} %reshape.303), calls=%async_computation | async-start | bytes 557056 | tf_op jit(solution)/shard_map/all_to_all | solution.py:190

commit v17 on v14

--- a/solution.py
+++ b/solution.py
@@ -132,7 +132,7 @@
     right = jnp.concatenate(
         [jnp.concatenate([f_re, f_im], 1), jnp.concatenate([-f_im, f_re], 1)], 0
     )
-    z2 = jnp.einsum("baj,jk->bak", ycat, right, precision=hp)
+    z2 = jnp.einsum("baj,jk->bak", ycat, right, preferred_element_type=jnp.float32)
     z = z2.reshape(z2.shape[0], 32, 2, 32).transpose(0, 2, 1, 3)
     return (z / 32.0).astype(jnp.bfloat16)
 

time: 92.6 us -> 91.8 us (level)
  no operation moved by 1% of the time
where the time goes in v17:
time: 91.8 us; the launch traced here: 91.4 us
  blocking collectives  52.1 us (57%)
  starting transfers between devices  10.5 us (11%)
  waiting for transfers between devices  9.74 us (11%)
  other arithmetic  6.45 us (7%)
  Pallas kernels  6.07 us (7%)
  local copies, waits for them, and re-layouts  3.44 us (4%)
  matrix products  2.93 us (3%)
    all_to_all x1, blocking collectives, gathered_total(): lax.all_to_all(flat.reshape(n, per // 128, 128), axis, 0, 0, tiled=True)  34.7 us
    all_to_all x1, blocking collectives, gathered_total(): whole = lax.all_to_all(spread, axis, 0, 0, tiled=True).astype(jnp.float32)  17.3 us
    all_to_all x1, starting transfers between devices, body(): lax.all_to_all(send.reshape(n_span, cap, 2052), 'span', 0, 0, tiled=True)  10.5 us
    all_to_all x1, waiting for transfers between devices, body(): lax.all_to_all(send.reshape(n_span, cap, 2052), 'span', 0, 0, tiled=True)  9.74 us
    pallas_call x1, Pallas kernels, s_matrices(): pl.pallas_call(s_kernel, grid=(n // per,), in_specs=[both, both, pl.Block...  6.07 us
    mul x1, other arithmetic, make_subgrids(): x2 = jnp.concatenate([taper * s_re, taper * s_im], axis=1)  1.88 us
  transfers between devices with their start and end apart: 1, of which 1 were waited for; matrix products, arithmetic and copies ran while one was open for 0% of the time, Pallas kernels for 0%

profile of v17, /device:TPU:1, one launch (start us, length us, event | category | flops | bytes accessed | tf_op | source)
XLA Modules:
  0.0 91.4 jit_solution(13206651645499790478)
XLA Ops:
  0.0 0.0 copy-start
  0.0 0.7 convert.18
  0.7 0.7 convert_bitcast_fusion.1
  1.4 0.9 convert_reduce_fusion
  2.3 0.7 multiply_add_fusion
  2.9 0.1 copy.41
  3.0 0.1 copy.42
  3.1 0.1 copy.40
  3.2 0.1 fusion.38
  3.4 6.1 %eval_jaxpr.2 = f32[32,64,64]{2,1,0:T(8,128)} custom-call(f32[32,2,512]{2,1,0:T(2,128)} %bitcast.51, bf16[32,2,512]{2,1,0:T(2,128)(2,1)} %bitcast.52, s32[1,32]{1,0:T(1,128)} %count_ref), custom_call_target="tpu_custom_call" | custom-call | flops 159383552 | bytes 720896 | tf_op jit(solution)/shard_map/while/body/eval_jaxpr/pallas_call | solution.py:104
  9.5 0.0 copy-done
  9.5 1.9 %fusion.21 = (f32[32,32,32]{2,1,0:T(8,128)S(1)}, f32[32,32,32]{2,1,0:T(8,128)S(1)}) fusion(f32[32,64,64]{2,1,0:T(8,128)} %eval_jaxpr.2, f32[32,32]{1,0:T(8,128)S(1)} %copy-done), kind=kLoop, calls=%fused_computation.26 | loop fusion | flops 131072 | bytes 790528 | tf_op jit(solution)/shard_map/while/body/eval_jaxpr/mul | solution.py:122
  11.3 1.0 %convolution_bitcast_fusion = bf16[32,64,32]{1,2,0:T(8,128)(2,1)S(1)} fusion(f32[32,32,32]{2,1,0:T(8,128)S(1)} %get-tuple-element.24, f32[32,32,32]{2,1,0:T(8,128)S(1)} %get-tuple-element.17, f32[32,32]{1,0:T(8,128)S(1)} %get-tuple-element.35, f32[32,32]{1,0:T(8,128)S(1)} %get-tuple-element.34, f32[32,32]{1,0:T(8,128)S(1)} %get-tuple-element.33), kind=kOutput, calls=%fused_computation.10 | convolution fusion | flops 25243648 | bytes 405504 | tf_op jit(solution)/shard_map/while/body/eval_jaxpr/ij,bjq->biq/dot_general | solution.py:130
  12.4 0.1 fusion.42
  12.5 0.3 fusion.9
  12.9 0.2 convert_element_type.94
  13.1 0.1 copy.58
  13.2 0.5 reshape_reshape.4
  13.8 0.1 concatenate.44
  13.9 0.2 convolution_convert_fusion
  14.1 0.8 reshape.311
  14.9 10.5 %all-to-all-start = ((bf16[32,2,2052]{2,1,0:T(2,128)(2,1)}), bf16[32,2,2052]{2,1,0:T(2,128)(2,1)S(1)}, u32[]{:S(2)}, u32[]{:S(2)}) async-start(bf16[32,2,2052]{2,1,0:T(2,128)(2,1)} %reshape.311), calls=%async_computation | async-start | bytes 557056 | tf_op jit(solution)/shard_map/all_to_all | solution.py:190
  25.4 9.7 %all-to-all-done = bf16[32,2,2052]{2,1,0:T(2,128)(2,1)S(1)} async-done(((bf16[32,2,2052]{2,1,0:T(2,128)(2,1)}), bf16[32,2,2052]{2,1,0:T(2,128)(2,1)S(1)}, u32[]{:S(2)}, u32[]{:S(2)}) %all-to-all-start) | async-done | bytes 262688 | tf_op jit(solution)/shard_map/all_to_all | solution.py:190
  35.2 0.2 slice_reduce_fusion.1
  35.4 0.1 add_multiply_fusion
  35.5 0.1 copy.54
  35.6 0.1 iota_add_fusion.1
  35.7 0.1 iota_add_fusion
  35.7 0.2 slice.89
  35.9 0.5 reshape.312
  36.4 0.3 fusion.19
  36.8 0.1 fusion.41
  36.9 0.5 fusion.5
  37.4 0.9 fusion.6
  38.3 0.1 copy.45
  38.5 34.7 %all_to_all.15 = f32[24,22,128]{2,1,0:T(8,128)S(1)} all-to-all(f32[24,22,128]{2,1,0:T(8,128)S(1)} %reshape.313), channel_id=1, replica_groups=mesh['span'=32,'freq'=24] {'freq'}, dimensions={0} | all-to-all | bytes 540672 | tf_op jit(solution)/shard_map/all_to_all | solution.py:28
  73.3 17.3 %all_to_all.16 = bf16[24,22,128]{2,1,0:T(8,128)(2,1)S(1)} all-to-all(bf16[24,22,128]{2,1,0:T(8,128)(2,1)S(1)} %broadcast_in_dim.26), channel_id=1, replica_groups=mesh['span'=32,'freq'=24] {'freq'}, dimensions={0} | all-to-all | bytes 270336 | tf_op jit(solution)/shard_map/all_to_all | solution.py:31
  90.7 0.7 convert_multiply_fusion
  (13 shorter events, 0.2 us)
Async XLA Ops:
  0.0 9.5 %copy-start = (f32[32,32]{1,0:T(8,128)S(1)}, f32[32,32]{1,0:T(8,128)}, u32[]{:S(2)}) copy-start(f32[32,32]{1,0:T(8,128)} %param.13) | copy-start | bytes 12292
  14.9 20.3 %all-to-all-start = ((bf16[32,2,2052]{2,1,0:T(2,128)(2,1)}), bf16[32,2,2052]{2,1,0:T(2,128)(2,1)S(1)}, u32[]{:S(2)}, u32[]{:S(2)}) async-start(bf16[32,2,2052]{2,1,0:T(2,128)(2,1)} %reshape.311), calls=%async_computation | async-start | bytes 557056 | tf_op jit(solution)/shard_map/all_to_all | solution.py:190
